TPU v7x, 512 devices: a whole 4x8x8 slice. The times are simulated.
512 devices in a mesh: series: 8 (over y_hi, x), tm: 64 (over z, y_lo, core).
Axes of the slice: x: 4, y: 8 (y_hi: 2, y_lo: 4; y = y_hi * 4 + y_lo), z: 8, core: 2. Of those that a mesh axis runs over, the one named last changes fastest.
Arguments:
- y_obs: bfloat16 [32768, 32768], P('series', 'tm'), may hold values from -6 to 6
- tile_mask: int32 [256, 256], P('series', 'tm'), may hold values 0 or 1
- factors: float32 [32768, 128], P(('series', 'tm')), may hold values from -0.5 to 0.5
- adam_m: float32 [32768, 128], P(('series', 'tm')), may hold values from -3 to 3
- adam_v: float32 [32768, 128], P(('series', 'tm')), may hold values from 0.1 to 10
- basis: float32 [128, 32768], P('series', 'tm'), may hold values from -6 to 6
- dilations: int32 [4], replicated, may hold values from 1 to 32, as said below
- conv_w: bfloat16 [4, 2, 128, 128], replicated, may hold values from -0.375 to 0.375
- conv_b: float32 [4, 128], replicated, may hold values from -3 to 3
Outputs:
- factors_new: float32 [32768, 128], P(('series', 'tm'))
- m_new: float32 [32768, 128], P(('series', 'tm'))
- v_new: float32 [32768, 128], P(('series', 'tm'))
- basis_new: float32 [128, 32768], P('series', 'tm')
Inputs may be any that keep to these rules, and one draw needn't show every extreme that they name: `dilations`: at least one layer has dilation 32.
All inputs are finite; a program needn't handle non-finite values. No bound on the sum of `tile_mask` on one device may be relied on, other than what follows from the above.
Results may differ from a plain program's by a relative error of at most 0.0031.
Values may be sent and summed in bfloat16 or wider, within the bound.
No kernel may reach another device: no remote copies, remote signals or barrier semaphores. Data moves between devices by JAX's collectives and lax.ppermute only.
A program may use at most 64 MiB of HBM per device.

v0:
```python
import math

import jax
import jax.numpy as jnp
from jax import lax
from jax.sharding import PartitionSpec as P

K = 128
TILE = 128
LAYERS = 4
D_MAX = 32


def passed_along(value, axis, steps):
    count = lax.axis_size(axis)
    leading, last = (max(0, -steps), min(count, count - steps))
    return lax.ppermute(value, axis, [(source, source + steps) for source in range(leading, last)])


def expand(tiles, tile):
    rows, cols = tiles.shape
    ones = tiles.astype(jnp.float32)
    return jnp.broadcast_to(ones[:, None, :, None], (rows, tile, cols, tile)).reshape(
        rows * tile, cols * tile
    )


def adam_update(factors, adam_m, adam_v, grad_f):
    m_new = 0.9 * adam_m + 0.1 * grad_f
    v_new = 0.999 * adam_v + 0.001 * grad_f * grad_f
    m_hat = m_new / (1.0 - 0.9**10)
    v_hat = v_new / (1.0 - 0.999**10)
    return (factors - 0.01 * m_hat / (jnp.sqrt(v_hat) + 1e-08), m_new, v_new)


def conv_layer(hidden, hb, past, weights, biases):
    z_val = jnp.dot(weights[0], past, preferred_element_type=jnp.float32)
    z_val = z_val + jnp.dot(weights[1], hb, preferred_element_type=jnp.float32)
    z_val = z_val + biases[:, None]
    return hidden + jax.nn.relu(z_val)


def on_device(y_obs, tile_mask, factors, adam_m, adam_v, basis, dilations, conv_w, conv_b):
    own_rows = factors.shape[0]
    width = basis.shape[1]
    rank_part = basis.shape[0]
    total_time = width * lax.axis_size("tm")
    total_series = own_rows * lax.axis_size("tm") * lax.axis_size("series")
    f_block = lax.all_gather(factors.astype(jnp.bfloat16), "tm", axis=0, tiled=True)
    x_full = lax.all_gather(basis.astype(jnp.bfloat16), "series", axis=0, tiled=True)
    pred = jnp.dot(f_block, x_full, preferred_element_type=jnp.float32)
    resid = expand(tile_mask, TILE) * (y_obs.astype(jnp.float32) - pred)
    rb = resid.astype(jnp.bfloat16)
    scale_f = 1.0 / math.sqrt(total_time)
    contract_time = (((1,), (1,)), ((), ()))
    grad_f = lax.psum_scatter(
        -lax.dot_general(rb, x_full, contract_time, preferred_element_type=jnp.float32) * scale_f,
        "tm",
        scatter_dimension=0,
        tiled=True,
    )
    factors_new, m_new, v_new = adam_update(factors, adam_m, adam_v, grad_f)
    partial_x = -lax.dot_general(
        f_block, rb, (((0,), (0,)), ((), ())), preferred_element_type=jnp.float32
    )
    partial_x = partial_x * math.sqrt(K / total_series)
    grad_x = lax.psum_scatter(partial_x, "series", scatter_dimension=0, tiled=True)
    hidden = x_full.astype(jnp.float32)
    for layer in range(LAYERS):
        hb = hidden.astype(jnp.bfloat16)
        rim = passed_along(hb[:, width - D_MAX :], "tm", 1)
        extended = jnp.concatenate([rim, hb], axis=1)
        past = lax.dynamic_slice_in_dim(extended, D_MAX - dilations[layer], width, 1)
        hidden = conv_layer(hidden, hb, past, conv_w[layer], conv_b[layer])
    target = lax.dynamic_slice_in_dim(hidden, lax.axis_index("series") * rank_part, rank_part, 0)
    basis_new = basis - 0.5 * (grad_x + (basis - target))
    return (factors_new, m_new, v_new, basis_new)


def solution(mesh):
    return jax.shard_map(
        on_device,
        mesh=mesh,
        in_specs=(
            P("series", "tm"),
            P("series", "tm"),
            P(("series", "tm"), None),
            P(("series", "tm"), None),
            P(("series", "tm"), None),
            P("series", "tm"),
            P(),
            P(),
            P(),
        ),
        out_specs=(
            P(("series", "tm"), None),
            P(("series", "tm"), None),
            P(("series", "tm"), None),
            P("series", "tm"),
        ),
        check_vma=False,
    )
```

profile of v0, /device:TPU:6, one launch (start us, length us, event | category | flops | bytes accessed | tf_op | source)
XLA Modules:
  0.0 517.4 jit_solution(5125097129864647785)
XLA Ops:
  7.2 1.4 convert_element_type.30
  8.7 0.7 convert_element_type.28
  9.4 0.8 convert_element_type.31
  10.2 43.9 %all_gather.7 = bf16[128,512]{1,0:T(8,128)(2,1)S(1)} all-gather(bf16[16,512]{1,0:T(8,128)(2,1)S(1)} %convert_element_type.31), channel_id=1, replica_groups=mesh['series'=8,'tm'=64] {'series'}, dimensions={0}, use_global_device_ids=true | all-gather | bytes 147456 | tf_op jit(solution)/shard_map/all_gather | solution.py:50
  54.1 76.9 %all-gather.2.cloned.1.call-done = bf16[4096,128]{1,0:T(8,128)(2,1)} async-done(((bf16[64,128]{1,0:T(8,128)(2,1)}), bf16[4096,128]{1,0:T(8,128)(2,1)}) %all-gather.2.cloned.1.call-update) | async-done | bytes 1048592 | tf_op jit(solution)/shard_map/all_gather | solution.py:49
  131.0 1.1 broadcast_in_dim.2
  132.2 1.0 copy-done.1
  133.5 1.2 fusion
  134.8 1.9 copy-done
  136.7 1.3 fusion.18
  138.0 0.8 copy.32
  138.9 4.8 fusion.1
  143.9 2.1 collective-permute-start
  152.7 3.1 collective-permute-start.1
  156.0 0.6 collective-permute-done.1
  156.8 2.2 collective-permute-start.2
  159.3 0.6 collective-permute-done.2
  160.1 4.0 collective-permute-start.3
  164.3 0.6 collective-permute-done.3
  165.1 60.5 %reduce-scatter.7.cloned.1.call-done = f32[16,512]{1,0:T(8,128)} async-done(((f32[128,512]{1,0:T(8,128)}), f32[16,512]{1,0:T(8,128)}) %reduce-scatter.7.cloned.1.call-update) | async-done | bytes 32784
  225.6 0.9 copy.33
  226.7 0.7 copy.28
  227.4 282.0 %reduce-scatter.5.cloned.1.call-done = f32[64,128]{1,0:T(8,128)} async-done(((f32[4096,128]{1,0:T(8,128)}), f32[64,128]{1,0:T(8,128)}) %reduce-scatter.5.cloned.1.call-update) | async-done | bytes 32784 | tf_op jit(solution)/shard_map/reduce_scatter | solution.py:56
  509.4 1.4 divide_subtract_fusion
  (43 shorter events, 3.5 us)
Async XLA Ops:
  7.2 123.9 %all-gather.2.cloned.1.call-start = ((), (), s32[]{:S(2)}) async-start(), calls=%async_computation.2 | async-start | bytes 1064960 | tf_op jit(solution)/shard_map/all_gather | solution.py:49
  8.6 217.0 %reduce-scatter.7.cloned.1.call-start = ((), (), s32[]{:S(2)}) async-start(), calls=%async_computation.4 | async-start | bytes 294912
  131.0 2.2 copy-start.1
  131.0 2.5 copy-start.2
  134.8 1.9 copy-start
  138.8 7.2 %copy-start.9 = (f32[4,128]{1,0:T(4,128)S(1)}, f32[4,128]{1,0:T(4,128)}, u32[]{:S(2)}) copy-start(f32[4,128]{1,0:T(4,128)} %param.17) | copy-start | bytes 6148
  138.9 7.2 %copy-start.3 = (bf16[4,2,128,128]{3,2,1,0:T(8,128)(2,1)S(1)}, bf16[4,2,128,128]{3,2,1,0:T(8,128)(2,1)}, u32[]{:S(2)}) copy-start(bf16[4,2,128,128]{3,2,1,0:T(8,128)(2,1)} %param.16) | copy-start | bytes 786436
  138.9 7.4 %copy-start.8 = (s32[4]{0:T(128)S(1)}, s32[4]{0:T(128)}, u32[]{:S(2)}) copy-start(s32[4]{0:T(128)} %param.15) | copy-start | bytes 52
  138.9 8.0 %copy-start.4 = (f32[16,512]{1,0:T(8,128)S(1)}, f32[16,512]{1,0:T(8,128)}, u32[]{:S(2)}) copy-start(f32[16,512]{1,0:T(8,128)} %param.14) | copy-start | bytes 98308
  138.9 370.5 %reduce-scatter.5.cloned.1.call-start = ((), (), s32[]{:S(2)}) async-start(), calls=%async_computation.3 | async-start | bytes 2129920 | tf_op jit(solution)/shard_map/reduce_scatter | solution.py:56
  143.8 365.6 %copy-start.5 = (f32[64,128]{1,0:T(8,128)S(1)}, f32[64,128]{1,0:T(8,128)}, u32[]{:S(2)}) copy-start(f32[64,128]{1,0:T(8,128)} %param.11) | copy-start | bytes 98308
  143.8 365.6 %copy-start.6 = (f32[64,128]{1,0:T(8,128)S(1)}, f32[64,128]{1,0:T(8,128)}, u32[]{:S(2)}) copy-start(f32[64,128]{1,0:T(8,128)} %param.12) | copy-start | bytes 98308
  143.8 365.6 %copy-start.7 = (f32[64,128]{1,0:T(8,128)S(1)}, f32[64,128]{1,0:T(8,128)}, u32[]{:S(2)}) copy-start(f32[64,128]{1,0:T(8,128)} %param.13) | copy-start | bytes 98308
  143.9 8.5 %collective-permute-start = (bf16[128,32]{1,0:T(8,128)(2,1)S(1)}, bf16[128,32]{1,0:T(8,128)(2,1)S(1)}, u32[]{:S(2)}, u32[]{:S(2)}) collective-permute-start(bf16[128,32]{1,0:T(8,128)(2,1)S(1)} %slice.100), channel_id=1, source_target_pairs={{0,1},{1,2},{2,3},{3,4},{4,5},{5,6},{6,7},{7,8},{8,9},{9,10},{10,1... | collective-permute-start | bytes 24584 | tf_op jit(solution)/shard_map/ppermute | solution.py:17
  152.7 3.9 collective-permute-start.1
  156.8 3.1 collective-permute-start.2
  160.1 4.8 collective-permute-start.3
Sparse Core Ops, SparseCore 0:
  10.7 120.2 all-gather.1
  139.0 86.6 reduce-scatter.6
  228.6 280.7 reduce-scatter.4
where the time goes:
time: 518 us; the launch traced here: 517 us
  waiting for transfers between devices  421 us (81%)
  blocking collectives  43.9 us (8%)
  between operations  19.2 us (4%)
  starting transfers between devices  11.6 us (2%)
  matrix products  9.04 us (2%)
  local copies, waits for them, and re-layouts  7.91 us (2%)
    reduce_scatter x1, waiting for transfers between devices, on_device(): lax.psum_scatter(-lax.dot_general(rb, x_full, contract_time, preferred_el...  282 us
    all_gather x1, waiting for transfers between devices, on_device(): lax.all_gather(factors.astype(jnp.bfloat16), 'tm', axis=0, tiled=True)  76.9 us
    unnamed x4, waiting for transfers between devices  60.5 us
    all_gather x1, blocking collectives, on_device(): lax.all_gather(basis.astype(jnp.bfloat16), 'series', axis=0, tiled=True)  43.9 us
    ppermute x4, starting transfers between devices, passed_along(): lax.ppermute(value, axis, [(source, source + steps) for source in range(l...  11.4 us
  transfers between devices with their start and end apart: 7, of which 6 were waited for; matrix products, arithmetic and copies ran while one was open for 2% of the time, Pallas kernels for 0%

commit v1 on v0

v1 whole, which is shorter than its diff:
```python
import math

import jax
import jax.numpy as jnp
from jax import lax
from jax.sharding import Mesh
from jax.sharding import PartitionSpec as P

K = 128
TILE = 128
LAYERS = 4
D_MAX = 32
HALO = LAYERS * D_MAX
CORES = 2
Y_LO = 4
TM = ("z", "ylo", "core")
ROW = ("z", "ylo")


def expand(tiles, tile):
    rows, cols = tiles.shape
    ones = tiles.astype(jnp.float32)
    return jnp.broadcast_to(ones[:, None, :, None], (rows, tile, cols, tile)).reshape(
        rows * tile, cols * tile
    )


def adam_update(factors, adam_m, adam_v, grad_f):
    m_new = 0.9 * adam_m + 0.1 * grad_f
    v_new = 0.999 * adam_v + 0.001 * grad_f * grad_f
    m_hat = m_new / (1.0 - 0.9**10)
    v_hat = v_new / (1.0 - 0.999**10)
    return (factors - 0.01 * m_hat / (jnp.sqrt(v_hat) + 1e-08), m_new, v_new)


def conv_layer(hidden, hb, past, weights, biases):
    z_val = jnp.dot(weights[0], past, preferred_element_type=jnp.float32)
    z_val = z_val + jnp.dot(weights[1], hb, preferred_element_type=jnp.float32)
    z_val = z_val + biases[:, None]
    return hidden + jax.nn.relu(z_val)


def gather_by_a2a(x, axis, count):
    copies = jnp.broadcast_to(x[None], (count,) + x.shape)
    return lax.all_to_all(copies, axis, 0, 0, tiled=True)


def on_device(y_obs, tile_mask, factors, adam_m, adam_v, basis, dilations, conv_w, conv_b):
    own_rows = factors.shape[0]
    width = basis.shape[1]
    rank_part = basis.shape[0]
    n_row = lax.axis_size(ROW)
    n_series = lax.axis_size("series")
    n_tm = n_row * CORES
    total_time = width * n_tm
    total_series = own_rows * n_tm * n_series

    fb = factors.astype(jnp.bfloat16)
    f_rows = gather_by_a2a(fb, ROW, n_row)
    f_all = gather_by_a2a(f_rows, "core", CORES)
    f_block = jnp.swapaxes(f_all, 0, 1).reshape(n_tm * own_rows, K)

    x_parts = gather_by_a2a(basis.astype(jnp.bfloat16), "series", n_series)
    x_full = x_parts.reshape(n_series * rank_part, width)

    pred = jnp.dot(f_block, x_full, preferred_element_type=jnp.float32)
    resid = expand(tile_mask, TILE) * (y_obs.astype(jnp.float32) - pred)
    rb = resid.astype(jnp.bfloat16)
    scale_f = 1.0 / math.sqrt(total_time)
    contract_time = (((1,), (1,)), ((), ()))
    partial_f = -lax.dot_general(rb, x_full, contract_time, preferred_element_type=jnp.float32) * scale_f
    by_core = partial_f.reshape(n_row, CORES, own_rows, K)
    by_core = lax.all_to_all(by_core, "core", 1, 1, tiled=True).sum(1)
    by_row = lax.all_to_all(by_core.astype(jnp.bfloat16), ROW, 0, 0, tiled=True)
    grad_f = by_row.astype(jnp.float32).sum(0)
    factors_new, m_new, v_new = adam_update(factors, adam_m, adam_v, grad_f)

    partial_x = -lax.dot_general(
        f_block, rb, (((0,), (0,)), ((), ())), preferred_element_type=jnp.float32
    )
    partial_x = partial_x * math.sqrt(K / total_series)
    pieces = partial_x.reshape(n_series, rank_part, width)
    grad_x = lax.all_to_all(pieces, "series", 0, 0, tiled=True).sum(0)

    xb = x_full
    halo = lax.ppermute(xb[:, width - HALO :], TM, [(i, i + 1) for i in range(n_tm - 1)])
    first = lax.axis_index(TM) == 0
    column = lax.broadcasted_iota(jnp.int32, (1, HALO + width), 1)
    keep = jnp.logical_or(jnp.logical_not(first), column >= HALO)
    hidden = jnp.concatenate([halo, xb], axis=1).astype(jnp.float32)
    for layer in range(LAYERS):
        hb = jnp.where(keep, hidden, 0.0).astype(jnp.bfloat16)
        extended = jnp.concatenate([jnp.zeros((K, D_MAX), jnp.bfloat16), hb], axis=1)
        past = lax.dynamic_slice_in_dim(extended, D_MAX - dilations[layer], HALO + width, 1)
        hidden = conv_layer(hidden, hb, past, conv_w[layer], conv_b[layer])
    target = lax.dynamic_slice_in_dim(hidden[:, HALO:], lax.axis_index("series") * rank_part, rank_part, 0)
    basis_new = basis - 0.5 * (grad_x + (basis - target))
    return (factors_new, m_new, v_new, basis_new)


def solution(mesh):
    n_series, n_tm = mesh.devices.shape
    devices = mesh.devices.reshape(n_series, n_tm // (Y_LO * CORES), Y_LO, CORES)
    fine = Mesh(devices, ("series",) + TM)
    block = P("series", TM)
    rows = P(("series",) + TM, None)
    return jax.shard_map(
        on_device,
        mesh=fine,
        in_specs=(block, block, rows, rows, rows, block, P(), P(), P()),
        out_specs=(rows, rows, rows, block),
        check_vma=False,
    )
```

time: 518 us -> 109 us (0.21)
  the two profiles are of different devices: /device:TPU:6 before, /device:TPU:8 now
where the time goes in v1:
time: 109 us; the launch traced here: 108 us
  waiting for transfers between devices  41.1 us (38%)
  starting transfers between devices  31.6 us (29%)
  blocking collectives  9.99 us (9%)
  matrix products  7.49 us (7%)
  local copies, waits for them, and re-layouts  6.73 us (6%)
  between operations  6.03 us (6%)
  other arithmetic  4.74 us (4%)
    all_to_all x2, starting transfers between devices, gather_by_a2a(): return lax.all_to_all(copies, axis, 0, 0, tiled=True)  20.7 us
    all_to_all x1, waiting for transfers between devices, on_device(): by_row = lax.all_to_all(by_core.astype(jnp.bfloat16), ROW, 0, 0, tiled=True)  14.6 us
    all_to_all x2, waiting for transfers between devices, gather_by_a2a(): return lax.all_to_all(copies, axis, 0, 0, tiled=True)  13.9 us
    all_to_all x1, waiting for transfers between devices, on_device(): grad_x = lax.all_to_all(pieces, 'series', 0, 0, tiled=True).sum(0)  12.7 us
    all_to_all x1, starting transfers between devices, on_device(): by_row = lax.all_to_all(by_core.astype(jnp.bfloat16), ROW, 0, 0, tiled=True)  5.58 us
    all_to_all x1, blocking collectives, on_device(): by_core = lax.all_to_all(by_core, 'core', 1, 1, tiled=True).sum(1)  5.42 us
    all_to_all x1, blocking collectives, gather_by_a2a(): return lax.all_to_all(copies, axis, 0, 0, tiled=True)  4.58 us
    all_to_all x1, starting transfers between devices, on_device(): grad_x = lax.all_to_all(pieces, 'series', 0, 0, tiled=True).sum(0)  3.41 us
  transfers between devices with their start and end apart: 5, of which 4 were waited for; matrix products, arithmetic and copies ran while one was open for 8% of the time, Pallas kernels for 0%

profile of v1, /device:TPU:8, one launch (start us, length us, event | category | flops | bytes accessed | tf_op | source)
XLA Modules:
  0.0 107.7 jit_solution(7087554357061556449)
XLA Ops:
  0.6 0.8 convert_element_type.39
  2.1 8.7 %all-to-all-start.2 = ((bf16[8,16,512]{2,1,0:T(8,128)(2,1)}), bf16[8,16,512]{2,1,0:T(8,128)(2,1)S(1)}, u32[]{:S(2)}, u32[]{:S(2)}) async-start(bf16[8,16,512]{2,1,0:T(8,128)(2,1)} %broadcast_in_dim.53), calls=%async_computation.2 | async-start | bytes 262144 | tf_op jit(solution)/shard_map/all_to_all | solution.py:45
  10.7 0.8 convert_element_type.38
  11.5 1.4 %fusion.59 = (s32[1]{0:T(128)}, s32[1]{0:T(128)}, s32[1]{0:T(128)}, s32[1]{0:T(128)}) fusion(s32[4]{0:T(128)} %param.15), kind=kLoop, calls=%fused_computation.83 | loop fusion | bytes 32 | tf_op jit(solution)/shard_map/slice | solution.py:94
  12.9 9.0 %all-to-all-done.2 = bf16[8,16,512]{2,1,0:T(8,128)(2,1)S(1)} async-done(((bf16[8,16,512]{2,1,0:T(8,128)(2,1)}), bf16[8,16,512]{2,1,0:T(8,128)(2,1)S(1)}, u32[]{:S(2)}, u32[]{:S(2)}) %all-to-all-start.2) | async-done | bytes 131104 | tf_op jit(solution)/shard_map/all_to_all | solution.py:45
  21.9 0.9 broadcast_in_dim.51
  22.8 12.0 %all-to-all-start = ((bf16[32,64,128]{2,1,0:T(8,128)(2,1)}), bf16[32,64,128]{2,1,0:T(8,128)(2,1)S(1)}, u32[]{:S(2)}, u32[]{:S(2)}) async-start(bf16[32,64,128]{2,1,0:T(8,128)(2,1)} %broadcast_in_dim.51), calls=%async_computation | async-start | bytes 1048576 | tf_op jit(solution)/shard_map/all_to_all | solution.py:45
  34.8 0.8 slice_bitcast_fusion
  35.7 1.9 %collective-permute-start = (bf16[128,128]{1,0:T(8,128)(2,1)S(1)}, bf16[128,128]{1,0:T(8,128)(2,1)S(1)}, u32[]{:S(2)}, u32[]{:S(2)}) collective-permute-start(bf16[128,128]{1,0:T(8,128)(2,1)S(1)} %slice.92), channel_id=1, source_target_pairs={{0,1},{1,2},{2,3},{3,4},{4,5},{5,6},{6,7},{7,8},{8,9},{9,10},{10,1... | collective-permute-start | bytes 98312 | tf_op jit(solution)/shard_map/ppermute | solution.py:86
  43.6 1.0 fusion.19
  44.6 1.0 select_convert_fusion.2
  45.6 4.9 %all-to-all-done = bf16[32,64,128]{2,1,0:T(8,128)(2,1)S(1)} async-done(((bf16[32,64,128]{2,1,0:T(8,128)(2,1)}), bf16[32,64,128]{2,1,0:T(8,128)(2,1)S(1)}, u32[]{:S(2)}, u32[]{:S(2)}) %all-to-all-start) | async-done | bytes 524320 | tf_op jit(solution)/shard_map/all_to_all | solution.py:45
  50.8 4.6 %all_to_all.30 = bf16[2,32,64,128]{3,2,1,0:T(8,128)(2,1)S(1)} all-to-all(bf16[2,32,64,128]{3,2,1,0:T(8,128)(2,1)S(1)} %broadcast_in_dim.52), channel_id=1, replica_groups=mesh['series'=8,'z'=8,'ylo'=4,'core'=2] {'core'}, dimensions={0} | all-to-all | bytes 2097152 | tf_op jit(solution)/shard_map/all_to_all | solution.py:45
  55.5 1.1 %broadcast_in_dim.50 = f32[32,128,4,128]{3,2,1,0:T(4,128)S(1)} broadcast(f32[32,4]{1,0:T(8,128)S(1)} %copy.50), dimensions={0,2} | broadcast | bytes 8389120 | tf_op jit(solution)/shard_map/broadcast_in_dim | solution.py:23
  56.6 1.0 copy-done
  57.7 1.2 %fusion = bf16[4096,512]{1,0:T(8,128)(2,1)S(1)} fusion(f32[512,8,4,128]{3,2,1,0:T(4,128)S(1)} %bitcast.81, bf16[4096,512]{1,0:T(8,128)(2,1)S(1)} %copy-done, bf16[4096,128]{1,0:T(8,128)(2,1)S(1)} %bitcast.88, bf16[128,512]{1,0:T(8,128)(2,1)S(1)} %bitcast.86), kind=kOutput, calls=%fused_computation.1 | convolution fusion | flops 545259520 | bytes 17956864 | tf_op jit(solution)/shard_map/dot_general | solution.py:66
  58.9 1.2 %fusion.1 = f32[4096,128]{1,0:T(8,128)S(1)} fusion(bf16[4096,512]{1,0:T(8,128)(2,1)S(1)} %fusion, bf16[128,512]{1,0:T(8,128)(2,1)S(1)} %bitcast.87), kind=kOutput, calls=%fused_computation.3 | convolution fusion | flops 537919488 | bytes 6422528 | tf_op jit(solution)/shard_map/dot_general | solution.py:71
  60.2 1.5 %fusion.17 = f32[512,128]{0,1:T(8,128)} fusion(bf16[4096,512]{1,0:T(8,128)(2,1)S(1)} %fusion, bf16[4096,128]{1,0:T(8,128)(2,1)S(1)} %bitcast.89), kind=kOutput, calls=%fused_computation.24 | convolution fusion | flops 537001984 | bytes 5505024 | tf_op jit(solution)/shard_map/dot_general | solution.py:78
  61.9 5.4 %all_to_all.31 = f32[32,2,64,128]{3,2,0,1:T(8,128)S(1)} all-to-all(f32[32,2,64,128]{3,2,0,1:T(8,128)S(1)} %copy.52), channel_id=1, replica_groups=mesh['series'=8,'z'=8,'ylo'=4,'core'=2] {'core'}, dimensions={1} | all-to-all | bytes 4194304 | tf_op jit(solution)/shard_map/all_to_all | solution.py:73
  67.3 3.4 %all-to-all-start.5 = ((f32[8,16,512]{2,1,0:T(8,128)}), f32[8,16,512]{2,1,0:T(8,128)S(1)}, u32[]{:S(2)}, u32[]{:S(2)}) async-start(f32[8,16,512]{2,1,0:T(8,128)} %bitcast.90), calls=%async_computation.5 | async-start | bytes 524288 | tf_op jit(solution)/shard_map/all_to_all | solution.py:83
  71.3 1.1 %reduce_sum.27 = bf16[32,64,128]{2,1,0:T(8,128)(2,1)} reduce(f32[32,2,64,128]{3,2,0,1:T(8,128)S(1)} %all_to_all.31, f32[]{:T(128)} %constant.55.clone.1), dimensions={1}, to_apply=%region_0.0 | reduce | flops 262144 | bytes 2621444 | tf_op jit(solution)/shard_map/reduce_sum | solution.py:73
  72.4 12.7 %all-to-all-done.5 = f32[8,16,512]{2,1,0:T(8,128)S(1)} async-done(((f32[8,16,512]{2,1,0:T(8,128)}), f32[8,16,512]{2,1,0:T(8,128)S(1)}, u32[]{:S(2)}, u32[]{:S(2)}) %all-to-all-start.5) | async-done | bytes 262176 | tf_op jit(solution)/shard_map/all_to_all | solution.py:83
  85.1 5.6 %all-to-all-start.4 = ((bf16[32,64,128]{2,1,0:T(8,128)(2,1)}), bf16[32,64,128]{2,1,0:T(8,128)(2,1)S(1)}, u32[]{:S(2)}, u32[]{:S(2)}) async-start(bf16[32,64,128]{2,1,0:T(8,128)(2,1)} %reduce_sum.27), calls=%async_computation.4 | async-start | bytes 1048576 | tf_op jit(solution)/shard_map/all_to_all | solution.py:74
  92.4 14.6 %all-to-all-done.4 = bf16[32,64,128]{2,1,0:T(8,128)(2,1)S(1)} async-done(((bf16[32,64,128]{2,1,0:T(8,128)(2,1)}), bf16[32,64,128]{2,1,0:T(8,128)(2,1)S(1)}, u32[]{:S(2)}, u32[]{:S(2)}) %all-to-all-start.4) | async-done | bytes 524320 | tf_op jit(solution)/shard_map/all_to_all | solution.py:74
  (33 shorter events, 5.0 us)
Async XLA Ops:
  2.1 19.8 %all-to-all-start.2 = ((bf16[8,16,512]{2,1,0:T(8,128)(2,1)}), bf16[8,16,512]{2,1,0:T(8,128)(2,1)S(1)}, u32[]{:S(2)}, u32[]{:S(2)}) async-start(bf16[8,16,512]{2,1,0:T(8,128)(2,1)} %broadcast_in_dim.53), calls=%async_computation.2 | async-start | bytes 262144 | tf_op jit(solution)/shard_map/all_to_all | solution.py:45
  22.8 27.8 %all-to-all-start = ((bf16[32,64,128]{2,1,0:T(8,128)(2,1)}), bf16[32,64,128]{2,1,0:T(8,128)(2,1)S(1)}, u32[]{:S(2)}, u32[]{:S(2)}) async-start(bf16[32,64,128]{2,1,0:T(8,128)(2,1)} %broadcast_in_dim.51), calls=%async_computation | async-start | bytes 1048576 | tf_op jit(solution)/shard_map/all_to_all | solution.py:45
  35.7 7.9 %collective-permute-start = (bf16[128,128]{1,0:T(8,128)(2,1)S(1)}, bf16[128,128]{1,0:T(8,128)(2,1)S(1)}, u32[]{:S(2)}, u32[]{:S(2)}) collective-permute-start(bf16[128,128]{1,0:T(8,128)(2,1)S(1)} %slice.92), channel_id=1, source_target_pairs={{0,1},{1,2},{2,3},{3,4},{4,5},{5,6},{6,7},{7,8},{8,9},{9,10},{10,1... | collective-permute-start | bytes 98312 | tf_op jit(solution)/shard_map/ppermute | solution.py:86
  55.5 2.2 %copy-start = (bf16[4096,512]{1,0:T(8,128)(2,1)S(1)}, bf16[4096,512]{1,0:T(8,128)(2,1)}, u32[]{:S(2)}) copy-start(bf16[4096,512]{1,0:T(8,128)(2,1)} %param.9) | copy-start | bytes 12582916
  61.7 9.1 %copy-start.1 = (bf16[4,2,128,128]{3,2,1,0:T(8,128)(2,1)S(1)}, bf16[4,2,128,128]{3,2,1,0:T(8,128)(2,1)}, u32[]{:S(2)}) copy-start(bf16[4,2,128,128]{3,2,1,0:T(8,128)(2,1)} %param.16) | copy-start | bytes 786436
  67.3 17.8 %all-to-all-start.5 = ((f32[8,16,512]{2,1,0:T(8,128)}), f32[8,16,512]{2,1,0:T(8,128)S(1)}, u32[]{:S(2)}, u32[]{:S(2)}) async-start(f32[8,16,512]{2,1,0:T(8,128)} %bitcast.90), calls=%async_computation.5 | async-start | bytes 524288 | tf_op jit(solution)/shard_map/all_to_all | solution.py:83
  71.3 20.5 %copy-start.2 = (f32[16,512]{1,0:T(8,128)S(1)}, f32[16,512]{1,0:T(8,128)}, u32[]{:S(2)}) copy-start(f32[16,512]{1,0:T(8,128)} %param.14) | copy-start | bytes 98308
  71.3 35.8 %copy-start.3 = (f32[64,128]{1,0:T(8,128)S(1)}, f32[64,128]{1,0:T(8,128)}, u32[]{:S(2)}) copy-start(f32[64,128]{1,0:T(8,128)} %param.11) | copy-start | bytes 98308
  71.3 35.8 %copy-start.4 = (f32[64,128]{1,0:T(8,128)S(1)}, f32[64,128]{1,0:T(8,128)}, u32[]{:S(2)}) copy-start(f32[64,128]{1,0:T(8,128)} %param.12) | copy-start | bytes 98308
  71.3 35.8 %copy-start.5 = (f32[64,128]{1,0:T(8,128)S(1)}, f32[64,128]{1,0:T(8,128)}, u32[]{:S(2)}) copy-start(f32[64,128]{1,0:T(8,128)} %param.13) | copy-start | bytes 98308
  85.1 21.9 %all-to-all-start.4 = ((bf16[32,64,128]{2,1,0:T(8,128)(2,1)}), bf16[32,64,128]{2,1,0:T(8,128)(2,1)S(1)}, u32[]{:S(2)}, u32[]{:S(2)}) async-start(bf16[32,64,128]{2,1,0:T(8,128)(2,1)} %reduce_sum.27), calls=%async_computation.4 | async-start | bytes 1048576 | tf_op jit(solution)/shard_map/all_to_all | solution.py:74

commit v2 on v1

--- a/solution.py
+++ b/solution.py
@@ -45,6 +45,23 @@
     return lax.all_to_all(copies, axis, 0, 0, tiled=True)
 
 
+def gather_by_permutes(x, me, count):
+    arrived = [x] + [
+        lax.ppermute(x, "series", [(i, (i + k) % count) for i in range(count)])
+        for k in range(1, count)
+    ]
+    from_ahead = jnp.stack([arrived[(count - m) % count] for m in range(count)])
+    return jnp.roll(from_ahead, me, axis=0)
+
+
+def reduce_by_permutes(pieces, me, count):
+    total = lax.dynamic_index_in_dim(pieces, me, 0, keepdims=False)
+    for k in range(1, count):
+        piece = lax.dynamic_index_in_dim(pieces, (me + k) % count, 0, keepdims=False)
+        total = total + lax.ppermute(piece, "series", [(i, (i + k) % count) for i in range(count)])
+    return total
+
+
 def on_device(y_obs, tile_mask, factors, adam_m, adam_v, basis, dilations, conv_w, conv_b):
     own_rows = factors.shape[0]
     width = basis.shape[1]
@@ -60,7 +77,8 @@
     f_all = gather_by_a2a(f_rows, "core", CORES)
     f_block = jnp.swapaxes(f_all, 0, 1).reshape(n_tm * own_rows, K)
 
-    x_parts = gather_by_a2a(basis.astype(jnp.bfloat16), "series", n_series)
+    me = lax.axis_index("series")
+    x_parts = gather_by_permutes(basis.astype(jnp.bfloat16), me, n_series)
     x_full = x_parts.reshape(n_series * rank_part, width)
 
     pred = jnp.dot(f_block, x_full, preferred_element_type=jnp.float32)
@@ -80,7 +98,7 @@
     )
     partial_x = partial_x * math.sqrt(K / total_series)
     pieces = partial_x.reshape(n_series, rank_part, width)
-    grad_x = lax.all_to_all(pieces, "series", 0, 0, tiled=True).sum(0)
+    grad_x = reduce_by_permutes(pieces, me, n_series)
 
     xb = x_full
     halo = lax.ppermute(xb[:, width - HALO :], TM, [(i, i + 1) for i in range(n_tm - 1)])

time: 109 us -> 180 us (1.65)
  the two profiles are of different devices: /device:TPU:8 before, /device:TPU:18 now
where the time goes in v2:
time: 180 us; the launch traced here: 178 us
  starting transfers between devices  85.9 us (48%)
  waiting for transfers between devices  37.7 us (21%)
  local copies, waits for them, and re-layouts  17.1 us (10%)
  matrix products  14.1 us (8%)
  blocking collectives  11 us (6%)
  between operations  6.5 us (4%)
  other arithmetic  5.84 us (3%)
    ppermute x7, waiting for transfers between devices, reduce_by_permutes(): lax.ppermute(piece, 'series', [(i, (i + k) % count) for i in range(count)])  31.5 us
    ppermute x7, starting transfers between devices, reduce_by_permutes(): lax.ppermute(piece, 'series', [(i, (i + k) % count) for i in range(count)])  30.6 us
    ppermute x7, starting transfers between devices, gather_by_permutes(): lax.ppermute(x, 'series', [(i, (i + k) % count) for i in range(count)])  30.3 us
    all_to_all x1, starting transfers between devices, gather_by_a2a(): return lax.all_to_all(copies, axis, 0, 0, tiled=True)  13.8 us
    unnamed x33, local copies, waits for them, and re-layouts  10.3 us
    all_to_all x1, starting transfers between devices, on_device(): by_row = lax.all_to_all(by_core.astype(jnp.bfloat16), ROW, 0, 0, tiled=True)  9.2 us
    ppermute x7, waiting for transfers between devices, gather_by_permutes(): lax.ppermute(x, 'series', [(i, (i + k) % count) for i in range(count)])  6.21 us
    all_to_all x1, blocking collectives, gather_by_a2a(): return lax.all_to_all(copies, axis, 0, 0, tiled=True)  5.64 us
  transfers between devices with their start and end apart: 17, of which 5 were waited for; matrix products, arithmetic and copies ran while one was open for 14% of the time, Pallas kernels for 0%

profile of v2, /device:TPU:18, one launch (start us, length us, event | category | flops | bytes accessed | tf_op | source)
XLA Modules:
  0.0 178.2 jit_solution(16301272512122099555)
XLA Ops:
  1.4 2.4 %collective-permute-start = (bf16[16,512]{1,0:T(8,128)(2,1)S(1)}, bf16[16,512]{1,0:T(8,128)(2,1)S(1)}, u32[]{:S(2)}, u32[]{:S(2)}) collective-permute-start(bf16[16,512]{1,0:T(8,128)(2,1)S(1)} %get-tuple-element.24), channel_id=1, source_target_pairs={{0,448},{64,0},{128,64},{192,128},{256,192},{320,256},{384,320},{4... | collective-permute-start | bytes 49160 | tf_op jit(solution)/shard_map/ppermute | solution.py:50
  3.8 7.8 %collective-permute-start.1 = (bf16[16,512]{1,0:T(8,128)(2,1)S(1)}, bf16[16,512]{1,0:T(8,128)(2,1)S(1)}, u32[]{:S(2)}, u32[]{:S(2)}) collective-permute-start(bf16[16,512]{1,0:T(8,128)(2,1)S(1)} %get-tuple-element.24), channel_id=1, source_target_pairs={{0,384},{64,448},{128,0},{192,64},{256,128},{320,192},{384,256},{4... | collective-permute-start | bytes 49160 | tf_op jit(solution)/shard_map/ppermute | solution.py:50
  11.6 5.1 %collective-permute-start.2 = (bf16[16,512]{1,0:T(8,128)(2,1)S(1)}, bf16[16,512]{1,0:T(8,128)(2,1)S(1)}, u32[]{:S(2)}, u32[]{:S(2)}) collective-permute-start(bf16[16,512]{1,0:T(8,128)(2,1)S(1)} %get-tuple-element.24), channel_id=1, source_target_pairs={{0,320},{64,384},{128,448},{192,0},{256,64},{320,128},{384,192},{4... | collective-permute-start | bytes 49160 | tf_op jit(solution)/shard_map/ppermute | solution.py:50
  16.7 5.9 %collective-permute-start.3 = (bf16[16,512]{1,0:T(8,128)(2,1)S(1)}, bf16[16,512]{1,0:T(8,128)(2,1)S(1)}, u32[]{:S(2)}, u32[]{:S(2)}) collective-permute-start(bf16[16,512]{1,0:T(8,128)(2,1)S(1)} %get-tuple-element.24), channel_id=1, source_target_pairs={{0,256},{64,320},{128,384},{192,448},{256,0},{320,64},{384,128},{4... | collective-permute-start | bytes 49160 | tf_op jit(solution)/shard_map/ppermute | solution.py:50
  22.6 3.5 %collective-permute-start.4 = (bf16[16,512]{1,0:T(8,128)(2,1)S(1)}, bf16[16,512]{1,0:T(8,128)(2,1)S(1)}, u32[]{:S(2)}, u32[]{:S(2)}) collective-permute-start(bf16[16,512]{1,0:T(8,128)(2,1)S(1)} %get-tuple-element.24), channel_id=1, source_target_pairs={{0,192},{64,256},{128,320},{192,384},{256,448},{320,0},{384,64},{4... | collective-permute-start | bytes 49160 | tf_op jit(solution)/shard_map/ppermute | solution.py:50
  27.8 13.8 %all-to-all-start = ((bf16[32,64,128]{2,1,0:T(8,128)(2,1)}), bf16[32,64,128]{2,1,0:T(8,128)(2,1)S(1)}, u32[]{:S(2)}, u32[]{:S(2)}) async-start(bf16[32,64,128]{2,1,0:T(8,128)(2,1)} %broadcast_in_dim.45), calls=%async_computation | async-start | bytes 1048576 | tf_op jit(solution)/shard_map/all_to_all | solution.py:45
  45.8 3.7 %collective-permute-start.6 = (bf16[16,512]{1,0:T(8,128)(2,1)S(1)}, bf16[16,512]{1,0:T(8,128)(2,1)S(1)}, u32[]{:S(2)}, u32[]{:S(2)}) collective-permute-start(bf16[16,512]{1,0:T(8,128)(2,1)S(1)} %get-tuple-element.24), channel_id=1, source_target_pairs={{0,64},{64,128},{128,192},{192,256},{256,320},{320,384},{384,448},... | collective-permute-start | bytes 49160 | tf_op jit(solution)/shard_map/ppermute | solution.py:50
  49.6 6.2 %collective-permute-done.5 = bf16[16,512]{1,0:T(8,128)(2,1)S(1)} collective-permute-done((bf16[16,512]{1,0:T(8,128)(2,1)S(1)}, bf16[16,512]{1,0:T(8,128)(2,1)S(1)}, u32[]{:S(2)}, u32[]{:S(2)}) %collective-permute-start.5) | collective-permute-done | bytes 16416 | tf_op jit(solution)/shard_map/ppermute | solution.py:50
  56.1 1.9 %collective-permute-start.14 = (bf16[128,128]{0,1:T(8,128)(2,1)S(1)}, bf16[128,128]{0,1:T(8,128)(2,1)S(1)}, u32[]{:S(2)}, u32[]{:S(2)}) collective-permute-start(bf16[128,128]{0,1:T(8,128)(2,1)S(1)} %slice.92), channel_id=1, source_target_pairs={{0,1},{1,2},{2,3},{3,4},{4,5},{5,6},{6,7},{7,8},{8,9},{9,10},{10,1... | collective-permute-start | bytes 98312 | tf_op jit(solution)/shard_map/ppermute | solution.py:104
  65.6 6.4 %copy.62 = bf16[4096,512]{0,1:T(8,128)(2,1)} copy(bf16[4096,512]{1,0:T(8,128)(2,1)} %param.9) | data formatting | bytes 8388608 | tf_op args[0]
  74.7 5.6 %all_to_all.20 = bf16[2,32,64,128]{3,2,1,0:T(8,128)(2,1)S(1)} all-to-all(bf16[2,32,64,128]{3,2,1,0:T(8,128)(2,1)S(1)} %broadcast_in_dim.46), channel_id=1, replica_groups=mesh['series'=8,'z'=8,'ylo'=4,'core'=2] {'core'}, dimensions={0} | all-to-all | bytes 2097152 | tf_op jit(solution)/shard_map/all_to_all | solution.py:45
  82.6 5.0 %fusion = bf16[4096,512]{0,1:T(8,128)(2,1)S(1)} fusion(f32[64,8,32,128]{3,2,1,0:T(8,128)S(1)} %bitcast.134, bf16[4096,512]{0,1:T(8,128)(2,1)S(1)} %copy-done.1, bf16[128,512]{1,0:T(8,128)(2,1)S(1)} %bitcast.139, bf16[4096,128]{1,0:T(8,128)(2,1)S(1)} %bitcast.136), kind=kOutput, calls=%fused_computation.1 | convolution fusion | flops 545259520 | bytes 17956864 | tf_op jit(solution)/shard_map/dot_general | solution.py:84
  89.6 5.4 %all_to_all.21 = f32[32,2,64,128]{3,2,0,1:T(8,128)S(1)} all-to-all(f32[32,2,64,128]{3,2,0,1:T(8,128)S(1)} %copy.64), channel_id=1, replica_groups=mesh['series'=8,'z'=8,'ylo'=4,'core'=2] {'core'}, dimensions={1} | all-to-all | bytes 4194304 | tf_op jit(solution)/shard_map/all_to_all | solution.py:91
  96.1 9.2 %all-to-all-start.3 = ((bf16[32,64,128]{2,1,0:T(8,128)(2,1)}), bf16[32,64,128]{2,1,0:T(8,128)(2,1)S(1)}, u32[]{:S(2)}, u32[]{:S(2)}) async-start(bf16[32,64,128]{2,1,0:T(8,128)(2,1)} %reduce_sum.18), calls=%async_computation.3 | async-start | bytes 1048576 | tf_op jit(solution)/shard_map/all_to_all | solution.py:92
  105.3 3.7 %fusion.17 = f32[512,128]{0,1:T(8,128)S(1)} fusion(bf16[4096,512]{0,1:T(8,128)(2,1)} %copy-done, bf16[4096,128]{1,0:T(8,128)(2,1)S(1)} %bitcast.137), kind=kOutput, calls=%fused_computation.25 | convolution fusion | flops 537001984 | bytes 5505024 | tf_op jit(solution)/shard_map/dot_general | solution.py:96
  109.9 5.0 %collective-permute-start.10 = (f32[16,512]{0,1:T(8,128)}, f32[16,512]{0,1:T(8,128)}, u32[]{:S(2)}, u32[]{:S(2)}) collective-permute-start(f32[16,512]{0,1:T(8,128)} %bitcast.21), channel_id=1, source_target_pairs={{0,256},{64,320},{128,384},{192,448},{256,0},{320,64},{384,128},{4... | collective-permute-start | bytes 98312 | tf_op jit(solution)/shard_map/ppermute | solution.py:61
  115.1 4.1 %collective-permute-start.11 = (f32[16,512]{0,1:T(8,128)S(1)}, f32[16,512]{0,1:T(8,128)}, u32[]{:S(2)}, u32[]{:S(2)}) collective-permute-start(f32[16,512]{0,1:T(8,128)S(1)} %bitcast.147), channel_id=1, source_target_pairs={{0,320},{64,384},{128,448},{192,0},{256,64},{320,128},{384,192},{4... | collective-permute-start | bytes 98312 | tf_op jit(solution)/shard_map/ppermute | solution.py:61
  120.3 9.5 %collective-permute-start.12 = (f32[16,512]{0,1:T(8,128)S(1)}, f32[16,512]{0,1:T(8,128)}, u32[]{:S(2)}, u32[]{:S(2)}) collective-permute-start(f32[16,512]{0,1:T(8,128)S(1)} %bitcast.142), channel_id=1, source_target_pairs={{0,384},{64,448},{128,0},{192,64},{256,128},{320,192},{384,256},{4... | collective-permute-start | bytes 98312 | tf_op jit(solution)/shard_map/ppermute | solution.py:61
  130.0 1.9 %collective-permute-start.13 = (f32[16,512]{0,1:T(8,128)S(1)}, f32[16,512]{0,1:T(8,128)}, u32[]{:S(2)}, u32[]{:S(2)}) collective-permute-start(f32[16,512]{0,1:T(8,128)S(1)} %bitcast.143), channel_id=1, source_target_pairs={{0,448},{64,0},{128,64},{192,128},{256,192},{320,256},{384,320},{4... | collective-permute-start | bytes 98312 | tf_op jit(solution)/shard_map/ppermute | solution.py:61
  132.1 3.9 %collective-permute-start.7 = (f32[16,512]{0,1:T(8,128)S(1)}, f32[16,512]{0,1:T(8,128)}, u32[]{:S(2)}, u32[]{:S(2)}) collective-permute-start(f32[16,512]{0,1:T(8,128)S(1)} %bitcast.144), channel_id=1, source_target_pairs={{0,64},{64,128},{128,192},{192,256},{256,320},{320,384},{384,448},... | collective-permute-start | bytes 98312 | tf_op jit(solution)/shard_map/ppermute | solution.py:61
  137.7 4.2 %collective-permute-start.8 = (f32[16,512]{0,1:T(8,128)S(1)}, f32[16,512]{0,1:T(8,128)}, u32[]{:S(2)}, u32[]{:S(2)}) collective-permute-start(f32[16,512]{0,1:T(8,128)S(1)} %bitcast.146), channel_id=1, source_target_pairs={{0,128},{64,192},{128,256},{192,320},{256,384},{320,448},{384,0},{... | collective-permute-start | bytes 98312 | tf_op jit(solution)/shard_map/ppermute | solution.py:61
  142.0 16.9 %collective-permute-done.11 = f32[16,512]{0,1:T(8,128)} collective-permute-done((f32[16,512]{0,1:T(8,128)S(1)}, f32[16,512]{0,1:T(8,128)}, u32[]{:S(2)}, u32[]{:S(2)}) %collective-permute-start.11) | collective-permute-done | bytes 32800 | tf_op jit(solution)/shard_map/ppermute | solution.py:61
  162.0 8.8 %collective-permute-done.8 = f32[16,512]{0,1:T(8,128)} collective-permute-done((f32[16,512]{0,1:T(8,128)S(1)}, f32[16,512]{0,1:T(8,128)}, u32[]{:S(2)}, u32[]{:S(2)}) %collective-permute-start.8) | collective-permute-done | bytes 32800 | tf_op jit(solution)/shard_map/ppermute | solution.py:61
  170.8 4.3 %collective-permute-done.9 = f32[16,512]{0,1:T(8,128)} collective-permute-done((f32[16,512]{0,1:T(8,128)S(1)}, f32[16,512]{0,1:T(8,128)}, u32[]{:S(2)}, u32[]{:S(2)}) %collective-permute-start.9) | collective-permute-done | bytes 32800 | tf_op jit(solution)/shard_map/ppermute | solution.py:61
  (87 shorter events, 27.2 us)
Async XLA Ops:
  1.4 42.5 %collective-permute-start = (bf16[16,512]{1,0:T(8,128)(2,1)S(1)}, bf16[16,512]{1,0:T(8,128)(2,1)S(1)}, u32[]{:S(2)}, u32[]{:S(2)}) collective-permute-start(bf16[16,512]{1,0:T(8,128)(2,1)S(1)} %get-tuple-element.24), channel_id=1, source_target_pairs={{0,448},{64,0},{128,64},{192,128},{256,192},{320,256},{384,320},{4... | collective-permute-start | bytes 49160 | tf_op jit(solution)/shard_map/ppermute | solution.py:50
  3.8 42.0 %collective-permute-start.1 = (bf16[16,512]{1,0:T(8,128)(2,1)S(1)}, bf16[16,512]{1,0:T(8,128)(2,1)S(1)}, u32[]{:S(2)}, u32[]{:S(2)}) collective-permute-start(bf16[16,512]{1,0:T(8,128)(2,1)S(1)} %get-tuple-element.24), channel_id=1, source_target_pairs={{0,384},{64,448},{128,0},{192,64},{256,128},{320,192},{384,256},{4... | collective-permute-start | bytes 49160 | tf_op jit(solution)/shard_map/ppermute | solution.py:50
  11.6 37.9 %collective-permute-start.2 = (bf16[16,512]{1,0:T(8,128)(2,1)S(1)}, bf16[16,512]{1,0:T(8,128)(2,1)S(1)}, u32[]{:S(2)}, u32[]{:S(2)}) collective-permute-start(bf16[16,512]{1,0:T(8,128)(2,1)S(1)} %get-tuple-element.24), channel_id=1, source_target_pairs={{0,320},{64,384},{128,448},{192,0},{256,64},{320,128},{384,192},{4... | collective-permute-start | bytes 49160 | tf_op jit(solution)/shard_map/ppermute | solution.py:50
  16.7 32.9 %collective-permute-start.3 = (bf16[16,512]{1,0:T(8,128)(2,1)S(1)}, bf16[16,512]{1,0:T(8,128)(2,1)S(1)}, u32[]{:S(2)}, u32[]{:S(2)}) collective-permute-start(bf16[16,512]{1,0:T(8,128)(2,1)S(1)} %get-tuple-element.24), channel_id=1, source_target_pairs={{0,256},{64,320},{128,384},{192,448},{256,0},{320,64},{384,128},{4... | collective-permute-start | bytes 49160 | tf_op jit(solution)/shard_map/ppermute | solution.py:50
  22.6 27.0 %collective-permute-start.4 = (bf16[16,512]{1,0:T(8,128)(2,1)S(1)}, bf16[16,512]{1,0:T(8,128)(2,1)S(1)}, u32[]{:S(2)}, u32[]{:S(2)}) collective-permute-start(bf16[16,512]{1,0:T(8,128)(2,1)S(1)} %get-tuple-element.24), channel_id=1, source_target_pairs={{0,192},{64,256},{128,320},{192,384},{256,448},{320,0},{384,64},{4... | collective-permute-start | bytes 49160 | tf_op jit(solution)/shard_map/ppermute | solution.py:50
  27.8 46.6 %all-to-all-start = ((bf16[32,64,128]{2,1,0:T(8,128)(2,1)}), bf16[32,64,128]{2,1,0:T(8,128)(2,1)S(1)}, u32[]{:S(2)}, u32[]{:S(2)}) async-start(bf16[32,64,128]{2,1,0:T(8,128)(2,1)} %broadcast_in_dim.45), calls=%async_computation | async-start | bytes 1048576 | tf_op jit(solution)/shard_map/all_to_all | solution.py:45
  43.9 11.9 %collective-permute-start.5 = (bf16[16,512]{1,0:T(8,128)(2,1)S(1)}, bf16[16,512]{1,0:T(8,128)(2,1)S(1)}, u32[]{:S(2)}, u32[]{:S(2)}) collective-permute-start(bf16[16,512]{1,0:T(8,128)(2,1)S(1)} %get-tuple-element.24), channel_id=1, source_target_pairs={{0,128},{64,192},{128,256},{192,320},{256,384},{320,448},{384,0},{... | collective-permute-start | bytes 49160 | tf_op jit(solution)/shard_map/ppermute | solution.py:50
  45.8 10.0 %collective-permute-start.6 = (bf16[16,512]{1,0:T(8,128)(2,1)S(1)}, bf16[16,512]{1,0:T(8,128)(2,1)S(1)}, u32[]{:S(2)}, u32[]{:S(2)}) collective-permute-start(bf16[16,512]{1,0:T(8,128)(2,1)S(1)} %get-tuple-element.24), channel_id=1, source_target_pairs={{0,64},{64,128},{128,192},{192,256},{256,320},{320,384},{384,448},... | collective-permute-start | bytes 49160 | tf_op jit(solution)/shard_map/ppermute | solution.py:50
  56.1 15.9 %collective-permute-start.14 = (bf16[128,128]{0,1:T(8,128)(2,1)S(1)}, bf16[128,128]{0,1:T(8,128)(2,1)S(1)}, u32[]{:S(2)}, u32[]{:S(2)}) collective-permute-start(bf16[128,128]{0,1:T(8,128)(2,1)S(1)} %slice.92), channel_id=1, source_target_pairs={{0,1},{1,2},{2,3},{3,4},{4,5},{5,6},{6,7},{7,8},{8,9},{9,10},{10,1... | collective-permute-start | bytes 98312 | tf_op jit(solution)/shard_map/ppermute | solution.py:104
  65.6 6.6 %copy-start.4 = (bf16[4,2,128,128]{3,2,1,0:T(8,128)(2,1)S(1)}, bf16[4,2,128,128]{3,2,1,0:T(8,128)(2,1)}, u32[]{:S(2)}) copy-start(bf16[4,2,128,128]{3,2,1,0:T(8,128)(2,1)} %param.16) | copy-start | bytes 786436
  80.4 2.2 %copy-start.1 = (bf16[4096,512]{0,1:T(8,128)(2,1)S(1)}, bf16[4096,512]{0,1:T(8,128)(2,1)}, u32[]{:S(2)}) copy-start(bf16[4096,512]{0,1:T(8,128)(2,1)} %copy.62) | copy-start | bytes 12582916
  96.1 81.3 %all-to-all-start.3 = ((bf16[32,64,128]{2,1,0:T(8,128)(2,1)}), bf16[32,64,128]{2,1,0:T(8,128)(2,1)S(1)}, u32[]{:S(2)}, u32[]{:S(2)}) async-start(bf16[32,64,128]{2,1,0:T(8,128)(2,1)} %reduce_sum.18), calls=%async_computation.3 | async-start | bytes 1048576 | tf_op jit(solution)/shard_map/all_to_all | solution.py:92
  109.0 52.8 %copy-start.2 = (f32[128,640]{0,1:T(8,128)S(1)}, f32[128,640]{0,1:T(8,128)}, u32[]{:S(2)}) copy-start(f32[128,640]{0,1:T(8,128)} %get-tuple-element.46) | copy-start | bytes 983044
  109.1 66.1 %copy-start.3 = (f32[16,512]{0,1:T(8,128)S(1)}, f32[16,512]{0,1:T(8,128)}, u32[]{:S(2)}) copy-start(f32[16,512]{0,1:T(8,128)} %copy.78) | copy-start | bytes 98308
  109.9 27.8 %collective-permute-start.10 = (f32[16,512]{0,1:T(8,128)}, f32[16,512]{0,1:T(8,128)}, u32[]{:S(2)}, u32[]{:S(2)}) collective-permute-start(f32[16,512]{0,1:T(8,128)} %bitcast.21), channel_id=1, source_target_pairs={{0,256},{64,320},{128,384},{192,448},{256,0},{320,64},{384,128},{4... | collective-permute-start | bytes 98312 | tf_op jit(solution)/shard_map/ppermute | solution.py:61
  115.0 62.6 %copy-start.5 = (f32[64,128]{1,0:T(8,128)S(1)}, f32[64,128]{1,0:T(8,128)}, u32[]{:S(2)}) copy-start(f32[64,128]{1,0:T(8,128)} %param.11) | copy-start | bytes 98308
  115.0 62.6 %copy-start.6 = (f32[64,128]{1,0:T(8,128)S(1)}, f32[64,128]{1,0:T(8,128)}, u32[]{:S(2)}) copy-start(f32[64,128]{1,0:T(8,128)} %param.12) | copy-start | bytes 98308
  115.0 62.6 %copy-start.7 = (f32[64,128]{1,0:T(8,128)S(1)}, f32[64,128]{1,0:T(8,128)}, u32[]{:S(2)}) copy-start(f32[64,128]{1,0:T(8,128)} %param.13) | copy-start | bytes 98308
  115.1 43.8 %collective-permute-start.11 = (f32[16,512]{0,1:T(8,128)S(1)}, f32[16,512]{0,1:T(8,128)}, u32[]{:S(2)}, u32[]{:S(2)}) collective-permute-start(f32[16,512]{0,1:T(8,128)S(1)} %bitcast.147), channel_id=1, source_target_pairs={{0,320},{64,384},{128,448},{192,0},{256,64},{320,128},{384,192},{4... | collective-permute-start | bytes 98312 | tf_op jit(solution)/shard_map/ppermute | solution.py:61
  120.3 41.6 %collective-permute-start.12 = (f32[16,512]{0,1:T(8,128)S(1)}, f32[16,512]{0,1:T(8,128)}, u32[]{:S(2)}, u32[]{:S(2)}) collective-permute-start(f32[16,512]{0,1:T(8,128)S(1)} %bitcast.142), channel_id=1, source_target_pairs={{0,384},{64,448},{128,0},{192,64},{256,128},{320,192},{384,256},{4... | collective-permute-start | bytes 98312 | tf_op jit(solution)/shard_map/ppermute | solution.py:61
  130.0 32.0 %collective-permute-start.13 = (f32[16,512]{0,1:T(8,128)S(1)}, f32[16,512]{0,1:T(8,128)}, u32[]{:S(2)}, u32[]{:S(2)}) collective-permute-start(f32[16,512]{0,1:T(8,128)S(1)} %bitcast.143), channel_id=1, source_target_pairs={{0,448},{64,0},{128,64},{192,128},{256,192},{320,256},{384,320},{4... | collective-permute-start | bytes 98312 | tf_op jit(solution)/shard_map/ppermute | solution.py:61
  132.1 29.9 %collective-permute-start.7 = (f32[16,512]{0,1:T(8,128)S(1)}, f32[16,512]{0,1:T(8,128)}, u32[]{:S(2)}, u32[]{:S(2)}) collective-permute-start(f32[16,512]{0,1:T(8,128)S(1)} %bitcast.144), channel_id=1, source_target_pairs={{0,64},{64,128},{128,192},{192,256},{256,320},{320,384},{384,448},... | collective-permute-start | bytes 98312 | tf_op jit(solution)/shard_map/ppermute | solution.py:61
  137.7 33.1 %collective-permute-start.8 = (f32[16,512]{0,1:T(8,128)S(1)}, f32[16,512]{0,1:T(8,128)}, u32[]{:S(2)}, u32[]{:S(2)}) collective-permute-start(f32[16,512]{0,1:T(8,128)S(1)} %bitcast.146), channel_id=1, source_target_pairs={{0,128},{64,192},{128,256},{192,320},{256,384},{320,448},{384,0},{... | collective-permute-start | bytes 98312 | tf_op jit(solution)/shard_map/ppermute | solution.py:61
  158.9 16.2 %collective-permute-start.9 = (f32[16,512]{0,1:T(8,128)S(1)}, f32[16,512]{0,1:T(8,128)}, u32[]{:S(2)}, u32[]{:S(2)}) collective-permute-start(f32[16,512]{0,1:T(8,128)S(1)} %bitcast.145), channel_id=1, source_target_pairs={{0,192},{64,256},{128,320},{192,384},{256,448},{320,0},{384,64},{4... | collective-permute-start | bytes 98312 | tf_op jit(solution)/shard_map/ppermute | solution.py:61
  (1 other events, 2.0 us)

commit v3 on v1

--- a/solution.py
+++ b/solution.py
@@ -70,7 +70,8 @@
     contract_time = (((1,), (1,)), ((), ()))
     partial_f = -lax.dot_general(rb, x_full, contract_time, preferred_element_type=jnp.float32) * scale_f
     by_core = partial_f.reshape(n_row, CORES, own_rows, K)
-    by_core = lax.all_to_all(by_core, "core", 1, 1, tiled=True).sum(1)
+    by_core = lax.all_to_all(by_core.astype(jnp.bfloat16), "core", 1, 1, tiled=True)
+    by_core = by_core.astype(jnp.float32).sum(1)
     by_row = lax.all_to_all(by_core.astype(jnp.bfloat16), ROW, 0, 0, tiled=True)
     grad_f = by_row.astype(jnp.float32).sum(0)
     factors_new, m_new, v_new = adam_update(factors, adam_m, adam_v, grad_f)
@@ -80,7 +81,8 @@
     )
     partial_x = partial_x * math.sqrt(K / total_series)
     pieces = partial_x.reshape(n_series, rank_part, width)
-    grad_x = lax.all_to_all(pieces, "series", 0, 0, tiled=True).sum(0)
+    arrived = lax.all_to_all(pieces.astype(jnp.bfloat16), "series", 0, 0, tiled=True)
+    grad_x = arrived.astype(jnp.float32).sum(0)
 
     xb = x_full
     halo = lax.ppermute(xb[:, width - HALO :], TM, [(i, i + 1) for i in range(n_tm - 1)])

time: 109 us -> 106 us (0.972)
  waiting for transfers between devices: 41.1 us -> 37.7 us
  starting transfers between devices: 31.6 us -> 33.2 us
    all_to_all x1, waiting for transfers between devices: 12.7 us -> 8.99 us  [on_device(): lax.all_to_all(pieces.astype(jnp.bfloat16), 'series', 0, 0, tiled=True)]
    all_to_all x1, starting transfers between devices: 5.58 us -> 7.02 us  [on_device(): by_row = lax.all_to_all(by_core.astype(jnp.bfloat16), ROW, 0, 0, tiled=True)]
  transfers between devices with their start and end apart: 5 -> 5, of which waited for: 4 -> 4; matrix products, arithmetic and copies ran while one was open for 8% -> 9% of each run, Pallas kernels for 0% -> 0%
where the time goes in v3:
time: 106 us; the launch traced here: 105 us
  waiting for transfers between devices  37.7 us (36%)
  starting transfers between devices  33.2 us (31%)
  blocking collectives  9.15 us (9%)
  matrix products  7.45 us (7%)
  local copies, waits for them, and re-layouts  6.56 us (6%)
  between operations  6.03 us (6%)
  other arithmetic  4.84 us (5%)
    all_to_all x2, starting transfers between devices, gather_by_a2a(): return lax.all_to_all(copies, axis, 0, 0, tiled=True)  20.7 us
    all_to_all x1, waiting for transfers between devices, on_device(): by_row = lax.all_to_all(by_core.astype(jnp.bfloat16), ROW, 0, 0, tiled=True)  15.4 us
    all_to_all x2, waiting for transfers between devices, gather_by_a2a(): return lax.all_to_all(copies, axis, 0, 0, tiled=True)  13.4 us
    all_to_all x1, waiting for transfers between devices, on_device(): lax.all_to_all(pieces.astype(jnp.bfloat16), 'series', 0, 0, tiled=True)  8.99 us
    all_to_all x1, starting transfers between devices, on_device(): by_row = lax.all_to_all(by_core.astype(jnp.bfloat16), ROW, 0, 0, tiled=True)  7.02 us
    all_to_all x1, blocking collectives, on_device(): lax.all_to_all(by_core.astype(jnp.bfloat16), 'core', 1, 1, tiled=True)  4.58 us
    all_to_all x1, blocking collectives, gather_by_a2a(): return lax.all_to_all(copies, axis, 0, 0, tiled=True)  4.58 us
    all_to_all x1, starting transfers between devices, on_device(): lax.all_to_all(pieces.astype(jnp.bfloat16), 'series', 0, 0, tiled=True)  3.5 us
  transfers between devices with their start and end apart: 5, of which 4 were waited for; matrix products, arithmetic and copies ran while one was open for 9% of the time, Pallas kernels for 0%

profile of v3, /device:TPU:8, one launch (start us, length us, event | category | flops | bytes accessed | tf_op | source)
XLA Modules:
  0.0 104.9 jit_solution(3054240931537746409)
XLA Ops:
  0.6 0.8 convert_element_type.56
  2.1 8.7 %all-to-all-start.2 = ((bf16[8,16,512]{2,1,0:T(8,128)(2,1)}), bf16[8,16,512]{2,1,0:T(8,128)(2,1)S(1)}, u32[]{:S(2)}, u32[]{:S(2)}) async-start(bf16[8,16,512]{2,1,0:T(8,128)(2,1)} %broadcast_in_dim.53), calls=%async_computation.2 | async-start | bytes 262144 | tf_op jit(solution)/shard_map/all_to_all | solution.py:45
  10.8 1.4 %fusion.61 = (s32[1]{0:T(128)}, s32[1]{0:T(128)}, s32[1]{0:T(128)}, s32[1]{0:T(128)}) fusion(s32[4]{0:T(128)} %param.15), kind=kLoop, calls=%fused_computation.86 | loop fusion | bytes 32 | tf_op jit(solution)/shard_map/slice | solution.py:96
  12.2 0.8 convert_element_type.55
  12.9 0.8 slice_bitcast_fusion
  13.8 8.1 %all-to-all-done.2 = bf16[8,16,512]{2,1,0:T(8,128)(2,1)S(1)} async-done(((bf16[8,16,512]{2,1,0:T(8,128)(2,1)}), bf16[8,16,512]{2,1,0:T(8,128)(2,1)S(1)}, u32[]{:S(2)}, u32[]{:S(2)}) %all-to-all-start.2) | async-done | bytes 131104 | tf_op jit(solution)/shard_map/all_to_all | solution.py:45
  21.9 0.9 broadcast_in_dim.51
  22.8 12.0 %all-to-all-start = ((bf16[32,64,128]{2,1,0:T(8,128)(2,1)}), bf16[32,64,128]{2,1,0:T(8,128)(2,1)S(1)}, u32[]{:S(2)}, u32[]{:S(2)}) async-start(bf16[32,64,128]{2,1,0:T(8,128)(2,1)} %broadcast_in_dim.51), calls=%async_computation | async-start | bytes 1048576 | tf_op jit(solution)/shard_map/all_to_all | solution.py:45
  34.9 1.9 %collective-permute-start = (bf16[128,128]{1,0:T(8,128)(2,1)S(1)}, bf16[128,128]{1,0:T(8,128)(2,1)S(1)}, u32[]{:S(2)}, u32[]{:S(2)}) collective-permute-start(bf16[128,128]{1,0:T(8,128)(2,1)S(1)} %slice.92), channel_id=1, source_target_pairs={{0,1},{1,2},{2,3},{3,4},{4,5},{5,6},{6,7},{7,8},{8,9},{9,10},{10,1... | collective-permute-start | bytes 98312 | tf_op jit(solution)/shard_map/ppermute | solution.py:88
  42.8 1.0 fusion.21
  43.9 1.0 select_convert_fusion.2
  45.4 5.2 %all-to-all-done = bf16[32,64,128]{2,1,0:T(8,128)(2,1)S(1)} async-done(((bf16[32,64,128]{2,1,0:T(8,128)(2,1)}), bf16[32,64,128]{2,1,0:T(8,128)(2,1)S(1)}, u32[]{:S(2)}, u32[]{:S(2)}) %all-to-all-start) | async-done | bytes 524320 | tf_op jit(solution)/shard_map/all_to_all | solution.py:45
  50.9 4.6 %all_to_all.30 = bf16[2,32,64,128]{3,2,1,0:T(8,128)(2,1)S(1)} all-to-all(bf16[2,32,64,128]{3,2,1,0:T(8,128)(2,1)S(1)} %broadcast_in_dim.52), channel_id=1, replica_groups=mesh['series'=8,'z'=8,'ylo'=4,'core'=2] {'core'}, dimensions={0} | all-to-all | bytes 2097152 | tf_op jit(solution)/shard_map/all_to_all | solution.py:45
  55.5 1.1 %broadcast_in_dim.50 = f32[32,128,4,128]{3,2,1,0:T(4,128)S(1)} broadcast(f32[32,4]{1,0:T(8,128)S(1)} %copy.50), dimensions={0,2} | broadcast | bytes 8389120 | tf_op jit(solution)/shard_map/broadcast_in_dim | solution.py:23
  56.7 1.0 copy-done
  57.7 1.2 %fusion = bf16[4096,512]{1,0:T(8,128)(2,1)S(1)} fusion(f32[512,8,4,128]{3,2,1,0:T(4,128)S(1)} %bitcast.81, bf16[4096,512]{1,0:T(8,128)(2,1)S(1)} %copy-done, bf16[4096,128]{1,0:T(8,128)(2,1)S(1)} %bitcast.82, bf16[128,512]{1,0:T(8,128)(2,1)S(1)} %bitcast.87), kind=kOutput, calls=%fused_computation.1 | convolution fusion | flops 545259520 | bytes 17956864 | tf_op jit(solution)/shard_map/dot_general | solution.py:66
  59.0 1.2 %fusion.2 = bf16[4096,128]{1,0:T(8,128)(2,1)S(1)} fusion(bf16[4096,512]{1,0:T(8,128)(2,1)S(1)} %fusion, bf16[128,512]{1,0:T(8,128)(2,1)S(1)} %bitcast.88), kind=kOutput, calls=%fused_computation.4 | convolution fusion | flops 538443776 | bytes 5373952 | tf_op jit(solution)/shard_map/dot_general | solution.py:71
  60.2 1.5 %fusion.19 = bf16[512,128]{0,1:T(8,128)(2,1)} fusion(bf16[4096,512]{1,0:T(8,128)(2,1)S(1)} %fusion, bf16[4096,128]{1,0:T(8,128)(2,1)S(1)} %bitcast.83), kind=kOutput, calls=%fused_computation.26 | convolution fusion | flops 537067520 | bytes 5373952 | tf_op jit(solution)/shard_map/dot_general | solution.py:79
  61.8 4.6 %all_to_all.31 = bf16[32,2,64,128]{3,2,0,1:T(8,128)(2,1)S(1)} all-to-all(bf16[32,2,64,128]{3,2,0,1:T(8,128)(2,1)S(1)} %copy.52), channel_id=1, replica_groups=mesh['series'=8,'z'=8,'ylo'=4,'core'=2] {'core'}, dimensions={1} | all-to-all | bytes 2097152 | tf_op jit(solution)/shard_map/all_to_all | solution.py:73
  66.4 3.5 %all-to-all-start.5 = ((bf16[8,16,512]{2,1,0:T(8,128)(2,1)}), bf16[8,16,512]{2,1,0:T(8,128)(2,1)S(1)}, u32[]{:S(2)}, u32[]{:S(2)}) async-start(bf16[8,16,512]{2,1,0:T(8,128)(2,1)} %bitcast.6), calls=%async_computation.5 | async-start | bytes 262144 | tf_op jit(solution)/shard_map/all_to_all | solution.py:84
  70.2 1.1 %reduce_sum.30 = bf16[32,64,128]{2,1,0:T(8,128)(2,1)} reduce(bf16[32,2,64,128]{3,2,0,1:T(8,128)(2,1)S(1)} %all_to_all.31, bf16[]{:T(256)} %constant.56.clone.1), dimensions={1}, to_apply=%region_0.0 | reduce | flops 262144 | bytes 1572866 | tf_op jit(solution)/shard_map/reduce_sum | solution.py:74
  71.3 9.0 %all-to-all-done.5 = bf16[8,16,512]{2,1,0:T(8,128)(2,1)S(1)} async-done(((bf16[8,16,512]{2,1,0:T(8,128)(2,1)}), bf16[8,16,512]{2,1,0:T(8,128)(2,1)S(1)}, u32[]{:S(2)}, u32[]{:S(2)}) %all-to-all-start.5) | async-done | bytes 131104 | tf_op jit(solution)/shard_map/all_to_all | solution.py:84
  80.3 7.0 %all-to-all-start.4 = ((bf16[32,64,128]{2,1,0:T(8,128)(2,1)}), bf16[32,64,128]{2,1,0:T(8,128)(2,1)S(1)}, u32[]{:S(2)}, u32[]{:S(2)}) async-start(bf16[32,64,128]{2,1,0:T(8,128)(2,1)} %reduce_sum.30), calls=%async_computation.4 | async-start | bytes 1048576 | tf_op jit(solution)/shard_map/all_to_all | solution.py:75
  88.8 15.4 %all-to-all-done.4 = bf16[32,64,128]{2,1,0:T(8,128)(2,1)S(1)} async-done(((bf16[32,64,128]{2,1,0:T(8,128)(2,1)}), bf16[32,64,128]{2,1,0:T(8,128)(2,1)S(1)}, u32[]{:S(2)}, u32[]{:S(2)}) %all-to-all-start.4) | async-done | bytes 524320 | tf_op jit(solution)/shard_map/all_to_all | solution.py:75
  (33 shorter events, 4.8 us)
Async XLA Ops:
  0.6 44.2 %copy-start.1 = (bf16[4,2,128,128]{3,2,1,0:T(8,128)(2,1)S(1)}, bf16[4,2,128,128]{3,2,1,0:T(8,128)(2,1)}, u32[]{:S(2)}) copy-start(bf16[4,2,128,128]{3,2,1,0:T(8,128)(2,1)} %param.16) | copy-start | bytes 786436
  2.1 19.8 %all-to-all-start.2 = ((bf16[8,16,512]{2,1,0:T(8,128)(2,1)}), bf16[8,16,512]{2,1,0:T(8,128)(2,1)S(1)}, u32[]{:S(2)}, u32[]{:S(2)}) async-start(bf16[8,16,512]{2,1,0:T(8,128)(2,1)} %broadcast_in_dim.53), calls=%async_computation.2 | async-start | bytes 262144 | tf_op jit(solution)/shard_map/all_to_all | solution.py:45
  22.8 27.8 %all-to-all-start = ((bf16[32,64,128]{2,1,0:T(8,128)(2,1)}), bf16[32,64,128]{2,1,0:T(8,128)(2,1)S(1)}, u32[]{:S(2)}, u32[]{:S(2)}) async-start(bf16[32,64,128]{2,1,0:T(8,128)(2,1)} %broadcast_in_dim.51), calls=%async_computation | async-start | bytes 1048576 | tf_op jit(solution)/shard_map/all_to_all | solution.py:45
  34.9 7.9 %collective-permute-start = (bf16[128,128]{1,0:T(8,128)(2,1)S(1)}, bf16[128,128]{1,0:T(8,128)(2,1)S(1)}, u32[]{:S(2)}, u32[]{:S(2)}) collective-permute-start(bf16[128,128]{1,0:T(8,128)(2,1)S(1)} %slice.92), channel_id=1, source_target_pairs={{0,1},{1,2},{2,3},{3,4},{4,5},{5,6},{6,7},{7,8},{8,9},{9,10},{10,1... | collective-permute-start | bytes 98312 | tf_op jit(solution)/shard_map/ppermute | solution.py:88
  55.5 2.2 %copy-start = (bf16[4096,512]{1,0:T(8,128)(2,1)S(1)}, bf16[4096,512]{1,0:T(8,128)(2,1)}, u32[]{:S(2)}) copy-start(bf16[4096,512]{1,0:T(8,128)(2,1)} %param.9) | copy-start | bytes 12582916
  61.8 26.4 %copy-start.2 = (f32[16,512]{1,0:T(8,128)S(1)}, f32[16,512]{1,0:T(8,128)}, u32[]{:S(2)}) copy-start(f32[16,512]{1,0:T(8,128)} %param.14) | copy-start | bytes 98308
  66.4 37.9 %copy-start.3 = (f32[64,128]{1,0:T(8,128)S(1)}, f32[64,128]{1,0:T(8,128)}, u32[]{:S(2)}) copy-start(f32[64,128]{1,0:T(8,128)} %param.11) | copy-start | bytes 98308
  66.4 37.9 %copy-start.4 = (f32[64,128]{1,0:T(8,128)S(1)}, f32[64,128]{1,0:T(8,128)}, u32[]{:S(2)}) copy-start(f32[64,128]{1,0:T(8,128)} %param.12) | copy-start | bytes 98308
  66.4 37.9 %copy-start.5 = (f32[64,128]{1,0:T(8,128)S(1)}, f32[64,128]{1,0:T(8,128)}, u32[]{:S(2)}) copy-start(f32[64,128]{1,0:T(8,128)} %param.13) | copy-start | bytes 98308
  66.4 13.9 %all-to-all-start.5 = ((bf16[8,16,512]{2,1,0:T(8,128)(2,1)}), bf16[8,16,512]{2,1,0:T(8,128)(2,1)S(1)}, u32[]{:S(2)}, u32[]{:S(2)}) async-start(bf16[8,16,512]{2,1,0:T(8,128)(2,1)} %bitcast.6), calls=%async_computation.5 | async-start | bytes 262144 | tf_op jit(solution)/shard_map/all_to_all | solution.py:84
  80.3 23.9 %all-to-all-start.4 = ((bf16[32,64,128]{2,1,0:T(8,128)(2,1)}), bf16[32,64,128]{2,1,0:T(8,128)(2,1)S(1)}, u32[]{:S(2)}, u32[]{:S(2)}) async-start(bf16[32,64,128]{2,1,0:T(8,128)(2,1)} %reduce_sum.30), calls=%async_computation.4 | async-start | bytes 1048576 | tf_op jit(solution)/shard_map/all_to_all | solution.py:75

commit v4 on v3

--- a/solution.py
+++ b/solution.py
@@ -57,8 +57,12 @@
 
     fb = factors.astype(jnp.bfloat16)
     f_rows = gather_by_a2a(fb, ROW, n_row)
-    f_all = gather_by_a2a(f_rows, "core", CORES)
-    f_block = jnp.swapaxes(f_all, 0, 1).reshape(n_tm * own_rows, K)
+    core = lax.axis_index("core")
+    f_other = lax.ppermute(f_rows, "core", [(0, 1), (1, 0)])
+    low = core == 0
+    f_block = jnp.stack(
+        [jnp.where(low, f_rows, f_other), jnp.where(low, f_other, f_rows)], axis=1
+    ).reshape(n_tm * own_rows, K)
 
     x_parts = gather_by_a2a(basis.astype(jnp.bfloat16), "series", n_series)
     x_full = x_parts.reshape(n_series * rank_part, width)
@@ -70,8 +74,9 @@
     contract_time = (((1,), (1,)), ((), ()))
     partial_f = -lax.dot_general(rb, x_full, contract_time, preferred_element_type=jnp.float32) * scale_f
     by_core = partial_f.reshape(n_row, CORES, own_rows, K)
-    by_core = lax.all_to_all(by_core.astype(jnp.bfloat16), "core", 1, 1, tiled=True)
-    by_core = by_core.astype(jnp.float32).sum(1)
+    kept = lax.dynamic_index_in_dim(by_core, core, 1, keepdims=False)
+    given = lax.dynamic_index_in_dim(by_core, 1 - core, 1, keepdims=False)
+    by_core = kept + lax.ppermute(given.astype(jnp.bfloat16), "core", [(0, 1), (1, 0)]).astype(jnp.float32)
     by_row = lax.all_to_all(by_core.astype(jnp.bfloat16), ROW, 0, 0, tiled=True)
     grad_f = by_row.astype(jnp.float32).sum(0)
     factors_new, m_new, v_new = adam_update(factors, adam_m, adam_v, grad_f)

time: 106 us -> 106 us (level)
  blocking collectives: 9.15 us -> 0 us
  matrix products: 7.45 us -> 11.9 us
  starting transfers between devices: 33.2 us -> 37.3 us
    all_to_all x2 -> x0, blocking collectives: 9.15 us -> none  [the longest x1 4.58 us: on_device(): lax.all_to_all(by_core.astype(jnp.bfloat16), 'core', 1, 1, tiled=True)]
    ppermute x0 -> x2, starting transfers between devices: none -> 4.31 us  [the longest x1 2.4 us: on_device(): lax.ppermute(given.astype(jnp.bfloat16), 'core', [(0, 1), (1, 0)])]
    dot_general x4, matrix products: 1.9 us -> 4.17 us  [conv_layer(): z_val = jnp.dot(weights[0], past, preferred_element_type=jnp.float32)]
    all_to_all x1, waiting for transfers between devices: 15.4 us -> 13.1 us  [on_device(): by_row = lax.all_to_all(by_core.astype(jnp.bfloat16), ROW, 0, 0, tiled=True)]
    dot_general x4, matrix products: 1.61 us -> 3.88 us  [conv_layer(): z_val = z_val + jnp.dot(weights[1], hb, preferred_element_type=jnp.float32)]
    all_to_all x2, waiting for transfers between devices: 13.4 us -> 14.9 us  [gather_by_a2a(): return lax.all_to_all(copies, axis, 0, 0, tiled=True)]
    reduce_sum x1 -> x0, other arithmetic: 1.15 us -> none  [on_device(): by_core = by_core.astype(jnp.float32).sum(1)]
  transfers between devices with their start and end apart: 5 -> 7, of which waited for: 4 -> 4; matrix products, arithmetic and copies ran while one was open for 9% -> 14% of each run, Pallas kernels for 0% -> 0%
where the time goes in v4:
time: 106 us; the launch traced here: 105 us
  waiting for transfers between devices  38 us (36%)
  starting transfers between devices  37.3 us (35%)
  matrix products  11.9 us (11%)
  local copies, waits for them, and re-layouts  7.01 us (7%)
  between operations  6.04 us (6%)
  other arithmetic  4.77 us (4%)
    all_to_all x2, starting transfers between devices, gather_by_a2a(): return lax.all_to_all(copies, axis, 0, 0, tiled=True)  20.7 us
    all_to_all x2, waiting for transfers between devices, gather_by_a2a(): return lax.all_to_all(copies, axis, 0, 0, tiled=True)  14.9 us
    all_to_all x1, waiting for transfers between devices, on_device(): by_row = lax.all_to_all(by_core.astype(jnp.bfloat16), ROW, 0, 0, tiled=True)  13.1 us
    all_to_all x1, waiting for transfers between devices, on_device(): lax.all_to_all(pieces.astype(jnp.bfloat16), 'series', 0, 0, tiled=True)  9.99 us
    all_to_all x1, starting transfers between devices, on_device(): by_row = lax.all_to_all(by_core.astype(jnp.bfloat16), ROW, 0, 0, tiled=True)  6.81 us
    dot_general x4, matrix products, conv_layer(): z_val = jnp.dot(weights[0], past, preferred_element_type=jnp.float32)  4.17 us
    dot_general x4, matrix products, conv_layer(): z_val = z_val + jnp.dot(weights[1], hb, preferred_element_type=jnp.float32)  3.88 us
    all_to_all x1, starting transfers between devices, on_device(): lax.all_to_all(pieces.astype(jnp.bfloat16), 'series', 0, 0, tiled=True)  3.51 us
  transfers between devices with their start and end apart: 7, of which 4 were waited for; matrix products, arithmetic and copies ran while one was open for 14% of the time, Pallas kernels for 0%

profile of v4, /device:TPU:8, one launch (start us, length us, event | category | flops | bytes accessed | tf_op | source)
XLA Modules:
  0.0 105.0 jit_solution(2192190244004047564)
XLA Ops:
  2.1 8.7 %all-to-all-start.1 = ((bf16[8,16,512]{2,1,0:T(8,128)(2,1)}), bf16[8,16,512]{2,1,0:T(8,128)(2,1)S(1)}, u32[]{:S(2)}, u32[]{:S(2)}) async-start(bf16[8,16,512]{2,1,0:T(8,128)(2,1)} %broadcast_in_dim.46), calls=%async_computation.1 | async-start | bytes 262144 | tf_op jit(solution)/shard_map/all_to_all | solution.py:45
  11.5 10.4 %all-to-all-done.1 = bf16[8,16,512]{2,1,0:T(8,128)(2,1)S(1)} async-done(((bf16[8,16,512]{2,1,0:T(8,128)(2,1)}), bf16[8,16,512]{2,1,0:T(8,128)(2,1)S(1)}, u32[]{:S(2)}, u32[]{:S(2)}) %all-to-all-start.1) | async-done | bytes 131104 | tf_op jit(solution)/shard_map/all_to_all | solution.py:45
  22.8 12.0 %all-to-all-start = ((bf16[32,64,128]{2,1,0:T(8,128)(2,1)}), bf16[32,64,128]{2,1,0:T(8,128)(2,1)S(1)}, u32[]{:S(2)}, u32[]{:S(2)}) async-start(bf16[32,64,128]{2,1,0:T(8,128)(2,1)} %broadcast_in_dim.45), calls=%async_computation | async-start | bytes 1048576 | tf_op jit(solution)/shard_map/all_to_all | solution.py:45
  34.8 1.4 %fusion.62 = (s32[1]{0:T(128)}, s32[1]{0:T(128)}, s32[1]{0:T(128)}, s32[1]{0:T(128)}) fusion(s32[4]{0:T(128)} %param.15), kind=kLoop, calls=%fused_computation.92 | loop fusion | bytes 32 | tf_op jit(solution)/shard_map/slice | solution.py:101
  37.1 1.9 %collective-permute-start.2 = (bf16[128,128]{1,0:T(8,128)(2,1)S(1)}, bf16[128,128]{1,0:T(8,128)(2,1)S(1)}, u32[]{:S(2)}, u32[]{:S(2)}) collective-permute-start(bf16[128,128]{1,0:T(8,128)(2,1)S(1)} %slice.92), channel_id=1, source_target_pairs={{0,1},{1,2},{2,3},{3,4},{4,5},{5,6},{6,7},{7,8},{8,9},{9,10},{10,1... | collective-permute-start | bytes 98312 | tf_op jit(solution)/shard_map/ppermute | solution.py:93
  45.0 1.0 fusion.22
  46.1 4.5 %all-to-all-done = bf16[32,64,128]{2,1,0:T(8,128)(2,1)S(1)} async-done(((bf16[32,64,128]{2,1,0:T(8,128)(2,1)}), bf16[32,64,128]{2,1,0:T(8,128)(2,1)S(1)}, u32[]{:S(2)}, u32[]{:S(2)}) %all-to-all-start) | async-done | bytes 524320 | tf_op jit(solution)/shard_map/all_to_all | solution.py:45
  50.5 1.9 %collective-permute-start = (bf16[32,64,128]{2,1,0:T(8,128)(2,1)S(1)}, bf16[32,64,128]{2,1,0:T(8,128)(2,1)S(1)}, u32[]{:S(2)}, u32[]{:S(2)}) collective-permute-start(bf16[32,64,128]{2,1,0:T(8,128)(2,1)S(1)} %all-to-all-done), channel_id=1, source_target_pairs={{0,1},{1,0},{2,3},{3,2},{4,5},{5,4},{6,7},{7,6},{8,9},{9,8},{10,11... | collective-permute-start | bytes 1572872 | tf_op jit(solution)/shard_map/ppermute | solution.py:61
  52.5 1.0 select_convert_fusion.2
  53.4 1.0 fusion.23
  54.5 1.0 select_convert_fusion.1
  55.7 1.1 %broadcast_in_dim.44 = f32[32,128,4,128]{3,2,1,0:T(4,128)S(1)} broadcast(f32[32,4]{1,0:T(8,128)S(1)} %copy.39), dimensions={0,2} | broadcast | bytes 8389120 | tf_op jit(solution)/shard_map/broadcast_in_dim | solution.py:23
  56.8 1.0 copy-done
  57.9 1.2 %fusion = bf16[4096,512]{1,0:T(8,128)(2,1)S(1)} fusion(f32[512,8,4,128]{3,2,1,0:T(4,128)S(1)} %bitcast.89, bf16[4096,512]{1,0:T(8,128)(2,1)S(1)} %copy-done, bf16[4096,128]{1,0:T(8,128)(2,1)S(1)} %bitcast.90, bf16[128,512]{1,0:T(8,128)(2,1)S(1)} %bitcast.97), kind=kOutput, calls=%fused_computation.1 | convolution fusion | flops 545259520 | bytes 17956864 | tf_op jit(solution)/shard_map/dot_general | solution.py:70
  59.1 1.2 %fusion.1 = f32[4096,128]{1,0:T(8,128)S(1)} fusion(bf16[4096,512]{1,0:T(8,128)(2,1)S(1)} %fusion, bf16[128,512]{1,0:T(8,128)(2,1)S(1)} %bitcast.98), kind=kOutput, calls=%fused_computation.3 | convolution fusion | flops 537919488 | bytes 6422528 | tf_op jit(solution)/shard_map/dot_general | solution.py:75
  61.2 2.4 %collective-permute-start.1 = (bf16[32,64,128]{2,1,0:T(8,128)(2,1)}, bf16[32,64,128]{2,1,0:T(8,128)(2,1)S(1)}, u32[]{:S(2)}, u32[]{:S(2)}) collective-permute-start(bf16[32,64,128]{2,1,0:T(8,128)(2,1)} %fusion.20), channel_id=1, source_target_pairs={{0,1},{1,0},{2,3},{3,2},{4,5},{5,4},{6,7},{7,6},{8,9},{9,8},{10,11... | collective-permute-start | bytes 1572872 | tf_op jit(solution)/shard_map/ppermute | solution.py:79
  63.6 1.0 fusion.24
  64.7 1.4 %fusion.18 = bf16[128,512]{1,0:T(8,128)(2,1)} fusion(bf16[4096,128]{1,0:T(8,128)(2,1)S(1)} %bitcast.91, bf16[4096,512]{1,0:T(8,128)(2,1)S(1)} %fusion), kind=kOutput, calls=%fused_computation.25 | convolution fusion | flops 537067520 | bytes 5373952 | tf_op jit(solution)/shard_map/dot_general | solution.py:84
  66.1 3.5 %all-to-all-start.3 = ((bf16[8,16,512]{2,1,0:T(8,128)(2,1)}), bf16[8,16,512]{2,1,0:T(8,128)(2,1)S(1)}, u32[]{:S(2)}, u32[]{:S(2)}) async-start(bf16[8,16,512]{2,1,0:T(8,128)(2,1)} %bitcast.8), calls=%async_computation.3 | async-start | bytes 262144 | tf_op jit(solution)/shard_map/all_to_all | solution.py:89
  70.6 10.0 %all-to-all-done.3 = bf16[8,16,512]{2,1,0:T(8,128)(2,1)S(1)} async-done(((bf16[8,16,512]{2,1,0:T(8,128)(2,1)}), bf16[8,16,512]{2,1,0:T(8,128)(2,1)S(1)}, u32[]{:S(2)}, u32[]{:S(2)}) %all-to-all-start.3) | async-done | bytes 131104 | tf_op jit(solution)/shard_map/all_to_all | solution.py:89
  80.6 6.8 %all-to-all-start.2 = ((bf16[32,64,128]{2,1,0:T(8,128)(2,1)}), bf16[32,64,128]{2,1,0:T(8,128)(2,1)S(1)}, u32[]{:S(2)}, u32[]{:S(2)}) async-start(bf16[32,64,128]{2,1,0:T(8,128)(2,1)} %fusion.19), calls=%async_computation.2 | async-start | bytes 1048576 | tf_op jit(solution)/shard_map/all_to_all | solution.py:80
  87.4 1.0 select_convert_fusion
  88.4 1.0 fusion.25
  91.1 13.1 %all-to-all-done.2 = bf16[32,64,128]{2,1,0:T(8,128)(2,1)S(1)} async-done(((bf16[32,64,128]{2,1,0:T(8,128)(2,1)}), bf16[32,64,128]{2,1,0:T(8,128)(2,1)S(1)}, u32[]{:S(2)}, u32[]{:S(2)}) %all-to-all-start.2) | async-done | bytes 524320 | tf_op jit(solution)/shard_map/all_to_all | solution.py:80
  (33 shorter events, 9.2 us)
Async XLA Ops:
  2.1 19.8 %all-to-all-start.1 = ((bf16[8,16,512]{2,1,0:T(8,128)(2,1)}), bf16[8,16,512]{2,1,0:T(8,128)(2,1)S(1)}, u32[]{:S(2)}, u32[]{:S(2)}) async-start(bf16[8,16,512]{2,1,0:T(8,128)(2,1)} %broadcast_in_dim.46), calls=%async_computation.1 | async-start | bytes 262144 | tf_op jit(solution)/shard_map/all_to_all | solution.py:45
  22.8 27.8 %all-to-all-start = ((bf16[32,64,128]{2,1,0:T(8,128)(2,1)}), bf16[32,64,128]{2,1,0:T(8,128)(2,1)S(1)}, u32[]{:S(2)}, u32[]{:S(2)}) async-start(bf16[32,64,128]{2,1,0:T(8,128)(2,1)} %broadcast_in_dim.45), calls=%async_computation | async-start | bytes 1048576 | tf_op jit(solution)/shard_map/all_to_all | solution.py:45
  37.1 7.9 %collective-permute-start.2 = (bf16[128,128]{1,0:T(8,128)(2,1)S(1)}, bf16[128,128]{1,0:T(8,128)(2,1)S(1)}, u32[]{:S(2)}, u32[]{:S(2)}) collective-permute-start(bf16[128,128]{1,0:T(8,128)(2,1)S(1)} %slice.92), channel_id=1, source_target_pairs={{0,1},{1,2},{2,3},{3,4},{4,5},{5,6},{6,7},{7,8},{8,9},{9,10},{10,1... | collective-permute-start | bytes 98312 | tf_op jit(solution)/shard_map/ppermute | solution.py:93
  50.5 4.9 %collective-permute-start = (bf16[32,64,128]{2,1,0:T(8,128)(2,1)S(1)}, bf16[32,64,128]{2,1,0:T(8,128)(2,1)S(1)}, u32[]{:S(2)}, u32[]{:S(2)}) collective-permute-start(bf16[32,64,128]{2,1,0:T(8,128)(2,1)S(1)} %all-to-all-done), channel_id=1, source_target_pairs={{0,1},{1,0},{2,3},{3,2},{4,5},{5,4},{6,7},{7,6},{8,9},{9,8},{10,11... | collective-permute-start | bytes 1572872 | tf_op jit(solution)/shard_map/ppermute | solution.py:61
  55.7 2.2 %copy-start = (bf16[4096,512]{1,0:T(8,128)(2,1)S(1)}, bf16[4096,512]{1,0:T(8,128)(2,1)}, u32[]{:S(2)}) copy-start(bf16[4096,512]{1,0:T(8,128)(2,1)} %param.9) | copy-start | bytes 12582916
  61.2 8.4 %collective-permute-start.1 = (bf16[32,64,128]{2,1,0:T(8,128)(2,1)}, bf16[32,64,128]{2,1,0:T(8,128)(2,1)S(1)}, u32[]{:S(2)}, u32[]{:S(2)}) collective-permute-start(bf16[32,64,128]{2,1,0:T(8,128)(2,1)} %fusion.20), channel_id=1, source_target_pairs={{0,1},{1,0},{2,3},{3,2},{4,5},{5,4},{6,7},{7,6},{8,9},{9,8},{10,11... | collective-permute-start | bytes 1572872 | tf_op jit(solution)/shard_map/ppermute | solution.py:79
  66.1 24.4 %copy-start.1 = (f32[16,512]{1,0:T(8,128)S(1)}, f32[16,512]{1,0:T(8,128)}, u32[]{:S(2)}) copy-start(f32[16,512]{1,0:T(8,128)} %param.14) | copy-start | bytes 98308
  66.1 38.2 %copy-start.2 = (f32[64,128]{1,0:T(8,128)S(1)}, f32[64,128]{1,0:T(8,128)}, u32[]{:S(2)}) copy-start(f32[64,128]{1,0:T(8,128)} %param.11) | copy-start | bytes 98308
  66.1 38.2 %copy-start.3 = (f32[64,128]{1,0:T(8,128)S(1)}, f32[64,128]{1,0:T(8,128)}, u32[]{:S(2)}) copy-start(f32[64,128]{1,0:T(8,128)} %param.12) | copy-start | bytes 98308
  66.1 38.2 %copy-start.4 = (f32[64,128]{1,0:T(8,128)S(1)}, f32[64,128]{1,0:T(8,128)}, u32[]{:S(2)}) copy-start(f32[64,128]{1,0:T(8,128)} %param.13) | copy-start | bytes 98308
  66.1 14.5 %all-to-all-start.3 = ((bf16[8,16,512]{2,1,0:T(8,128)(2,1)}), bf16[8,16,512]{2,1,0:T(8,128)(2,1)S(1)}, u32[]{:S(2)}, u32[]{:S(2)}) async-start(bf16[8,16,512]{2,1,0:T(8,128)(2,1)} %bitcast.8), calls=%async_computation.3 | async-start | bytes 262144 | tf_op jit(solution)/shard_map/all_to_all | solution.py:89
  80.6 23.7 %all-to-all-start.2 = ((bf16[32,64,128]{2,1,0:T(8,128)(2,1)}), bf16[32,64,128]{2,1,0:T(8,128)(2,1)S(1)}, u32[]{:S(2)}, u32[]{:S(2)}) async-start(bf16[32,64,128]{2,1,0:T(8,128)(2,1)} %fusion.19), calls=%async_computation.2 | async-start | bytes 1048576 | tf_op jit(solution)/shard_map/all_to_all | solution.py:80

commit v5 on v3

--- a/solution.py
+++ b/solution.py
@@ -64,7 +64,10 @@
     x_full = x_parts.reshape(n_series * rank_part, width)
 
     pred = jnp.dot(f_block, x_full, preferred_element_type=jnp.float32)
-    resid = expand(tile_mask, TILE) * (y_obs.astype(jnp.float32) - pred)
+    tiles = tile_mask.shape[0]
+    mask_cols = jnp.repeat(tile_mask.astype(jnp.float32), TILE, axis=1)
+    gap = (y_obs.astype(jnp.float32) - pred).reshape(tiles, TILE, width)
+    resid = (mask_cols[:, None, :] * gap).reshape(tiles * TILE, width)
     rb = resid.astype(jnp.bfloat16)
     scale_f = 1.0 / math.sqrt(total_time)
     contract_time = (((1,), (1,)), ((), ()))

time: 106 us -> 104 us (0.981)
  local copies, waits for them, and re-layouts: 6.56 us -> 4.48 us
where the time goes in v5:
time: 104 us; the launch traced here: 103 us
  waiting for transfers between devices  37.6 us (36%)
  starting transfers between devices  33.2 us (32%)
  blocking collectives  9.41 us (9%)
  matrix products  7.44 us (7%)
  between operations  6.08 us (6%)
  other arithmetic  4.84 us (5%)
  local copies, waits for them, and re-layouts  4.48 us (4%)
    all_to_all x2, starting transfers between devices, gather_by_a2a(): return lax.all_to_all(copies, axis, 0, 0, tiled=True)  20.7 us
    all_to_all x1, waiting for transfers between devices, on_device(): by_row = lax.all_to_all(by_core.astype(jnp.bfloat16), ROW, 0, 0, tiled=True)  15.4 us
    all_to_all x2, waiting for transfers between devices, gather_by_a2a(): return lax.all_to_all(copies, axis, 0, 0, tiled=True)  13.2 us
    all_to_all x1, waiting for transfers between devices, on_device(): lax.all_to_all(pieces.astype(jnp.bfloat16), 'series', 0, 0, tiled=True)  8.99 us
    all_to_all x1, starting transfers between devices, on_device(): by_row = lax.all_to_all(by_core.astype(jnp.bfloat16), ROW, 0, 0, tiled=True)  7.03 us
    all_to_all x1, blocking collectives, gather_by_a2a(): return lax.all_to_all(copies, axis, 0, 0, tiled=True)  4.84 us
    all_to_all x1, blocking collectives, on_device(): lax.all_to_all(by_core.astype(jnp.bfloat16), 'core', 1, 1, tiled=True)  4.58 us
    all_to_all x1, starting transfers between devices, on_device(): lax.all_to_all(pieces.astype(jnp.bfloat16), 'series', 0, 0, tiled=True)  3.5 us
  transfers between devices with their start and end apart: 5, of which 4 were waited for; matrix products, arithmetic and copies ran while one was open for 9% of the time, Pallas kernels for 0%

profile of v5, /device:TPU:8, one launch (start us, length us, event | category | flops | bytes accessed | tf_op | source)
XLA Modules:
  0.0 103.0 jit_solution(12320721505225844366)
XLA Ops:
  0.6 0.8 convert_element_type.56
  1.4 0.7 broadcast_in_dim.50
  2.1 8.7 %all-to-all-start.2 = ((bf16[8,16,512]{2,1,0:T(8,128)(2,1)}), bf16[8,16,512]{2,1,0:T(8,128)(2,1)S(1)}, u32[]{:S(2)}, u32[]{:S(2)}) async-start(bf16[8,16,512]{2,1,0:T(8,128)(2,1)} %broadcast_in_dim.50), calls=%async_computation.2 | async-start | bytes 262144 | tf_op jit(solution)/shard_map/all_to_all | solution.py:45
  10.8 1.4 %fusion.61 = (s32[1]{0:T(128)}, s32[1]{0:T(128)}, s32[1]{0:T(128)}, s32[1]{0:T(128)}) fusion(s32[4]{0:T(128)} %param.15), kind=kLoop, calls=%fused_computation.87 | loop fusion | bytes 32 | tf_op jit(solution)/shard_map/slice | solution.py:99
  12.2 0.8 convert_element_type.55
  12.9 0.8 slice_bitcast_fusion
  13.8 8.1 %all-to-all-done.2 = bf16[8,16,512]{2,1,0:T(8,128)(2,1)S(1)} async-done(((bf16[8,16,512]{2,1,0:T(8,128)(2,1)}), bf16[8,16,512]{2,1,0:T(8,128)(2,1)S(1)}, u32[]{:S(2)}, u32[]{:S(2)}) %all-to-all-start.2) | async-done | bytes 131104 | tf_op jit(solution)/shard_map/all_to_all | solution.py:45
  21.9 0.9 broadcast_in_dim.48
  22.8 12.0 %all-to-all-start = ((bf16[32,64,128]{2,1,0:T(8,128)(2,1)}), bf16[32,64,128]{2,1,0:T(8,128)(2,1)S(1)}, u32[]{:S(2)}, u32[]{:S(2)}) async-start(bf16[32,64,128]{2,1,0:T(8,128)(2,1)} %broadcast_in_dim.48), calls=%async_computation | async-start | bytes 1048576 | tf_op jit(solution)/shard_map/all_to_all | solution.py:45
  34.9 1.9 %collective-permute-start = (bf16[128,128]{1,0:T(8,128)(2,1)S(1)}, bf16[128,128]{1,0:T(8,128)(2,1)S(1)}, u32[]{:S(2)}, u32[]{:S(2)}) collective-permute-start(bf16[128,128]{1,0:T(8,128)(2,1)S(1)} %slice.92), channel_id=1, source_target_pairs={{0,1},{1,2},{2,3},{3,4},{4,5},{5,6},{6,7},{7,8},{8,9},{9,10},{10,1... | collective-permute-start | bytes 98312 | tf_op jit(solution)/shard_map/ppermute | solution.py:91
  42.0 0.7 convert_element_type.53
  43.0 1.0 %fusion.21 = f32[640,128]{0,1:T(8,128)S(1)} fusion(s32[]{:T(128)S(6)} %select_n.29, bf16[128,640]{1,0:T(8,128)(2,1)S(1)} %fusion.20, bf16[4,2,128,128]{3,2,1,0:T(8,128)(2,1)} %param.16), kind=kOutput, calls=%fused_computation.38 | convolution fusion | flops 20971520 | bytes 524292 | tf_op jit(solution)/shard_map/dot_general | solution.py:37
  44.0 1.0 select_convert_fusion.2
  45.5 5.1 %all-to-all-done = bf16[32,64,128]{2,1,0:T(8,128)(2,1)S(1)} async-done(((bf16[32,64,128]{2,1,0:T(8,128)(2,1)}), bf16[32,64,128]{2,1,0:T(8,128)(2,1)S(1)}, u32[]{:S(2)}, u32[]{:S(2)}) %all-to-all-start) | async-done | bytes 524320 | tf_op jit(solution)/shard_map/all_to_all | solution.py:45
  50.9 4.8 %all_to_all.30 = bf16[2,32,64,128]{3,2,1,0:T(8,128)(2,1)S(1)} all-to-all(bf16[2,32,64,128]{3,2,1,0:T(8,128)(2,1)S(1)} %broadcast_in_dim.49), channel_id=1, replica_groups=mesh['series'=8,'z'=8,'ylo'=4,'core'=2] {'core'}, dimensions={0} | all-to-all | bytes 2097152 | tf_op jit(solution)/shard_map/all_to_all | solution.py:45
  55.8 1.2 %fusion = bf16[4096,512]{1,0:T(8,128)(2,1)S(1)} fusion(bf16[4096,512]{1,0:T(8,128)(2,1)S(1)} %copy-done, bf16[4096,128]{1,0:T(8,128)(2,1)S(1)} %bitcast.83, bf16[128,512]{1,0:T(8,128)(2,1)S(1)} %bitcast.88, f32[32,512]{1,0:T(8,128)S(1)} %bitcast.91), kind=kOutput, calls=%fused_computation.1 | convolution fusion | flops 545259520 | bytes 9633792 | tf_op jit(solution)/shard_map/dot_general | solution.py:66
  57.0 1.5 %fusion.19 = bf16[512,128]{0,1:T(8,128)(2,1)} fusion(bf16[4096,512]{1,0:T(8,128)(2,1)S(1)} %fusion, bf16[4096,128]{1,0:T(8,128)(2,1)S(1)} %bitcast.84), kind=kOutput, calls=%fused_computation.26 | convolution fusion | flops 537067520 | bytes 5373952 | tf_op jit(solution)/shard_map/dot_general | solution.py:82
  58.5 1.2 %fusion.2 = bf16[4096,128]{1,0:T(8,128)(2,1)S(1)} fusion(bf16[4096,512]{1,0:T(8,128)(2,1)S(1)} %fusion, bf16[128,512]{1,0:T(8,128)(2,1)S(1)} %bitcast.89), kind=kOutput, calls=%fused_computation.4 | convolution fusion | flops 538443776 | bytes 5373952 | tf_op jit(solution)/shard_map/dot_general | solution.py:74
  59.9 4.6 %all_to_all.31 = bf16[32,2,64,128]{3,2,0,1:T(8,128)(2,1)S(1)} all-to-all(bf16[32,2,64,128]{3,2,0,1:T(8,128)(2,1)S(1)} %copy.52), channel_id=1, replica_groups=mesh['series'=8,'z'=8,'ylo'=4,'core'=2] {'core'}, dimensions={1} | all-to-all | bytes 2097152 | tf_op jit(solution)/shard_map/all_to_all | solution.py:76
  64.4 3.5 %all-to-all-start.5 = ((bf16[8,16,512]{2,1,0:T(8,128)(2,1)}), bf16[8,16,512]{2,1,0:T(8,128)(2,1)S(1)}, u32[]{:S(2)}, u32[]{:S(2)}) async-start(bf16[8,16,512]{2,1,0:T(8,128)(2,1)} %bitcast.7), calls=%async_computation.5 | async-start | bytes 262144 | tf_op jit(solution)/shard_map/all_to_all | solution.py:87
  68.2 1.1 %reduce_sum.30 = bf16[32,64,128]{2,1,0:T(8,128)(2,1)} reduce(bf16[32,2,64,128]{3,2,0,1:T(8,128)(2,1)S(1)} %all_to_all.31, bf16[]{:T(256)} %constant.56.clone.1), dimensions={1}, to_apply=%region_0.0 | reduce | flops 262144 | bytes 1572866 | tf_op jit(solution)/shard_map/reduce_sum | solution.py:77
  69.4 9.0 %all-to-all-done.5 = bf16[8,16,512]{2,1,0:T(8,128)(2,1)S(1)} async-done(((bf16[8,16,512]{2,1,0:T(8,128)(2,1)}), bf16[8,16,512]{2,1,0:T(8,128)(2,1)S(1)}, u32[]{:S(2)}, u32[]{:S(2)}) %all-to-all-start.5) | async-done | bytes 131104 | tf_op jit(solution)/shard_map/all_to_all | solution.py:87
  78.4 7.0 %all-to-all-start.4 = ((bf16[32,64,128]{2,1,0:T(8,128)(2,1)}), bf16[32,64,128]{2,1,0:T(8,128)(2,1)S(1)}, u32[]{:S(2)}, u32[]{:S(2)}) async-start(bf16[32,64,128]{2,1,0:T(8,128)(2,1)} %reduce_sum.30), calls=%async_computation.4 | async-start | bytes 1048576 | tf_op jit(solution)/shard_map/all_to_all | solution.py:78
  86.8 15.4 %all-to-all-done.4 = bf16[32,64,128]{2,1,0:T(8,128)(2,1)S(1)} async-done(((bf16[32,64,128]{2,1,0:T(8,128)(2,1)}), bf16[32,64,128]{2,1,0:T(8,128)(2,1)S(1)}, u32[]{:S(2)}, u32[]{:S(2)}) %all-to-all-start.4) | async-done | bytes 524320 | tf_op jit(solution)/shard_map/all_to_all | solution.py:78
  (34 shorter events, 3.6 us)
Async XLA Ops:
  0.6 44.4 %copy-start.1 = (bf16[4,2,128,128]{3,2,1,0:T(8,128)(2,1)S(1)}, bf16[4,2,128,128]{3,2,1,0:T(8,128)(2,1)}, u32[]{:S(2)}) copy-start(bf16[4,2,128,128]{3,2,1,0:T(8,128)(2,1)} %param.16) | copy-start | bytes 786436
  2.1 19.8 %all-to-all-start.2 = ((bf16[8,16,512]{2,1,0:T(8,128)(2,1)}), bf16[8,16,512]{2,1,0:T(8,128)(2,1)S(1)}, u32[]{:S(2)}, u32[]{:S(2)}) async-start(bf16[8,16,512]{2,1,0:T(8,128)(2,1)} %broadcast_in_dim.50), calls=%async_computation.2 | async-start | bytes 262144 | tf_op jit(solution)/shard_map/all_to_all | solution.py:45
  22.8 27.8 %all-to-all-start = ((bf16[32,64,128]{2,1,0:T(8,128)(2,1)}), bf16[32,64,128]{2,1,0:T(8,128)(2,1)S(1)}, u32[]{:S(2)}, u32[]{:S(2)}) async-start(bf16[32,64,128]{2,1,0:T(8,128)(2,1)} %broadcast_in_dim.48), calls=%async_computation | async-start | bytes 1048576 | tf_op jit(solution)/shard_map/all_to_all | solution.py:45
  34.9 8.0 %collective-permute-start = (bf16[128,128]{1,0:T(8,128)(2,1)S(1)}, bf16[128,128]{1,0:T(8,128)(2,1)S(1)}, u32[]{:S(2)}, u32[]{:S(2)}) collective-permute-start(bf16[128,128]{1,0:T(8,128)(2,1)S(1)} %slice.92), channel_id=1, source_target_pairs={{0,1},{1,2},{2,3},{3,4},{4,5},{5,6},{6,7},{7,8},{8,9},{9,10},{10,1... | collective-permute-start | bytes 98312 | tf_op jit(solution)/shard_map/ppermute | solution.py:91
  50.6 5.2 %copy-start = (bf16[4096,512]{1,0:T(8,128)(2,1)S(1)}, bf16[4096,512]{1,0:T(8,128)(2,1)}, u32[]{:S(2)}) copy-start(bf16[4096,512]{1,0:T(8,128)(2,1)} %param.9) | copy-start | bytes 12582916
  59.8 26.4 %copy-start.2 = (f32[16,512]{1,0:T(8,128)S(1)}, f32[16,512]{1,0:T(8,128)}, u32[]{:S(2)}) copy-start(f32[16,512]{1,0:T(8,128)} %param.14) | copy-start | bytes 98308
  64.4 37.9 %copy-start.3 = (f32[64,128]{1,0:T(8,128)S(1)}, f32[64,128]{1,0:T(8,128)}, u32[]{:S(2)}) copy-start(f32[64,128]{1,0:T(8,128)} %param.11) | copy-start | bytes 98308
  64.4 37.9 %copy-start.4 = (f32[64,128]{1,0:T(8,128)S(1)}, f32[64,128]{1,0:T(8,128)}, u32[]{:S(2)}) copy-start(f32[64,128]{1,0:T(8,128)} %param.12) | copy-start | bytes 98308
  64.4 37.9 %copy-start.5 = (f32[64,128]{1,0:T(8,128)S(1)}, f32[64,128]{1,0:T(8,128)}, u32[]{:S(2)}) copy-start(f32[64,128]{1,0:T(8,128)} %param.13) | copy-start | bytes 98308
  64.4 13.9 %all-to-all-start.5 = ((bf16[8,16,512]{2,1,0:T(8,128)(2,1)}), bf16[8,16,512]{2,1,0:T(8,128)(2,1)S(1)}, u32[]{:S(2)}, u32[]{:S(2)}) async-start(bf16[8,16,512]{2,1,0:T(8,128)(2,1)} %bitcast.7), calls=%async_computation.5 | async-start | bytes 262144 | tf_op jit(solution)/shard_map/all_to_all | solution.py:87
  78.4 23.9 %all-to-all-start.4 = ((bf16[32,64,128]{2,1,0:T(8,128)(2,1)}), bf16[32,64,128]{2,1,0:T(8,128)(2,1)S(1)}, u32[]{:S(2)}, u32[]{:S(2)}) async-start(bf16[32,64,128]{2,1,0:T(8,128)(2,1)} %reduce_sum.30), calls=%async_computation.4 | async-start | bytes 1048576 | tf_op jit(solution)/shard_map/all_to_all | solution.py:78

commit v6 on v3

--- a/solution.py
+++ b/solution.py
@@ -3,6 +3,8 @@
 import jax
 import jax.numpy as jnp
 from jax import lax
+from jax.experimental import pallas as pl
+from jax.experimental.pallas import tpu as pltpu
 from jax.sharding import Mesh
 from jax.sharding import PartitionSpec as P
 
@@ -45,6 +47,56 @@
     return lax.all_to_all(copies, axis, 0, 0, tiled=True)
 
 
+def residual_kernel(scale_f, y_ref, m_ref, f_ref, x_ref, pf_ref, px_ref):
+    step = pl.program_id(0)
+    rows, width = y_ref.shape
+    f = f_ref[...]
+    x = x_ref[...]
+    pred = jnp.dot(f, x, preferred_element_type=jnp.float32)
+    gap = (y_ref[...].astype(jnp.float32) - pred).reshape(rows // TILE, TILE, width)
+    rb = (m_ref[...][:, None, :] * gap).reshape(rows, width).astype(jnp.bfloat16)
+    contract_time = (((1,), (1,)), ((), ()))
+    pf_ref[...] = -lax.dot_general(rb, x, contract_time, preferred_element_type=jnp.float32) * scale_f
+    part = lax.dot_general(f, rb, (((0,), (0,)), ((), ())), preferred_element_type=jnp.float32)
+
+    @pl.when(step == 0)
+    def _():
+        px_ref[...] = part
+
+    @pl.when(step > 0)
+    def _():
+        px_ref[...] += part
+
+
+def residual_products(y_obs, mask_cols, f_block, x_full, scale_f):
+    n_rows, width = y_obs.shape
+    block = 8 * TILE
+    steps = n_rows // block
+    kernel = lambda *refs: residual_kernel(scale_f, *refs)
+    flops = 3 * 2 * n_rows * width * K
+    moved = n_rows * width * 2 + n_rows * K * 2 + n_rows * K * 4 + 2 * K * width * 4
+    return pl.pallas_call(
+        kernel,
+        grid=(steps,),
+        in_specs=[
+            pl.BlockSpec((block, width), lambda i: (i, 0)),
+            pl.BlockSpec((block // TILE, width), lambda i: (i, 0)),
+            pl.BlockSpec((block, K), lambda i: (i, 0)),
+            pl.BlockSpec((K, width), lambda i: (0, 0)),
+        ],
+        out_specs=[
+            pl.BlockSpec((block, K), lambda i: (i, 0)),
+            pl.BlockSpec((K, width), lambda i: (0, 0)),
+        ],
+        out_shape=[
+            jax.ShapeDtypeStruct((n_rows, K), jnp.float32),
+            jax.ShapeDtypeStruct((K, width), jnp.float32),
+        ],
+        compiler_params=pltpu.CompilerParams(dimension_semantics=("arbitrary",)),
+        cost_estimate=pl.CostEstimate(flops=flops, bytes_accessed=moved, transcendentals=0),
+    )(y_obs, mask_cols, f_block, x_full)
+
+
 def on_device(y_obs, tile_mask, factors, adam_m, adam_v, basis, dilations, conv_w, conv_b):
     own_rows = factors.shape[0]
     width = basis.shape[1]
@@ -63,12 +115,9 @@
     x_parts = gather_by_a2a(basis.astype(jnp.bfloat16), "series", n_series)
     x_full = x_parts.reshape(n_series * rank_part, width)
 
-    pred = jnp.dot(f_block, x_full, preferred_element_type=jnp.float32)
-    resid = expand(tile_mask, TILE) * (y_obs.astype(jnp.float32) - pred)
-    rb = resid.astype(jnp.bfloat16)
+    mask_cols = jnp.repeat(tile_mask.astype(jnp.float32), TILE, axis=1)
     scale_f = 1.0 / math.sqrt(total_time)
-    contract_time = (((1,), (1,)), ((), ()))
-    partial_f = -lax.dot_general(rb, x_full, contract_time, preferred_element_type=jnp.float32) * scale_f
+    partial_f, product_x = residual_products(y_obs, mask_cols, f_block, x_full, scale_f)
     by_core = partial_f.reshape(n_row, CORES, own_rows, K)
     by_core = lax.all_to_all(by_core.astype(jnp.bfloat16), "core", 1, 1, tiled=True)
     by_core = by_core.astype(jnp.float32).sum(1)
@@ -76,10 +125,7 @@
     grad_f = by_row.astype(jnp.float32).sum(0)
     factors_new, m_new, v_new = adam_update(factors, adam_m, adam_v, grad_f)
 
-    partial_x = -lax.dot_general(
-        f_block, rb, (((0,), (0,)), ((), ())), preferred_element_type=jnp.float32
-    )
-    partial_x = partial_x * math.sqrt(K / total_series)
+    partial_x = -product_x * math.sqrt(K / total_series)
     pieces = partial_x.reshape(n_series, rank_part, width)
     arrived = lax.all_to_all(pieces.astype(jnp.bfloat16), "series", 0, 0, tiled=True)
     grad_x = arrived.astype(jnp.float32).sum(0)

time: 106 us -> 111 us (1.047)
  Pallas kernels: 0 us -> 6.45 us
  blocking collectives: 9.15 us -> 4.58 us
  matrix products: 7.45 us -> 3.5 us
  starting transfers between devices: 33.2 us -> 36.6 us
  other arithmetic: 4.84 us -> 7.24 us
    pallas_call x0 -> x1, Pallas kernels: none -> 6.45 us  [residual_products(): pl.pallas_call(kernel, grid=(steps,), in_specs=[pl.BlockSpec((block, widt...]
    all_to_all x1 -> x0, blocking collectives: 4.58 us -> none  [on_device(): lax.all_to_all(by_core.astype(jnp.bfloat16), 'core', 1, 1, tiled=True)]
    dot_general x3 -> x0, matrix products: 3.94 us -> none  [the longest x1 1.46 us: on_device(): lax.dot_general(f_block, rb, (((0,), (0,)), ((), ())), preferred_element_...]
    all_to_all x0 -> x1, starting transfers between devices: none -> 3.58 us  [on_device(): lax.all_to_all(by_core.astype(jnp.bfloat16), 'core', 1, 1, tiled=True)]
    convert_element_type x1 -> x3, other arithmetic: 0.69 us -> 3.1 us  [the longest x1 1.74 us: on_device(): by_core.astype(jnp.bfloat16)]
    all_to_all x0 -> x1, waiting for transfers between devices: none -> 1.37 us  [on_device(): lax.all_to_all(by_core.astype(jnp.bfloat16), 'core', 1, 1, tiled=True)]
  transfers between devices with their start and end apart: 5 -> 6, of which waited for: 4 -> 5; matrix products, arithmetic and copies ran while one was open for 9% -> 10% of each run, Pallas kernels for 0% -> 0%
where the time goes in v6:
time: 111 us; the launch traced here: 110 us
  waiting for transfers between devices  38.4 us (35%)
  starting transfers between devices  36.6 us (33%)
  other arithmetic  7.24 us (7%)
  local copies, waits for them, and re-layouts  7.07 us (6%)
  Pallas kernels  6.45 us (6%)
  between operations  6.04 us (5%)
  blocking collectives  4.58 us (4%)
  matrix products  3.5 us (3%)
    all_to_all x2, starting transfers between devices, gather_by_a2a(): return lax.all_to_all(copies, axis, 0, 0, tiled=True)  20.7 us
    all_to_all x1, waiting for transfers between devices, on_device(): by_row = lax.all_to_all(by_core.astype(jnp.bfloat16), ROW, 0, 0, tiled=True)  15.4 us
    all_to_all x2, waiting for transfers between devices, gather_by_a2a(): return lax.all_to_all(copies, axis, 0, 0, tiled=True)  12.6 us
    all_to_all x1, waiting for transfers between devices, on_device(): lax.all_to_all(pieces.astype(jnp.bfloat16), 'series', 0, 0, tiled=True)  9 us
    all_to_all x1, starting transfers between devices, on_device(): by_row = lax.all_to_all(by_core.astype(jnp.bfloat16), ROW, 0, 0, tiled=True)  7.04 us
    pallas_call x1, Pallas kernels, residual_products(): pl.pallas_call(kernel, grid=(steps,), in_specs=[pl.BlockSpec((block, widt...  6.45 us
    all_to_all x1, blocking collectives, gather_by_a2a(): return lax.all_to_all(copies, axis, 0, 0, tiled=True)  4.58 us
    all_to_all x1, starting transfers between devices, on_device(): lax.all_to_all(by_core.astype(jnp.bfloat16), 'core', 1, 1, tiled=True)  3.58 us
  transfers between devices with their start and end apart: 6, of which 5 were waited for; matrix products, arithmetic and copies ran while one was open for 10% of the time, Pallas kernels for 0%

profile of v6, /device:TPU:8, one launch (start us, length us, event | category | flops | bytes accessed | tf_op | source)
XLA Modules:
  0.0 109.9 jit_solution(14335401748051953001)
XLA Ops:
  0.6 0.8 convert_element_type.46
  2.1 8.7 %all-to-all-start.2 = ((bf16[8,16,512]{2,1,0:T(8,128)(2,1)}), bf16[8,16,512]{2,1,0:T(8,128)(2,1)S(1)}, u32[]{:S(2)}, u32[]{:S(2)}) async-start(bf16[8,16,512]{2,1,0:T(8,128)(2,1)} %broadcast_in_dim.50), calls=%async_computation.2 | async-start | bytes 262144 | tf_op jit(solution)/shard_map/all_to_all | solution.py:47
  10.8 1.4 %fusion.56 = (s32[1]{0:T(128)}, s32[1]{0:T(128)}, s32[1]{0:T(128)}, s32[1]{0:T(128)}) fusion(s32[4]{0:T(128)} %param.15), kind=kLoop, calls=%fused_computation.80 | loop fusion | bytes 32 | tf_op jit(solution)/shard_map/slice | solution.py:142
  12.2 0.8 convert_element_type.45
  12.9 0.8 slice_bitcast_fusion
  13.8 8.1 %all-to-all-done.2 = bf16[8,16,512]{2,1,0:T(8,128)(2,1)S(1)} async-done(((bf16[8,16,512]{2,1,0:T(8,128)(2,1)}), bf16[8,16,512]{2,1,0:T(8,128)(2,1)S(1)}, u32[]{:S(2)}, u32[]{:S(2)}) %all-to-all-start.2) | async-done | bytes 131104 | tf_op jit(solution)/shard_map/all_to_all | solution.py:47
  21.9 0.9 broadcast_in_dim.48
  22.8 12.0 %all-to-all-start = ((bf16[32,64,128]{2,1,0:T(8,128)(2,1)}), bf16[32,64,128]{2,1,0:T(8,128)(2,1)S(1)}, u32[]{:S(2)}, u32[]{:S(2)}) async-start(bf16[32,64,128]{2,1,0:T(8,128)(2,1)} %broadcast_in_dim.48), calls=%async_computation | async-start | bytes 1048576 | tf_op jit(solution)/shard_map/all_to_all | solution.py:47
  34.9 1.9 %collective-permute-start = (bf16[128,128]{1,0:T(8,128)(2,1)S(1)}, bf16[128,128]{1,0:T(8,128)(2,1)S(1)}, u32[]{:S(2)}, u32[]{:S(2)}) collective-permute-start(bf16[128,128]{1,0:T(8,128)(2,1)S(1)} %slice.92), channel_id=1, source_target_pairs={{0,1},{1,2},{2,3},{3,4},{4,5},{5,6},{6,7},{7,8},{8,9},{9,10},{10,1... | collective-permute-start | bytes 98312 | tf_op jit(solution)/shard_map/ppermute | solution.py:134
  43.5 1.0 fusion.16
  44.6 1.0 select_convert_fusion.2
  46.1 4.5 %all-to-all-done = bf16[32,64,128]{2,1,0:T(8,128)(2,1)S(1)} async-done(((bf16[32,64,128]{2,1,0:T(8,128)(2,1)}), bf16[32,64,128]{2,1,0:T(8,128)(2,1)S(1)}, u32[]{:S(2)}, u32[]{:S(2)}) %all-to-all-start) | async-done | bytes 524320 | tf_op jit(solution)/shard_map/all_to_all | solution.py:47
  50.9 4.6 %all_to_all.30 = bf16[2,32,64,128]{3,2,1,0:T(8,128)(2,1)S(1)} all-to-all(bf16[2,32,64,128]{3,2,1,0:T(8,128)(2,1)S(1)} %broadcast_in_dim.49), channel_id=1, replica_groups=mesh['series'=8,'z'=8,'ylo'=4,'core'=2] {'core'}, dimensions={0} | all-to-all | bytes 2097152 | tf_op jit(solution)/shard_map/all_to_all | solution.py:47
  55.4 1.1 copy.30
  56.5 6.4 %shard_map.120 = (f32[4096,128]{1,0:T(8,128)}, f32[128,512]{1,0:T(8,128)}) custom-call(bf16[4096,512]{1,0:T(8,128)(2,1)} %refs_0_.1, f32[32,512]{1,0:T(8,128)} %bitcast.78, bf16[4096,128]{1,0:T(8,128)(2,1)} %bitcast.76, bf16[128,512]{1,0:T(8,128)(2,1)} %bitcast.75), custom_call_target="tpu_custom_call" | custom-call | flops 1610612736 | bytes 7864320 | tf_op jit(solution)/shard_map/pallas_call | solution.py:78
  63.0 1.7 %convert_element_type.47 = bf16[4096,128]{1,0:T(8,128)(2,1)S(1)} convert(f32[4096,128]{1,0:T(8,128)} %get-tuple-element.6) | non-fusion elementwise | flops 524288 | bytes 3145728 | tf_op jit(solution)/shard_map/convert_element_type | solution.py:122
  64.7 1.1 copy.31
  65.7 3.6 %all-to-all-start.3 = ((bf16[32,2,64,128]{3,2,0,1:T(8,128)(2,1)}), bf16[32,2,64,128]{3,2,0,1:T(8,128)(2,1)S(1)}, u32[]{:S(2)}, u32[]{:S(2)}) async-start(bf16[32,2,64,128]{3,2,0,1:T(8,128)(2,1)} %copy.31), calls=%async_computation.3 | async-start | bytes 2097152 | tf_op jit(solution)/shard_map/all_to_all | solution.py:122
  70.1 1.4 %all-to-all-done.3 = bf16[32,2,64,128]{3,2,0,1:T(8,128)(2,1)S(1)} async-done(((bf16[32,2,64,128]{3,2,0,1:T(8,128)(2,1)}), bf16[32,2,64,128]{3,2,0,1:T(8,128)(2,1)S(1)}, u32[]{:S(2)}, u32[]{:S(2)}) %all-to-all-start.3) | async-done | bytes 1048608 | tf_op jit(solution)/shard_map/all_to_all | solution.py:122
  71.4 3.4 %all-to-all-start.5 = ((bf16[8,16,512]{2,1,0:T(8,128)(2,1)}), bf16[8,16,512]{2,1,0:T(8,128)(2,1)S(1)}, u32[]{:S(2)}, u32[]{:S(2)}) async-start(bf16[8,16,512]{2,1,0:T(8,128)(2,1)} %bitcast.4), calls=%async_computation.5 | async-start | bytes 262144 | tf_op jit(solution)/shard_map/all_to_all | solution.py:130
  75.1 1.1 %reduce_sum.30 = bf16[32,64,128]{2,1,0:T(8,128)(2,1)} reduce(bf16[32,2,64,128]{3,2,0,1:T(8,128)(2,1)S(1)} %all-to-all-done.3, bf16[]{:T(256)} %constant.54.clone.1), dimensions={1}, to_apply=%region_0.0 | reduce | flops 262144 | bytes 1572866 | tf_op jit(solution)/shard_map/reduce_sum | solution.py:123
  76.2 9.0 %all-to-all-done.5 = bf16[8,16,512]{2,1,0:T(8,128)(2,1)S(1)} async-done(((bf16[8,16,512]{2,1,0:T(8,128)(2,1)}), bf16[8,16,512]{2,1,0:T(8,128)(2,1)S(1)}, u32[]{:S(2)}, u32[]{:S(2)}) %all-to-all-start.5) | async-done | bytes 131104 | tf_op jit(solution)/shard_map/all_to_all | solution.py:130
  85.2 7.0 %all-to-all-start.4 = ((bf16[32,64,128]{2,1,0:T(8,128)(2,1)}), bf16[32,64,128]{2,1,0:T(8,128)(2,1)S(1)}, u32[]{:S(2)}, u32[]{:S(2)}) async-start(bf16[32,64,128]{2,1,0:T(8,128)(2,1)} %reduce_sum.30), calls=%async_computation.4 | async-start | bytes 1048576 | tf_op jit(solution)/shard_map/all_to_all | solution.py:124
  93.7 15.4 %all-to-all-done.4 = bf16[32,64,128]{2,1,0:T(8,128)(2,1)S(1)} async-done(((bf16[32,64,128]{2,1,0:T(8,128)(2,1)}), bf16[32,64,128]{2,1,0:T(8,128)(2,1)S(1)}, u32[]{:S(2)}, u32[]{:S(2)}) %all-to-all-start.4) | async-done | bytes 524320 | tf_op jit(solution)/shard_map/all_to_all | solution.py:124
  (37 shorter events, 6.1 us)
Async XLA Ops:
  0.6 45.0 %copy-start.1 = (bf16[4,2,128,128]{3,2,1,0:T(8,128)(2,1)S(1)}, bf16[4,2,128,128]{3,2,1,0:T(8,128)(2,1)}, u32[]{:S(2)}) copy-start(bf16[4,2,128,128]{3,2,1,0:T(8,128)(2,1)} %param.16) | copy-start | bytes 786436
  2.1 19.8 %all-to-all-start.2 = ((bf16[8,16,512]{2,1,0:T(8,128)(2,1)}), bf16[8,16,512]{2,1,0:T(8,128)(2,1)S(1)}, u32[]{:S(2)}, u32[]{:S(2)}) async-start(bf16[8,16,512]{2,1,0:T(8,128)(2,1)} %broadcast_in_dim.50), calls=%async_computation.2 | async-start | bytes 262144 | tf_op jit(solution)/shard_map/all_to_all | solution.py:47
  21.9 33.5 %copy-start = (bf16[8,16,512]{2,1,0:T(8,128)(2,1)}, bf16[8,16,512]{2,1,0:T(8,128)(2,1)S(1)}, u32[]{:S(2)}) copy-start(bf16[8,16,512]{2,1,0:T(8,128)(2,1)S(1)} %all-to-all-done.2) | copy-start | bytes 393220
  22.8 27.8 %all-to-all-start = ((bf16[32,64,128]{2,1,0:T(8,128)(2,1)}), bf16[32,64,128]{2,1,0:T(8,128)(2,1)S(1)}, u32[]{:S(2)}, u32[]{:S(2)}) async-start(bf16[32,64,128]{2,1,0:T(8,128)(2,1)} %broadcast_in_dim.48), calls=%async_computation | async-start | bytes 1048576 | tf_op jit(solution)/shard_map/all_to_all | solution.py:47
  34.9 8.6 %collective-permute-start = (bf16[128,128]{1,0:T(8,128)(2,1)S(1)}, bf16[128,128]{1,0:T(8,128)(2,1)S(1)}, u32[]{:S(2)}, u32[]{:S(2)}) collective-permute-start(bf16[128,128]{1,0:T(8,128)(2,1)S(1)} %slice.92), channel_id=1, source_target_pairs={{0,1},{1,2},{2,3},{3,4},{4,5},{5,6},{6,7},{7,8},{8,9},{9,10},{10,1... | collective-permute-start | bytes 98312 | tf_op jit(solution)/shard_map/ppermute | solution.py:134
  63.0 6.4 %copy-start.2 = (f32[128,512]{1,0:T(8,128)S(1)}, f32[128,512]{1,0:T(8,128)}, u32[]{:S(2)}) copy-start(f32[128,512]{1,0:T(8,128)} %get-tuple-element.7) | copy-start | bytes 786436
  65.7 5.7 %all-to-all-start.3 = ((bf16[32,2,64,128]{3,2,0,1:T(8,128)(2,1)}), bf16[32,2,64,128]{3,2,0,1:T(8,128)(2,1)S(1)}, u32[]{:S(2)}, u32[]{:S(2)}) async-start(bf16[32,2,64,128]{3,2,0,1:T(8,128)(2,1)} %copy.31), calls=%async_computation.3 | async-start | bytes 2097152 | tf_op jit(solution)/shard_map/all_to_all | solution.py:122
  69.3 23.8 %copy-start.3 = (f32[16,512]{1,0:T(8,128)S(1)}, f32[16,512]{1,0:T(8,128)}, u32[]{:S(2)}) copy-start(f32[16,512]{1,0:T(8,128)} %param.14) | copy-start | bytes 98308
  69.3 39.9 %copy-start.4 = (f32[64,128]{1,0:T(8,128)S(1)}, f32[64,128]{1,0:T(8,128)}, u32[]{:S(2)}) copy-start(f32[64,128]{1,0:T(8,128)} %param.11) | copy-start | bytes 98308
  69.4 39.9 %copy-start.5 = (f32[64,128]{1,0:T(8,128)S(1)}, f32[64,128]{1,0:T(8,128)}, u32[]{:S(2)}) copy-start(f32[64,128]{1,0:T(8,128)} %param.12) | copy-start | bytes 98308
  69.4 39.9 %copy-start.6 = (f32[64,128]{1,0:T(8,128)S(1)}, f32[64,128]{1,0:T(8,128)}, u32[]{:S(2)}) copy-start(f32[64,128]{1,0:T(8,128)} %param.13) | copy-start | bytes 98308
  71.4 13.8 %all-to-all-start.5 = ((bf16[8,16,512]{2,1,0:T(8,128)(2,1)}), bf16[8,16,512]{2,1,0:T(8,128)(2,1)S(1)}, u32[]{:S(2)}, u32[]{:S(2)}) async-start(bf16[8,16,512]{2,1,0:T(8,128)(2,1)} %bitcast.4), calls=%async_computation.5 | async-start | bytes 262144 | tf_op jit(solution)/shard_map/all_to_all | solution.py:130
  85.2 23.9 %all-to-all-start.4 = ((bf16[32,64,128]{2,1,0:T(8,128)(2,1)}), bf16[32,64,128]{2,1,0:T(8,128)(2,1)S(1)}, u32[]{:S(2)}, u32[]{:S(2)}) async-start(bf16[32,64,128]{2,1,0:T(8,128)(2,1)} %reduce_sum.30), calls=%async_computation.4 | async-start | bytes 1048576 | tf_op jit(solution)/shard_map/all_to_all | solution.py:124

commit v7 on v5

--- a/solution.py
+++ b/solution.py
@@ -57,11 +57,12 @@
 
     fb = factors.astype(jnp.bfloat16)
     f_rows = gather_by_a2a(fb, ROW, n_row)
+    x_copies = jnp.broadcast_to(basis.astype(jnp.bfloat16)[None], (n_series,) + basis.shape)
+    f_rows, x_copies = lax.optimization_barrier((f_rows, x_copies))
+    x_parts = lax.all_to_all(x_copies, "series", 0, 0, tiled=True)
+    x_full = x_parts.reshape(n_series * rank_part, width)
     f_all = gather_by_a2a(f_rows, "core", CORES)
     f_block = jnp.swapaxes(f_all, 0, 1).reshape(n_tm * own_rows, K)
-
-    x_parts = gather_by_a2a(basis.astype(jnp.bfloat16), "series", n_series)
-    x_full = x_parts.reshape(n_series * rank_part, width)
 
     pred = jnp.dot(f_block, x_full, preferred_element_type=jnp.float32)
     tiles = tile_mask.shape[0]

time: 104 us -> 109 us (1.048)
  waiting for transfers between devices: 37.6 us -> 41.9 us
    all_to_all x0 -> x1, starting transfers between devices: none -> 6.86 us  [on_device(): x_parts = lax.all_to_all(x_copies, 'series', 0, 0, tiled=True)]
    all_to_all x2 -> x1, starting transfers between devices: 20.7 us -> 14 us  [gather_by_a2a(): return lax.all_to_all(copies, axis, 0, 0, tiled=True)]
    all_to_all x0 -> x1, waiting for transfers between devices: none -> 4.91 us  [on_device(): x_parts = lax.all_to_all(x_copies, 'series', 0, 0, tiled=True)]
    dot_general x1, matrix products: 1.23 us -> 3.43 us  [on_device(): pred = jnp.dot(f_block, x_full, preferred_element_type=jnp.float32)]
    all_to_all x2 -> x1, waiting for transfers between devices: 13.2 us -> 14.7 us  [gather_by_a2a(): return lax.all_to_all(copies, axis, 0, 0, tiled=True)]
    all_to_all x1, blocking collectives: 4.58 us -> 5.77 us  [on_device(): lax.all_to_all(by_core.astype(jnp.bfloat16), 'core', 1, 1, tiled=True)]
  transfers between devices with their start and end apart: 5 -> 5, of which waited for: 4 -> 4; matrix products, arithmetic and copies ran while one was open for 9% -> 12% of each run, Pallas kernels for 0% -> 0%
where the time goes in v7:
time: 109 us; the launch traced here: 108 us
  waiting for transfers between devices  41.9 us (38%)
  starting transfers between devices  33.8 us (31%)
  blocking collectives  10.3 us (9%)
  matrix products  8.05 us (7%)
  between operations  6.15 us (6%)
  other arithmetic  4.11 us (4%)
  local copies, waits for them, and re-layouts  3.66 us (3%)
    all_to_all x1, waiting for transfers between devices, gather_by_a2a(): return lax.all_to_all(copies, axis, 0, 0, tiled=True)  14.7 us
    all_to_all x1, waiting for transfers between devices, on_device(): by_row = lax.all_to_all(by_core.astype(jnp.bfloat16), ROW, 0, 0, tiled=True)  14.3 us
    all_to_all x1, starting transfers between devices, gather_by_a2a(): return lax.all_to_all(copies, axis, 0, 0, tiled=True)  14 us
    all_to_all x1, waiting for transfers between devices, on_device(): lax.all_to_all(pieces.astype(jnp.bfloat16), 'series', 0, 0, tiled=True)  7.94 us
    all_to_all x1, starting transfers between devices, on_device(): by_row = lax.all_to_all(by_core.astype(jnp.bfloat16), ROW, 0, 0, tiled=True)  7.22 us
    all_to_all x1, starting transfers between devices, on_device(): x_parts = lax.all_to_all(x_copies, 'series', 0, 0, tiled=True)  6.86 us
    all_to_all x1, blocking collectives, on_device(): lax.all_to_all(by_core.astype(jnp.bfloat16), 'core', 1, 1, tiled=True)  5.77 us
    all_to_all x1, waiting for transfers between devices, on_device(): x_parts = lax.all_to_all(x_copies, 'series', 0, 0, tiled=True)  4.91 us
  transfers between devices with their start and end apart: 5, of which 4 were waited for; matrix products, arithmetic and copies ran while one was open for 12% of the time, Pallas kernels for 0%

profile of v7, /device:TPU:8, one launch (start us, length us, event | category | flops | bytes accessed | tf_op | source)
XLA Modules:
  0.0 108.0 jit_solution(11268439815528431127)
XLA Ops:
  0.7 0.8 convert_element_type.52
  1.4 0.9 broadcast_in_dim.48
  2.3 14.0 %all-to-all-start = ((bf16[32,64,128]{2,1,0:T(8,128)(2,1)}), bf16[32,64,128]{2,1,0:T(8,128)(2,1)S(1)}, u32[]{:S(2)}, u32[]{:S(2)}) async-start(bf16[32,64,128]{2,1,0:T(8,128)(2,1)} %broadcast_in_dim.48), calls=%async_computation | async-start | bytes 1048576 | tf_op jit(solution)/shard_map/all_to_all | solution.py:45
  16.3 0.8 convert_element_type.53
  17.1 1.4 %fusion.61 = (s32[1]{0:T(128)}, s32[1]{0:T(128)}, s32[1]{0:T(128)}, s32[1]{0:T(128)}) fusion(s32[4]{0:T(128)} %param.15), kind=kLoop, calls=%fused_computation.87 | loop fusion | bytes 32 | tf_op jit(solution)/shard_map/slice | solution.py:100
  18.5 14.7 %all-to-all-done = bf16[32,64,128]{2,1,0:T(8,128)(2,1)S(1)} async-done(((bf16[32,64,128]{2,1,0:T(8,128)(2,1)}), bf16[32,64,128]{2,1,0:T(8,128)(2,1)S(1)}, u32[]{:S(2)}, u32[]{:S(2)}) %all-to-all-start) | async-done | bytes 524320 | tf_op jit(solution)/shard_map/all_to_all | solution.py:45
  33.2 0.7 broadcast_in_dim.49
  34.1 4.6 %all_to_all.30 = bf16[2,32,64,128]{3,2,1,0:T(8,128)(2,1)S(1)} all-to-all(bf16[2,32,64,128]{3,2,1,0:T(8,128)(2,1)S(1)} %broadcast_in_dim.50), channel_id=1, replica_groups=mesh['series'=8,'z'=8,'ylo'=4,'core'=2] {'core'}, dimensions={0} | all-to-all | bytes 2097152 | tf_op jit(solution)/shard_map/all_to_all | solution.py:45
  38.7 6.9 %all-to-all-start.2 = ((bf16[8,16,512]{2,1,0:T(8,128)(2,1)}), bf16[8,16,512]{2,1,0:T(8,128)(2,1)S(1)}, u32[]{:S(2)}, u32[]{:S(2)}) async-start(bf16[8,16,512]{2,1,0:T(8,128)(2,1)} %broadcast_in_dim.49), calls=%async_computation.2 | async-start | bytes 262144 | tf_op jit(solution)/shard_map/all_to_all | solution.py:62
  51.1 4.9 %all-to-all-done.2 = bf16[8,16,512]{2,1,0:T(8,128)(2,1)S(1)} async-done(((bf16[8,16,512]{2,1,0:T(8,128)(2,1)}), bf16[8,16,512]{2,1,0:T(8,128)(2,1)S(1)}, u32[]{:S(2)}, u32[]{:S(2)}) %all-to-all-start.2) | async-done | bytes 131104 | tf_op jit(solution)/shard_map/all_to_all | solution.py:62
  56.0 1.9 %collective-permute-start = (bf16[128,128]{1,0:T(8,128)(2,1)S(1)}, bf16[128,128]{1,0:T(8,128)(2,1)S(1)}, u32[]{:S(2)}, u32[]{:S(2)}) collective-permute-start(bf16[128,128]{1,0:T(8,128)(2,1)S(1)} %slice.92), channel_id=1, source_target_pairs={{0,1},{1,2},{2,3},{3,4},{4,5},{5,6},{6,7},{7,8},{8,9},{9,10},{10,1... | collective-permute-start | bytes 98312 | tf_op jit(solution)/shard_map/ppermute | solution.py:92
  58.0 3.4 %fusion = bf16[4096,512]{1,0:T(8,128)(2,1)S(1)} fusion(bf16[4096,512]{1,0:T(8,128)(2,1)} %param.9, bf16[4096,128]{1,0:T(8,128)(2,1)S(1)} %bitcast.81, bf16[128,512]{1,0:T(8,128)(2,1)S(1)} %bitcast.84, f32[32,512]{1,0:T(8,128)S(1)} %bitcast.89), kind=kOutput, calls=%fused_computation.1 | convolution fusion | flops 545259520 | bytes 9633792 | tf_op jit(solution)/shard_map/dot_general | solution.py:67
  61.4 1.4 %fusion.19 = bf16[128,512]{1,0:T(8,128)(2,1)} fusion(bf16[4096,128]{1,0:T(8,128)(2,1)S(1)} %bitcast.82, bf16[4096,512]{1,0:T(8,128)(2,1)S(1)} %fusion), kind=kOutput, calls=%fused_computation.26 | convolution fusion | flops 537067520 | bytes 5373952 | tf_op jit(solution)/shard_map/dot_general | solution.py:83
  62.8 1.2 %fusion.2 = bf16[4096,128]{1,0:T(8,128)(2,1)S(1)} fusion(bf16[4096,512]{1,0:T(8,128)(2,1)S(1)} %fusion, bf16[128,512]{1,0:T(8,128)(2,1)S(1)} %bitcast.85), kind=kOutput, calls=%fused_computation.4 | convolution fusion | flops 538443776 | bytes 5373952 | tf_op jit(solution)/shard_map/dot_general | solution.py:75
  64.1 5.8 %all_to_all.31 = bf16[32,2,64,128]{3,2,0,1:T(8,128)(2,1)S(1)} all-to-all(bf16[32,2,64,128]{3,2,0,1:T(8,128)(2,1)S(1)} %copy.52), channel_id=1, replica_groups=mesh['series'=8,'z'=8,'ylo'=4,'core'=2] {'core'}, dimensions={1} | all-to-all | bytes 2097152 | tf_op jit(solution)/shard_map/all_to_all | solution.py:77
  69.9 3.8 %all-to-all-start.5 = ((bf16[8,16,512]{2,1,0:T(8,128)(2,1)}), bf16[8,16,512]{2,1,0:T(8,128)(2,1)S(1)}, u32[]{:S(2)}, u32[]{:S(2)}) async-start(bf16[8,16,512]{2,1,0:T(8,128)(2,1)} %bitcast.6), calls=%async_computation.5 | async-start | bytes 262144 | tf_op jit(solution)/shard_map/all_to_all | solution.py:88
  73.7 1.1 %reduce_sum.30 = bf16[32,64,128]{2,1,0:T(8,128)(2,1)} reduce(bf16[32,2,64,128]{3,2,0,1:T(8,128)(2,1)S(1)} %all_to_all.31, bf16[]{:T(256)} %constant.56.clone.1), dimensions={1}, to_apply=%region_0.0 | reduce | flops 262144 | bytes 1572866 | tf_op jit(solution)/shard_map/reduce_sum | solution.py:78
  75.5 0.3 fusion.22
  76.0 0.3 fusion.23
  76.3 7.9 %all-to-all-done.5 = bf16[8,16,512]{2,1,0:T(8,128)(2,1)S(1)} async-done(((bf16[8,16,512]{2,1,0:T(8,128)(2,1)}), bf16[8,16,512]{2,1,0:T(8,128)(2,1)S(1)}, u32[]{:S(2)}, u32[]{:S(2)}) %all-to-all-start.5) | async-done | bytes 131104 | tf_op jit(solution)/shard_map/all_to_all | solution.py:88
  84.2 7.2 %all-to-all-start.4 = ((bf16[32,64,128]{2,1,0:T(8,128)(2,1)}), bf16[32,64,128]{2,1,0:T(8,128)(2,1)S(1)}, u32[]{:S(2)}, u32[]{:S(2)}) async-start(bf16[32,64,128]{2,1,0:T(8,128)(2,1)} %reduce_sum.30), calls=%async_computation.4 | async-start | bytes 1048576 | tf_op jit(solution)/shard_map/all_to_all | solution.py:79
  92.3 0.6 fusion.29
  92.9 14.3 %all-to-all-done.4 = bf16[32,64,128]{2,1,0:T(8,128)(2,1)S(1)} async-done(((bf16[32,64,128]{2,1,0:T(8,128)(2,1)}), bf16[32,64,128]{2,1,0:T(8,128)(2,1)S(1)}, u32[]{:S(2)}, u32[]{:S(2)}) %all-to-all-start.4) | async-done | bytes 524320 | tf_op jit(solution)/shard_map/all_to_all | solution.py:79
  107.3 0.7 divide_subtract_fusion
  (36 shorter events, 2.2 us)
Async XLA Ops:
  0.6 50.1 %copy-start.5 = (s32[32,4]{0,1:T(4,128)S(1)}, s32[32,4]{0,1:T(4,128)}, u32[]{:S(2)}) copy-start(s32[32,4]{0,1:T(4,128)} %param.10) | copy-start | bytes 1540
  0.6 50.4 %copy-start.6 = (f32[4,128]{1,0:T(4,128)S(1)}, f32[4,128]{1,0:T(4,128)}, u32[]{:S(2)}) copy-start(f32[4,128]{1,0:T(4,128)} %param.17) | copy-start | bytes 6148
  2.3 30.8 %all-to-all-start = ((bf16[32,64,128]{2,1,0:T(8,128)(2,1)}), bf16[32,64,128]{2,1,0:T(8,128)(2,1)S(1)}, u32[]{:S(2)}, u32[]{:S(2)}) async-start(bf16[32,64,128]{2,1,0:T(8,128)(2,1)} %broadcast_in_dim.48), calls=%async_computation | async-start | bytes 1048576 | tf_op jit(solution)/shard_map/all_to_all | solution.py:45
  38.7 17.4 %all-to-all-start.2 = ((bf16[8,16,512]{2,1,0:T(8,128)(2,1)}), bf16[8,16,512]{2,1,0:T(8,128)(2,1)S(1)}, u32[]{:S(2)}, u32[]{:S(2)}) async-start(bf16[8,16,512]{2,1,0:T(8,128)(2,1)} %broadcast_in_dim.49), calls=%async_computation.2 | async-start | bytes 262144 | tf_op jit(solution)/shard_map/all_to_all | solution.py:62
  56.0 18.8 %collective-permute-start = (bf16[128,128]{1,0:T(8,128)(2,1)S(1)}, bf16[128,128]{1,0:T(8,128)(2,1)S(1)}, u32[]{:S(2)}, u32[]{:S(2)}) collective-permute-start(bf16[128,128]{1,0:T(8,128)(2,1)S(1)} %slice.92), channel_id=1, source_target_pairs={{0,1},{1,2},{2,3},{3,4},{4,5},{5,6},{6,7},{7,8},{8,9},{9,10},{10,1... | collective-permute-start | bytes 98312 | tf_op jit(solution)/shard_map/ppermute | solution.py:92
  64.0 10.9 %copy-start = (bf16[4,2,128,128]{3,2,1,0:T(8,128)(2,1)S(1)}, bf16[4,2,128,128]{3,2,1,0:T(8,128)(2,1)}, u32[]{:S(2)}) copy-start(bf16[4,2,128,128]{3,2,1,0:T(8,128)(2,1)} %param.16) | copy-start | bytes 786436
  69.9 14.3 %all-to-all-start.5 = ((bf16[8,16,512]{2,1,0:T(8,128)(2,1)}), bf16[8,16,512]{2,1,0:T(8,128)(2,1)S(1)}, u32[]{:S(2)}, u32[]{:S(2)}) async-start(bf16[8,16,512]{2,1,0:T(8,128)(2,1)} %bitcast.6), calls=%async_computation.5 | async-start | bytes 262144 | tf_op jit(solution)/shard_map/all_to_all | solution.py:88
  75.2 17.0 %copy-start.1 = (f32[16,512]{1,0:T(8,128)S(1)}, f32[16,512]{1,0:T(8,128)}, u32[]{:S(2)}) copy-start(f32[16,512]{1,0:T(8,128)} %param.14) | copy-start | bytes 98308
  75.2 32.1 %copy-start.2 = (f32[64,128]{1,0:T(8,128)S(1)}, f32[64,128]{1,0:T(8,128)}, u32[]{:S(2)}) copy-start(f32[64,128]{1,0:T(8,128)} %param.11) | copy-start | bytes 98308
  75.2 32.1 %copy-start.3 = (f32[64,128]{1,0:T(8,128)S(1)}, f32[64,128]{1,0:T(8,128)}, u32[]{:S(2)}) copy-start(f32[64,128]{1,0:T(8,128)} %param.12) | copy-start | bytes 98308
  75.3 32.1 %copy-start.4 = (f32[64,128]{1,0:T(8,128)S(1)}, f32[64,128]{1,0:T(8,128)}, u32[]{:S(2)}) copy-start(f32[64,128]{1,0:T(8,128)} %param.13) | copy-start | bytes 98308
  84.2 23.0 %all-to-all-start.4 = ((bf16[32,64,128]{2,1,0:T(8,128)(2,1)}), bf16[32,64,128]{2,1,0:T(8,128)(2,1)S(1)}, u32[]{:S(2)}, u32[]{:S(2)}) async-start(bf16[32,64,128]{2,1,0:T(8,128)(2,1)} %reduce_sum.30), calls=%async_computation.4 | async-start | bytes 1048576 | tf_op jit(solution)/shard_map/all_to_all | solution.py:79

commit v8 on v5

--- a/solution.py
+++ b/solution.py
@@ -73,8 +73,10 @@
     contract_time = (((1,), (1,)), ((), ()))
     partial_f = -lax.dot_general(rb, x_full, contract_time, preferred_element_type=jnp.float32) * scale_f
     by_core = partial_f.reshape(n_row, CORES, own_rows, K)
-    by_core = lax.all_to_all(by_core.astype(jnp.bfloat16), "core", 1, 1, tiled=True)
-    by_core = by_core.astype(jnp.float32).sum(1)
+    core = lax.axis_index("core")
+    kept = lax.dynamic_index_in_dim(by_core, core, 1, keepdims=False)
+    given = lax.dynamic_index_in_dim(by_core, 1 - core, 1, keepdims=False)
+    by_core = kept + lax.ppermute(given.astype(jnp.bfloat16), "core", [(0, 1), (1, 0)]).astype(jnp.float32)
     by_row = lax.all_to_all(by_core.astype(jnp.bfloat16), ROW, 0, 0, tiled=True)
     grad_f = by_row.astype(jnp.float32).sum(0)
     factors_new, m_new, v_new = adam_update(factors, adam_m, adam_v, grad_f)

time: 104 us -> 103 us (level)
  blocking collectives: 9.41 us -> 4.84 us
  starting transfers between devices: 33.2 us -> 35.4 us
    all_to_all x1 -> x0, blocking collectives: 4.58 us -> none  [on_device(): lax.all_to_all(by_core.astype(jnp.bfloat16), 'core', 1, 1, tiled=True)]
    ppermute x0 -> x1, starting transfers between devices: none -> 2.02 us  [on_device(): lax.ppermute(given.astype(jnp.bfloat16), 'core', [(0, 1), (1, 0)])]
    convert_element_type x0 -> x1, other arithmetic: none -> 2 us  [on_device(): by_row = lax.all_to_all(by_core.astype(jnp.bfloat16), ROW, 0, 0, tiled=True)]
    reduce_sum x1 -> x0, other arithmetic: 1.15 us -> none  [on_device(): by_core = by_core.astype(jnp.float32).sum(1)]
  transfers between devices with their start and end apart: 5 -> 6, of which waited for: 4 -> 4; matrix products, arithmetic and copies ran while one was open for 9% -> 11% of each run, Pallas kernels for 0% -> 0%
where the time goes in v8:
time: 103 us; the launch traced here: 102 us
  waiting for transfers between devices  37.1 us (36%)
  starting transfers between devices  35.4 us (34%)
  matrix products  7.46 us (7%)
  between operations  6.1 us (6%)
  other arithmetic  5.69 us (6%)
  local copies, waits for them, and re-layouts  5.3 us (5%)
  blocking collectives  4.84 us (5%)
    all_to_all x2, starting transfers between devices, gather_by_a2a(): return lax.all_to_all(copies, axis, 0, 0, tiled=True)  20.7 us
    all_to_all x1, waiting for transfers between devices, on_device(): by_row = lax.all_to_all(by_core.astype(jnp.bfloat16), ROW, 0, 0, tiled=True)  15.4 us
    all_to_all x2, waiting for transfers between devices, gather_by_a2a(): return lax.all_to_all(copies, axis, 0, 0, tiled=True)  13.2 us
    all_to_all x1, waiting for transfers between devices, on_device(): lax.all_to_all(pieces.astype(jnp.bfloat16), 'series', 0, 0, tiled=True)  8.53 us
    all_to_all x1, starting transfers between devices, on_device(): by_row = lax.all_to_all(by_core.astype(jnp.bfloat16), ROW, 0, 0, tiled=True)  7.24 us
    all_to_all x1, blocking collectives, gather_by_a2a(): return lax.all_to_all(copies, axis, 0, 0, tiled=True)  4.84 us
    all_to_all x1, starting transfers between devices, on_device(): lax.all_to_all(pieces.astype(jnp.bfloat16), 'series', 0, 0, tiled=True)  3.51 us
  transfers between devices with their start and end apart: 6, of which 4 were waited for; matrix products, arithmetic and copies ran while one was open for 11% of the time, Pallas kernels for 0%

profile of v8, /device:TPU:8, one launch (start us, length us, event | category | flops | bytes accessed | tf_op | source)
XLA Modules:
  0.0 101.9 jit_solution(1567144826141952745)
XLA Ops:
  0.6 0.8 convert_element_type.60
  2.1 8.7 %all-to-all-start.2 = ((bf16[8,16,512]{2,1,0:T(8,128)(2,1)}), bf16[8,16,512]{2,1,0:T(8,128)(2,1)S(1)}, u32[]{:S(2)}, u32[]{:S(2)}) async-start(bf16[8,16,512]{2,1,0:T(8,128)(2,1)} %broadcast_in_dim.50), calls=%async_computation.2 | async-start | bytes 262144 | tf_op jit(solution)/shard_map/all_to_all | solution.py:45
  10.8 1.4 %fusion.62 = (s32[1]{0:T(128)}, s32[1]{0:T(128)}, s32[1]{0:T(128)}, s32[1]{0:T(128)}) fusion(s32[4]{0:T(128)} %param.15), kind=kLoop, calls=%fused_computation.90 | loop fusion | bytes 32 | tf_op jit(solution)/shard_map/slice | solution.py:101
  12.2 0.8 convert_element_type.59
  12.9 0.8 slice_bitcast_fusion
  13.8 8.1 %all-to-all-done.2 = bf16[8,16,512]{2,1,0:T(8,128)(2,1)S(1)} async-done(((bf16[8,16,512]{2,1,0:T(8,128)(2,1)}), bf16[8,16,512]{2,1,0:T(8,128)(2,1)S(1)}, u32[]{:S(2)}, u32[]{:S(2)}) %all-to-all-start.2) | async-done | bytes 131104 | tf_op jit(solution)/shard_map/all_to_all | solution.py:45
  21.9 0.9 broadcast_in_dim.48
  22.8 12.0 %all-to-all-start = ((bf16[32,64,128]{2,1,0:T(8,128)(2,1)}), bf16[32,64,128]{2,1,0:T(8,128)(2,1)S(1)}, u32[]{:S(2)}, u32[]{:S(2)}) async-start(bf16[32,64,128]{2,1,0:T(8,128)(2,1)} %broadcast_in_dim.48), calls=%async_computation | async-start | bytes 1048576 | tf_op jit(solution)/shard_map/all_to_all | solution.py:45
  34.9 1.9 %collective-permute-start.1 = (bf16[128,128]{1,0:T(8,128)(2,1)S(1)}, bf16[128,128]{1,0:T(8,128)(2,1)S(1)}, u32[]{:S(2)}, u32[]{:S(2)}) collective-permute-start(bf16[128,128]{1,0:T(8,128)(2,1)S(1)} %slice.92), channel_id=1, source_target_pairs={{0,1},{1,2},{2,3},{3,4},{4,5},{5,6},{6,7},{7,8},{8,9},{9,10},{10,1... | collective-permute-start | bytes 98312 | tf_op jit(solution)/shard_map/ppermute | solution.py:93
  42.0 0.7 convert_element_type.57
  43.0 1.0 %fusion.22 = f32[640,128]{0,1:T(8,128)S(1)} fusion(s32[]{:T(128)S(6)} %select_n.38, bf16[128,640]{1,0:T(8,128)(2,1)S(1)} %fusion.21, bf16[4,2,128,128]{3,2,1,0:T(8,128)(2,1)} %param.16), kind=kOutput, calls=%fused_computation.41 | convolution fusion | flops 20971520 | bytes 524292 | tf_op jit(solution)/shard_map/dot_general | solution.py:37
  44.0 1.0 select_convert_fusion.2
  45.5 5.1 %all-to-all-done = bf16[32,64,128]{2,1,0:T(8,128)(2,1)S(1)} async-done(((bf16[32,64,128]{2,1,0:T(8,128)(2,1)}), bf16[32,64,128]{2,1,0:T(8,128)(2,1)S(1)}, u32[]{:S(2)}, u32[]{:S(2)}) %all-to-all-start) | async-done | bytes 524320 | tf_op jit(solution)/shard_map/all_to_all | solution.py:45
  50.9 4.8 %all_to_all.25 = bf16[2,32,64,128]{3,2,1,0:T(8,128)(2,1)S(1)} all-to-all(bf16[2,32,64,128]{3,2,1,0:T(8,128)(2,1)S(1)} %broadcast_in_dim.49), channel_id=1, replica_groups=mesh['series'=8,'z'=8,'ylo'=4,'core'=2] {'core'}, dimensions={0} | all-to-all | bytes 2097152 | tf_op jit(solution)/shard_map/all_to_all | solution.py:45
  55.8 1.2 %fusion = bf16[4096,512]{1,0:T(8,128)(2,1)S(1)} fusion(bf16[4096,512]{1,0:T(8,128)(2,1)S(1)} %copy-done, bf16[4096,128]{1,0:T(8,128)(2,1)S(1)} %bitcast.96, bf16[128,512]{1,0:T(8,128)(2,1)S(1)} %bitcast.94, f32[32,512]{1,0:T(8,128)S(1)} %bitcast.98), kind=kOutput, calls=%fused_computation.1 | convolution fusion | flops 545259520 | bytes 9633792 | tf_op jit(solution)/shard_map/dot_general | solution.py:66
  57.1 1.3 %fusion.1 = f32[4096,128]{1,0:T(8,128)S(1)} fusion(bf16[4096,512]{1,0:T(8,128)(2,1)S(1)} %fusion, bf16[128,512]{1,0:T(8,128)(2,1)S(1)} %bitcast.95), kind=kOutput, calls=%fused_computation.3 | convolution fusion | flops 537919488 | bytes 6422528 | tf_op jit(solution)/shard_map/dot_general | solution.py:74
  58.3 0.9 fusion.20
  59.2 2.0 %collective-permute-start = (bf16[32,64,128]{2,1,0:T(8,128)(2,1)}, bf16[32,64,128]{2,1,0:T(8,128)(2,1)}, u32[]{:S(2)}, u32[]{:S(2)}) collective-permute-start(bf16[32,64,128]{2,1,0:T(8,128)(2,1)} %fusion.20), channel_id=1, source_target_pairs={{0,1},{1,0},{2,3},{3,2},{4,5},{5,4},{6,7},{7,6},{8,9},{9,8},{10,11... | collective-permute-start | bytes 1572872 | tf_op jit(solution)/shard_map/ppermute | solution.py:79
  61.5 1.5 %fusion.18 = bf16[512,128]{0,1:T(8,128)(2,1)} fusion(bf16[4096,512]{1,0:T(8,128)(2,1)S(1)} %fusion, bf16[4096,128]{1,0:T(8,128)(2,1)S(1)} %bitcast.97), kind=kOutput, calls=%fused_computation.25 | convolution fusion | flops 537067520 | bytes 5373952 | tf_op jit(solution)/shard_map/dot_general | solution.py:84
  63.0 3.5 %all-to-all-start.4 = ((bf16[8,16,512]{2,1,0:T(8,128)(2,1)}), bf16[8,16,512]{2,1,0:T(8,128)(2,1)S(1)}, u32[]{:S(2)}, u32[]{:S(2)}) async-start(bf16[8,16,512]{2,1,0:T(8,128)(2,1)} %bitcast.9), calls=%async_computation.4 | async-start | bytes 262144 | tf_op jit(solution)/shard_map/all_to_all | solution.py:89
  66.5 2.0 %fusion.19 = bf16[32,64,128]{2,1,0:T(8,128)(2,1)} fusion(bf16[32,64,128]{2,1,0:T(8,128)(2,1)} %collective-permute-done, f32[32,2,64,128]{3,2,1,0:T(8,128)S(1)} %bitcast.90, s32[]{:T(128)S(6)} %select_n.35), kind=kLoop, calls=%fused_computation.27 | loop fusion | flops 786432 | bytes 2097156 | tf_op jit(solution)/shard_map/convert_element_type | solution.py:80
  68.5 8.5 %all-to-all-done.4 = bf16[8,16,512]{2,1,0:T(8,128)(2,1)S(1)} async-done(((bf16[8,16,512]{2,1,0:T(8,128)(2,1)}), bf16[8,16,512]{2,1,0:T(8,128)(2,1)S(1)}, u32[]{:S(2)}, u32[]{:S(2)}) %all-to-all-start.4) | async-done | bytes 131104 | tf_op jit(solution)/shard_map/all_to_all | solution.py:89
  77.1 7.2 %all-to-all-start.3 = ((bf16[32,64,128]{2,1,0:T(8,128)(2,1)}), bf16[32,64,128]{2,1,0:T(8,128)(2,1)S(1)}, u32[]{:S(2)}, u32[]{:S(2)}) async-start(bf16[32,64,128]{2,1,0:T(8,128)(2,1)} %fusion.19), calls=%async_computation.3 | async-start | bytes 1048576 | tf_op jit(solution)/shard_map/all_to_all | solution.py:80
  85.7 15.4 %all-to-all-done.3 = bf16[32,64,128]{2,1,0:T(8,128)(2,1)S(1)} async-done(((bf16[32,64,128]{2,1,0:T(8,128)(2,1)}), bf16[32,64,128]{2,1,0:T(8,128)(2,1)S(1)}, u32[]{:S(2)}, u32[]{:S(2)}) %all-to-all-start.3) | async-done | bytes 524320 | tf_op jit(solution)/shard_map/all_to_all | solution.py:80
  (35 shorter events, 4.2 us)
Async XLA Ops:
  0.6 44.4 %copy-start.1 = (bf16[4,2,128,128]{3,2,1,0:T(8,128)(2,1)S(1)}, bf16[4,2,128,128]{3,2,1,0:T(8,128)(2,1)}, u32[]{:S(2)}) copy-start(bf16[4,2,128,128]{3,2,1,0:T(8,128)(2,1)} %param.16) | copy-start | bytes 786436
  2.1 19.8 %all-to-all-start.2 = ((bf16[8,16,512]{2,1,0:T(8,128)(2,1)}), bf16[8,16,512]{2,1,0:T(8,128)(2,1)S(1)}, u32[]{:S(2)}, u32[]{:S(2)}) async-start(bf16[8,16,512]{2,1,0:T(8,128)(2,1)} %broadcast_in_dim.50), calls=%async_computation.2 | async-start | bytes 262144 | tf_op jit(solution)/shard_map/all_to_all | solution.py:45
  22.8 27.8 %all-to-all-start = ((bf16[32,64,128]{2,1,0:T(8,128)(2,1)}), bf16[32,64,128]{2,1,0:T(8,128)(2,1)S(1)}, u32[]{:S(2)}, u32[]{:S(2)}) async-start(bf16[32,64,128]{2,1,0:T(8,128)(2,1)} %broadcast_in_dim.48), calls=%async_computation | async-start | bytes 1048576 | tf_op jit(solution)/shard_map/all_to_all | solution.py:45
  34.9 8.1 %collective-permute-start.1 = (bf16[128,128]{1,0:T(8,128)(2,1)S(1)}, bf16[128,128]{1,0:T(8,128)(2,1)S(1)}, u32[]{:S(2)}, u32[]{:S(2)}) collective-permute-start(bf16[128,128]{1,0:T(8,128)(2,1)S(1)} %slice.92), channel_id=1, source_target_pairs={{0,1},{1,2},{2,3},{3,4},{4,5},{5,6},{6,7},{7,8},{8,9},{9,10},{10,1... | collective-permute-start | bytes 98312 | tf_op jit(solution)/shard_map/ppermute | solution.py:93
  50.6 5.2 %copy-start = (bf16[4096,512]{1,0:T(8,128)(2,1)S(1)}, bf16[4096,512]{1,0:T(8,128)(2,1)}, u32[]{:S(2)}) copy-start(bf16[4096,512]{1,0:T(8,128)(2,1)} %param.9) | copy-start | bytes 12582916
  59.2 7.3 %collective-permute-start = (bf16[32,64,128]{2,1,0:T(8,128)(2,1)}, bf16[32,64,128]{2,1,0:T(8,128)(2,1)}, u32[]{:S(2)}, u32[]{:S(2)}) collective-permute-start(bf16[32,64,128]{2,1,0:T(8,128)(2,1)} %fusion.20), channel_id=1, source_target_pairs={{0,1},{1,0},{2,3},{3,2},{4,5},{5,4},{6,7},{7,6},{8,9},{9,8},{10,11... | collective-permute-start | bytes 1572872 | tf_op jit(solution)/shard_map/ppermute | solution.py:79
  63.0 22.1 %copy-start.2 = (f32[16,512]{1,0:T(8,128)S(1)}, f32[16,512]{1,0:T(8,128)}, u32[]{:S(2)}) copy-start(f32[16,512]{1,0:T(8,128)} %param.14) | copy-start | bytes 98308
  63.0 38.2 %copy-start.3 = (f32[64,128]{1,0:T(8,128)S(1)}, f32[64,128]{1,0:T(8,128)}, u32[]{:S(2)}) copy-start(f32[64,128]{1,0:T(8,128)} %param.11) | copy-start | bytes 98308
  63.0 38.2 %copy-start.4 = (f32[64,128]{1,0:T(8,128)S(1)}, f32[64,128]{1,0:T(8,128)}, u32[]{:S(2)}) copy-start(f32[64,128]{1,0:T(8,128)} %param.12) | copy-start | bytes 98308
  63.0 38.3 %copy-start.5 = (f32[64,128]{1,0:T(8,128)S(1)}, f32[64,128]{1,0:T(8,128)}, u32[]{:S(2)}) copy-start(f32[64,128]{1,0:T(8,128)} %param.13) | copy-start | bytes 98308
  63.0 14.1 %all-to-all-start.4 = ((bf16[8,16,512]{2,1,0:T(8,128)(2,1)}), bf16[8,16,512]{2,1,0:T(8,128)(2,1)S(1)}, u32[]{:S(2)}, u32[]{:S(2)}) async-start(bf16[8,16,512]{2,1,0:T(8,128)(2,1)} %bitcast.9), calls=%async_computation.4 | async-start | bytes 262144 | tf_op jit(solution)/shard_map/all_to_all | solution.py:89
  77.1 24.1 %all-to-all-start.3 = ((bf16[32,64,128]{2,1,0:T(8,128)(2,1)}), bf16[32,64,128]{2,1,0:T(8,128)(2,1)S(1)}, u32[]{:S(2)}, u32[]{:S(2)}) async-start(bf16[32,64,128]{2,1,0:T(8,128)(2,1)} %fusion.19), calls=%async_computation.3 | async-start | bytes 1048576 | tf_op jit(solution)/shard_map/all_to_all | solution.py:80

commit v9 on v8

--- a/solution.py
+++ b/solution.py
@@ -57,34 +57,36 @@
 
     fb = factors.astype(jnp.bfloat16)
     f_rows = gather_by_a2a(fb, ROW, n_row)
-    f_all = gather_by_a2a(f_rows, "core", CORES)
-    f_block = jnp.swapaxes(f_all, 0, 1).reshape(n_tm * own_rows, K)
+    core = lax.axis_index("core")
+    f_other = lax.ppermute(f_rows, "core", [(0, 1), (1, 0)])
 
     x_parts = gather_by_a2a(basis.astype(jnp.bfloat16), "series", n_series)
     x_full = x_parts.reshape(n_series * rank_part, width)
 
-    pred = jnp.dot(f_block, x_full, preferred_element_type=jnp.float32)
     tiles = tile_mask.shape[0]
     mask_cols = jnp.repeat(tile_mask.astype(jnp.float32), TILE, axis=1)
-    gap = (y_obs.astype(jnp.float32) - pred).reshape(tiles, TILE, width)
-    resid = (mask_cols[:, None, :] * gap).reshape(tiles * TILE, width)
-    rb = resid.astype(jnp.bfloat16)
     scale_f = 1.0 / math.sqrt(total_time)
     contract_time = (((1,), (1,)), ((), ()))
-    partial_f = -lax.dot_general(rb, x_full, contract_time, preferred_element_type=jnp.float32) * scale_f
-    by_core = partial_f.reshape(n_row, CORES, own_rows, K)
-    core = lax.axis_index("core")
-    kept = lax.dynamic_index_in_dim(by_core, core, 1, keepdims=False)
-    given = lax.dynamic_index_in_dim(by_core, 1 - core, 1, keepdims=False)
+    y_rows = y_obs.reshape(n_row, CORES, own_rows, width)
+
+    def half(f_half, owner):
+        f2 = f_half.reshape(n_row * own_rows, K)
+        y_half = lax.dynamic_index_in_dim(y_rows, owner, 1, keepdims=False)
+        pred = jnp.dot(f2, x_full, preferred_element_type=jnp.float32).reshape(n_row, own_rows, width)
+        gap = y_half.astype(jnp.float32) - pred
+        rb = (mask_cols[:, None, :] * gap).reshape(n_row * own_rows, width).astype(jnp.bfloat16)
+        part_f = -lax.dot_general(rb, x_full, contract_time, preferred_element_type=jnp.float32) * scale_f
+        part_x = lax.dot_general(f2, rb, (((0,), (0,)), ((), ())), preferred_element_type=jnp.float32)
+        return part_f.reshape(n_row, own_rows, K), part_x
+
+    kept, x_mine = half(f_rows, core)
+    given, x_theirs = half(f_other, 1 - core)
     by_core = kept + lax.ppermute(given.astype(jnp.bfloat16), "core", [(0, 1), (1, 0)]).astype(jnp.float32)
     by_row = lax.all_to_all(by_core.astype(jnp.bfloat16), ROW, 0, 0, tiled=True)
     grad_f = by_row.astype(jnp.float32).sum(0)
     factors_new, m_new, v_new = adam_update(factors, adam_m, adam_v, grad_f)
 
-    partial_x = -lax.dot_general(
-        f_block, rb, (((0,), (0,)), ((), ())), preferred_element_type=jnp.float32
-    )
-    partial_x = partial_x * math.sqrt(K / total_series)
+    partial_x = -(x_mine + x_theirs) * math.sqrt(K / total_series)
     pieces = partial_x.reshape(n_series, rank_part, width)
     arrived = lax.all_to_all(pieces.astype(jnp.bfloat16), "series", 0, 0, tiled=True)
     grad_x = arrived.astype(jnp.float32).sum(0)

time: 103 us -> 98.7 us (0.958)
  blocking collectives: 4.84 us -> 0 us
  other arithmetic: 5.69 us -> 3.97 us
  matrix products: 7.46 us -> 9 us
  waiting for transfers between devices: 37.1 us -> 38.6 us
  local copies, waits for them, and re-layouts: 5.3 us -> 4.1 us
    all_to_all x1 -> x0, blocking collectives: 4.84 us -> none  [gather_by_a2a(): return lax.all_to_all(copies, axis, 0, 0, tiled=True)]
    dot_general x3 -> x6, matrix products: 3.96 us -> 7.01 us  [the longest x2 3.15 us: half(): jnp.dot(f2, x_full, preferred_element_type=jnp.float32)]
    all_to_all x1, waiting for transfers between devices: 15.4 us -> 13.5 us  [on_device(): by_row = lax.all_to_all(by_core.astype(jnp.bfloat16), ROW, 0, 0, tiled=True)]
    ppermute x0 -> x1, starting transfers between devices: none -> 1.91 us  [on_device(): f_other = lax.ppermute(f_rows, 'core', [(0, 1), (1, 0)])]
    all_to_all x2, waiting for transfers between devices: 13.2 us -> 15.1 us  [gather_by_a2a(): return lax.all_to_all(copies, axis, 0, 0, tiled=True)]
    all_to_all x1, waiting for transfers between devices: 8.53 us -> 9.98 us  [on_device(): lax.all_to_all(pieces.astype(jnp.bfloat16), 'series', 0, 0, tiled=True)]
    all_to_all x1, starting transfers between devices: 7.24 us -> 5.79 us  [on_device(): by_row = lax.all_to_all(by_core.astype(jnp.bfloat16), ROW, 0, 0, tiled=True)]
    convert_element_type x1, other arithmetic: 2 us -> 0.96 us  [on_device(): by_row = lax.all_to_all(by_core.astype(jnp.bfloat16), ROW, 0, 0, tiled=True)]
  transfers between devices with their start and end apart: 6 -> 7, of which waited for: 4 -> 4; matrix products, arithmetic and copies ran while one was open for 11% -> 12% of each run, Pallas kernels for 0% -> 0%
where the time goes in v9:
time: 98.7 us; the launch traced here: 97.9 us
  waiting for transfers between devices  38.6 us (39%)
  starting transfers between devices  36.1 us (37%)
  matrix products  9 us (9%)
  between operations  6.17 us (6%)
  local copies, waits for them, and re-layouts  4.1 us (4%)
  other arithmetic  3.97 us (4%)
    all_to_all x2, starting transfers between devices, gather_by_a2a(): return lax.all_to_all(copies, axis, 0, 0, tiled=True)  20.7 us
    all_to_all x2, waiting for transfers between devices, gather_by_a2a(): return lax.all_to_all(copies, axis, 0, 0, tiled=True)  15.1 us
    all_to_all x1, waiting for transfers between devices, on_device(): by_row = lax.all_to_all(by_core.astype(jnp.bfloat16), ROW, 0, 0, tiled=True)  13.5 us
    all_to_all x1, waiting for transfers between devices, on_device(): lax.all_to_all(pieces.astype(jnp.bfloat16), 'series', 0, 0, tiled=True)  9.98 us
    all_to_all x1, starting transfers between devices, on_device(): by_row = lax.all_to_all(by_core.astype(jnp.bfloat16), ROW, 0, 0, tiled=True)  5.79 us
    all_to_all x1, starting transfers between devices, on_device(): lax.all_to_all(pieces.astype(jnp.bfloat16), 'series', 0, 0, tiled=True)  3.37 us
    dot_general x2, matrix products, half(): jnp.dot(f2, x_full, preferred_element_type=jnp.float32)  3.15 us
    ppermute x1, starting transfers between devices, on_device(): lax.ppermute(given.astype(jnp.bfloat16), 'core', [(0, 1), (1, 0)])  2.4 us
  transfers between devices with their start and end apart: 7, of which 4 were waited for; matrix products, arithmetic and copies ran while one was open for 12% of the time, Pallas kernels for 0%

profile of v9, /device:TPU:8, one launch (start us, length us, event | category | flops | bytes accessed | tf_op | source)
XLA Modules:
  0.0 97.9 jit_solution(2619672621450948621)
XLA Ops:
  0.7 0.8 convert_element_type.81
  1.5 0.7 broadcast_in_dim.43
  2.1 8.7 %all-to-all-start.1 = ((bf16[8,16,512]{2,1,0:T(8,128)(2,1)}), bf16[8,16,512]{2,1,0:T(8,128)(2,1)S(1)}, u32[]{:S(2)}, u32[]{:S(2)}) async-start(bf16[8,16,512]{2,1,0:T(8,128)(2,1)} %broadcast_in_dim.43), calls=%async_computation.1 | async-start | bytes 262144 | tf_op jit(solution)/shard_map/all_to_all | solution.py:45
  10.8 1.4 %fusion.67 = (s32[1]{0:T(128)}, s32[1]{0:T(128)}, s32[1]{0:T(128)}, s32[1]{0:T(128)}) fusion(s32[4]{0:T(128)} %param.15), kind=kLoop, calls=%fused_computation.97 | loop fusion | bytes 32 | tf_op jit(solution)/shard_map/slice | solution.py:103
  12.2 0.8 convert_element_type.80
  13.0 0.8 slice_bitcast_fusion
  13.8 8.1 %all-to-all-done.1 = bf16[8,16,512]{2,1,0:T(8,128)(2,1)S(1)} async-done(((bf16[8,16,512]{2,1,0:T(8,128)(2,1)}), bf16[8,16,512]{2,1,0:T(8,128)(2,1)S(1)}, u32[]{:S(2)}, u32[]{:S(2)}) %all-to-all-start.1) | async-done | bytes 131104 | tf_op jit(solution)/shard_map/all_to_all | solution.py:45
  21.9 0.9 broadcast_in_dim.42
  22.9 12.0 %all-to-all-start = ((bf16[32,64,128]{2,1,0:T(8,128)(2,1)}), bf16[32,64,128]{2,1,0:T(8,128)(2,1)S(1)}, u32[]{:S(2)}, u32[]{:S(2)}) async-start(bf16[32,64,128]{2,1,0:T(8,128)(2,1)} %broadcast_in_dim.42), calls=%async_computation | async-start | bytes 1048576 | tf_op jit(solution)/shard_map/all_to_all | solution.py:45
  34.9 1.9 %collective-permute-start.2 = (bf16[128,128]{1,0:T(8,128)(2,1)S(1)}, bf16[128,128]{1,0:T(8,128)(2,1)S(1)}, u32[]{:S(2)}, u32[]{:S(2)}) collective-permute-start(bf16[128,128]{1,0:T(8,128)(2,1)S(1)} %slice.92), channel_id=1, source_target_pairs={{0,1},{1,2},{2,3},{3,4},{4,5},{5,6},{6,7},{7,8},{8,9},{9,10},{10,1... | collective-permute-start | bytes 98312 | tf_op jit(solution)/shard_map/ppermute | solution.py:95
  43.7 6.9 %all-to-all-done = bf16[32,64,128]{2,1,0:T(8,128)(2,1)S(1)} async-done(((bf16[32,64,128]{2,1,0:T(8,128)(2,1)}), bf16[32,64,128]{2,1,0:T(8,128)(2,1)S(1)}, u32[]{:S(2)}, u32[]{:S(2)}) %all-to-all-start) | async-done | bytes 524320 | tf_op jit(solution)/shard_map/all_to_all | solution.py:45
  50.6 1.9 %collective-permute-start = (bf16[32,64,128]{2,1,0:T(8,128)(2,1)S(1)}, bf16[32,64,128]{2,1,0:T(8,128)(2,1)S(1)}, u32[]{:S(2)}, u32[]{:S(2)}) collective-permute-start(bf16[32,64,128]{2,1,0:T(8,128)(2,1)S(1)} %all-to-all-done), channel_id=1, source_target_pairs={{0,1},{1,0},{2,3},{3,2},{4,5},{5,4},{6,7},{7,6},{8,9},{9,8},{10,11... | collective-permute-start | bytes 1572872 | tf_op jit(solution)/shard_map/ppermute | solution.py:61
  52.6 2.4 %fusion.3 = bf16[32,64,512]{2,1,0:T(8,128)(2,1)S(1)} fusion(bf16[32,64,128]{2,1,0:T(8,128)(2,1)S(1)} %all-to-all-done, bf16[128,512,1]{1,0,2:T(8,128)(2,1)S(1)} %bitcast.114, bf16[32,2,64,512]{3,2,1,0:T(8,128)(2,1)} %bitcast.118, s32[]{:T(128)S(6)} %select_n.35, f32[32,512]{1,0:T(8,128)S(1)} %bitcast.122), kind=kOutput, calls=%fused_computation.5 | convolution fusion | flops 272629760 | bytes 4915204 | tf_op jit(solution)/shard_map/dot_general | solution.py:75
  55.0 0.7 fusion.5
  55.7 0.7 fusion.1
  56.5 1.5 %fusion.6 = bf16[2048,128]{1,0:T(8,128)(2,1)} fusion(bf16[2048,512]{1,0:T(8,128)(2,1)S(1)} %bitcast.121, bf16[128,512]{1,0:T(8,128)(2,1)S(1)} %bitcast.117), kind=kOutput, calls=%fused_computation.10 | convolution fusion | flops 269221888 | bytes 2752512 | tf_op jit(solution)/shard_map/dot_general | solution.py:78
  58.0 2.4 %collective-permute-start.1 = (bf16[32,64,128]{2,1,0:T(8,128)(2,1)}, bf16[32,64,128]{2,1,0:T(8,128)(2,1)S(1)}, u32[]{:S(2)}, u32[]{:S(2)}) collective-permute-start(bf16[32,64,128]{2,1,0:T(8,128)(2,1)} %bitcast.9), channel_id=1, source_target_pairs={{0,1},{1,0},{2,3},{3,2},{4,5},{5,4},{6,7},{7,6},{8,9},{9,8},{10,11... | collective-permute-start | bytes 1572872 | tf_op jit(solution)/shard_map/ppermute | solution.py:84
  60.9 1.1 %fusion.25 = bf16[512,128]{0,1:T(8,128)(2,1)} fusion(f32[512,128]{0,1:T(8,128)S(1)} %convolution_bitcast_fusion.1, bf16[32,64,512]{2,1,0:T(8,128)(2,1)S(1)} %fusion.1, bf16[32,64,128]{2,1,0:T(8,128)(2,1)S(1)} %collective-permute-done), kind=kOutput, calls=%fused_computation.35 | convolution fusion | flops 268697600 | bytes 3014656 | tf_op jit(solution)/shard_map/dot_general | solution.py:79
  62.0 3.4 %all-to-all-start.3 = ((bf16[8,16,512]{2,1,0:T(8,128)(2,1)}), bf16[8,16,512]{2,1,0:T(8,128)(2,1)S(1)}, u32[]{:S(2)}, u32[]{:S(2)}) async-start(bf16[8,16,512]{2,1,0:T(8,128)(2,1)} %bitcast.13), calls=%async_computation.3 | async-start | bytes 262144 | tf_op jit(solution)/shard_map/all_to_all | solution.py:91
  65.4 1.0 add_convert_fusion
  66.4 10.0 %all-to-all-done.3 = bf16[8,16,512]{2,1,0:T(8,128)(2,1)S(1)} async-done(((bf16[8,16,512]{2,1,0:T(8,128)(2,1)}), bf16[8,16,512]{2,1,0:T(8,128)(2,1)S(1)}, u32[]{:S(2)}, u32[]{:S(2)}) %all-to-all-start.3) | async-done | bytes 131104 | tf_op jit(solution)/shard_map/all_to_all | solution.py:91
  76.4 5.8 %all-to-all-start.2 = ((bf16[32,64,128]{2,1,0:T(8,128)(2,1)}), bf16[32,64,128]{2,1,0:T(8,128)(2,1)S(1)}, u32[]{:S(2)}, u32[]{:S(2)}) async-start(bf16[32,64,128]{2,1,0:T(8,128)(2,1)} %add_convert_fusion), calls=%async_computation.2 | async-start | bytes 1048576 | tf_op jit(solution)/shard_map/all_to_all | solution.py:85
  83.7 13.5 %all-to-all-done.2 = bf16[32,64,128]{2,1,0:T(8,128)(2,1)S(1)} async-done(((bf16[32,64,128]{2,1,0:T(8,128)(2,1)}), bf16[32,64,128]{2,1,0:T(8,128)(2,1)S(1)}, u32[]{:S(2)}, u32[]{:S(2)}) %all-to-all-start.2) | async-done | bytes 524320 | tf_op jit(solution)/shard_map/all_to_all | solution.py:85
  97.2 0.7 divide_subtract_fusion
  (38 shorter events, 3.5 us)
Async XLA Ops:
  0.6 41.4 %copy-start.6 = (s32[32,4]{0,1:T(4,128)S(1)}, s32[32,4]{0,1:T(4,128)}, u32[]{:S(2)}) copy-start(s32[32,4]{0,1:T(4,128)} %param.10) | copy-start | bytes 1540
  0.6 41.7 %copy-start.1 = (bf16[4,2,128,128]{3,2,1,0:T(8,128)(2,1)S(1)}, bf16[4,2,128,128]{3,2,1,0:T(8,128)(2,1)}, u32[]{:S(2)}) copy-start(bf16[4,2,128,128]{3,2,1,0:T(8,128)(2,1)} %param.16) | copy-start | bytes 786436
  2.1 19.8 %all-to-all-start.1 = ((bf16[8,16,512]{2,1,0:T(8,128)(2,1)}), bf16[8,16,512]{2,1,0:T(8,128)(2,1)S(1)}, u32[]{:S(2)}, u32[]{:S(2)}) async-start(bf16[8,16,512]{2,1,0:T(8,128)(2,1)} %broadcast_in_dim.43), calls=%async_computation.1 | async-start | bytes 262144 | tf_op jit(solution)/shard_map/all_to_all | solution.py:45
  22.9 27.8 %all-to-all-start = ((bf16[32,64,128]{2,1,0:T(8,128)(2,1)}), bf16[32,64,128]{2,1,0:T(8,128)(2,1)S(1)}, u32[]{:S(2)}, u32[]{:S(2)}) async-start(bf16[32,64,128]{2,1,0:T(8,128)(2,1)} %broadcast_in_dim.42), calls=%async_computation | async-start | bytes 1048576 | tf_op jit(solution)/shard_map/all_to_all | solution.py:45
  34.9 7.4 %collective-permute-start.2 = (bf16[128,128]{1,0:T(8,128)(2,1)S(1)}, bf16[128,128]{1,0:T(8,128)(2,1)S(1)}, u32[]{:S(2)}, u32[]{:S(2)}) collective-permute-start(bf16[128,128]{1,0:T(8,128)(2,1)S(1)} %slice.92), channel_id=1, source_target_pairs={{0,1},{1,2},{2,3},{3,4},{4,5},{5,6},{6,7},{7,8},{8,9},{9,10},{10,1... | collective-permute-start | bytes 98312 | tf_op jit(solution)/shard_map/ppermute | solution.py:95
  50.6 5.1 %collective-permute-start = (bf16[32,64,128]{2,1,0:T(8,128)(2,1)S(1)}, bf16[32,64,128]{2,1,0:T(8,128)(2,1)S(1)}, u32[]{:S(2)}, u32[]{:S(2)}) collective-permute-start(bf16[32,64,128]{2,1,0:T(8,128)(2,1)S(1)} %all-to-all-done), channel_id=1, source_target_pairs={{0,1},{1,0},{2,3},{3,2},{4,5},{5,4},{6,7},{7,6},{8,9},{9,8},{10,11... | collective-permute-start | bytes 1572872 | tf_op jit(solution)/shard_map/ppermute | solution.py:61
  52.6 3.2 %copy-start = (bf16[4096,512]{1,0:T(8,128)(2,1)S(1)}, bf16[4096,512]{1,0:T(8,128)(2,1)}, u32[]{:S(2)}) copy-start(bf16[4096,512]{1,0:T(8,128)(2,1)} %param.9) | copy-start | bytes 12582916
  58.0 7.4 %collective-permute-start.1 = (bf16[32,64,128]{2,1,0:T(8,128)(2,1)}, bf16[32,64,128]{2,1,0:T(8,128)(2,1)S(1)}, u32[]{:S(2)}, u32[]{:S(2)}) collective-permute-start(bf16[32,64,128]{2,1,0:T(8,128)(2,1)} %bitcast.9), channel_id=1, source_target_pairs={{0,1},{1,0},{2,3},{3,2},{4,5},{5,4},{6,7},{7,6},{8,9},{9,8},{10,11... | collective-permute-start | bytes 1572872 | tf_op jit(solution)/shard_map/ppermute | solution.py:84
  62.0 14.3 %all-to-all-start.3 = ((bf16[8,16,512]{2,1,0:T(8,128)(2,1)}), bf16[8,16,512]{2,1,0:T(8,128)(2,1)S(1)}, u32[]{:S(2)}, u32[]{:S(2)}) async-start(bf16[8,16,512]{2,1,0:T(8,128)(2,1)} %bitcast.13), calls=%async_computation.3 | async-start | bytes 262144 | tf_op jit(solution)/shard_map/all_to_all | solution.py:91
  76.4 20.8 %all-to-all-start.2 = ((bf16[32,64,128]{2,1,0:T(8,128)(2,1)}), bf16[32,64,128]{2,1,0:T(8,128)(2,1)S(1)}, u32[]{:S(2)}, u32[]{:S(2)}) async-start(bf16[32,64,128]{2,1,0:T(8,128)(2,1)} %add_convert_fusion), calls=%async_computation.2 | async-start | bytes 1048576 | tf_op jit(solution)/shard_map/all_to_all | solution.py:85
  82.2 0.8 copy-start.2
  82.2 15.0 %copy-start.3 = (f32[64,128]{1,0:T(8,128)S(1)}, f32[64,128]{1,0:T(8,128)}, u32[]{:S(2)}) copy-start(f32[64,128]{1,0:T(8,128)} %param.11) | copy-start | bytes 98308
  82.2 15.0 %copy-start.4 = (f32[64,128]{1,0:T(8,128)S(1)}, f32[64,128]{1,0:T(8,128)}, u32[]{:S(2)}) copy-start(f32[64,128]{1,0:T(8,128)} %param.12) | copy-start | bytes 98308
  82.2 15.0 %copy-start.5 = (f32[64,128]{1,0:T(8,128)S(1)}, f32[64,128]{1,0:T(8,128)}, u32[]{:S(2)}) copy-start(f32[64,128]{1,0:T(8,128)} %param.13) | copy-start | bytes 98308

commit v10 on v9

--- a/solution.py
+++ b/solution.py
@@ -83,12 +83,13 @@
     given, x_theirs = half(f_other, 1 - core)
     by_core = kept + lax.ppermute(given.astype(jnp.bfloat16), "core", [(0, 1), (1, 0)]).astype(jnp.float32)
     by_row = lax.all_to_all(by_core.astype(jnp.bfloat16), ROW, 0, 0, tiled=True)
-    grad_f = by_row.astype(jnp.float32).sum(0)
-    factors_new, m_new, v_new = adam_update(factors, adam_m, adam_v, grad_f)
 
     partial_x = -(x_mine + x_theirs) * math.sqrt(K / total_series)
     pieces = partial_x.reshape(n_series, rank_part, width)
-    arrived = lax.all_to_all(pieces.astype(jnp.bfloat16), "series", 0, 0, tiled=True)
+    by_row, sent_x = lax.optimization_barrier((by_row, pieces.astype(jnp.bfloat16)))
+    arrived = lax.all_to_all(sent_x, "series", 0, 0, tiled=True)
+    grad_f = by_row.astype(jnp.float32).sum(0)
+    factors_new, m_new, v_new = adam_update(factors, adam_m, adam_v, grad_f)
     grad_x = arrived.astype(jnp.float32).sum(0)
 
     xb = x_full

time: 98.7 us -> 101 us (1.023)
  transfers between devices with their start and end apart: 7 -> 7, of which waited for: 4 -> 6; matrix products, arithmetic and copies ran while one was open for 12% -> 11% of each run, Pallas kernels for 0% -> 0%
where the time goes in v10:
time: 101 us; the launch traced here: 100 us
  waiting for transfers between devices  39.4 us (39%)
  starting transfers between devices  35.2 us (35%)
  matrix products  9.95 us (10%)
  between operations  6.18 us (6%)
  local copies, waits for them, and re-layouts  4.82 us (5%)
  other arithmetic  4.72 us (5%)
    all_to_all x2, starting transfers between devices, gather_by_a2a(): return lax.all_to_all(copies, axis, 0, 0, tiled=True)  20.7 us
    all_to_all x2, waiting for transfers between devices, gather_by_a2a(): return lax.all_to_all(copies, axis, 0, 0, tiled=True)  15.6 us
    all_to_all x1, waiting for transfers between devices, on_device(): by_row = lax.all_to_all(by_core.astype(jnp.bfloat16), ROW, 0, 0, tiled=True)  13.1 us
    all_to_all x1, waiting for transfers between devices, on_device(): arrived = lax.all_to_all(sent_x, 'series', 0, 0, tiled=True)  9.98 us
    all_to_all x1, starting transfers between devices, on_device(): by_row = lax.all_to_all(by_core.astype(jnp.bfloat16), ROW, 0, 0, tiled=True)  5.19 us
    all_to_all x1, starting transfers between devices, on_device(): arrived = lax.all_to_all(sent_x, 'series', 0, 0, tiled=True)  3.38 us
    dot_general x2, matrix products, half(): jnp.dot(f2, x_full, preferred_element_type=jnp.float32)  3.23 us
    ppermute x1, starting transfers between devices, on_device(): lax.ppermute(given.astype(jnp.bfloat16), 'core', [(0, 1), (1, 0)])  2.04 us
  transfers between devices with their start and end apart: 7, of which 6 were waited for; matrix products, arithmetic and copies ran while one was open for 11% of the time, Pallas kernels for 0%

profile of v10, /device:TPU:8, one launch (start us, length us, event | category | flops | bytes accessed | tf_op | source)
XLA Modules:
  0.0 100.2 jit_solution(3579647470247008237)
XLA Ops:
  0.7 0.8 convert_element_type.81
  2.1 8.7 %all-to-all-start.1 = ((bf16[8,16,512]{2,1,0:T(8,128)(2,1)}), bf16[8,16,512]{2,1,0:T(8,128)(2,1)S(1)}, u32[]{:S(2)}, u32[]{:S(2)}) async-start(bf16[8,16,512]{2,1,0:T(8,128)(2,1)} %broadcast_in_dim.43), calls=%async_computation.1 | async-start | bytes 262144 | tf_op jit(solution)/shard_map/all_to_all | solution.py:45
  10.8 1.4 %fusion.67 = (s32[1]{0:T(128)}, s32[1]{0:T(128)}, s32[1]{0:T(128)}, s32[1]{0:T(128)}) fusion(s32[4]{0:T(128)} %param.15), kind=kLoop, calls=%fused_computation.97 | loop fusion | bytes 32 | tf_op jit(solution)/shard_map/slice | solution.py:104
  12.2 0.8 convert_element_type.80
  12.9 0.8 slice_bitcast_fusion
  13.8 8.1 %all-to-all-done.1 = bf16[8,16,512]{2,1,0:T(8,128)(2,1)S(1)} async-done(((bf16[8,16,512]{2,1,0:T(8,128)(2,1)}), bf16[8,16,512]{2,1,0:T(8,128)(2,1)S(1)}, u32[]{:S(2)}, u32[]{:S(2)}) %all-to-all-start.1) | async-done | bytes 131104 | tf_op jit(solution)/shard_map/all_to_all | solution.py:45
  21.9 0.9 broadcast_in_dim.42
  22.8 12.0 %all-to-all-start = ((bf16[32,64,128]{2,1,0:T(8,128)(2,1)}), bf16[32,64,128]{2,1,0:T(8,128)(2,1)S(1)}, u32[]{:S(2)}, u32[]{:S(2)}) async-start(bf16[32,64,128]{2,1,0:T(8,128)(2,1)} %broadcast_in_dim.42), calls=%async_computation | async-start | bytes 1048576 | tf_op jit(solution)/shard_map/all_to_all | solution.py:45
  34.9 1.9 %collective-permute-start.2 = (bf16[128,128]{1,0:T(8,128)(2,1)S(1)}, bf16[128,128]{1,0:T(8,128)(2,1)S(1)}, u32[]{:S(2)}, u32[]{:S(2)}) collective-permute-start(bf16[128,128]{1,0:T(8,128)(2,1)S(1)} %slice.92), channel_id=1, source_target_pairs={{0,1},{1,2},{2,3},{3,4},{4,5},{5,6},{6,7},{7,8},{8,9},{9,10},{10,1... | collective-permute-start | bytes 98312 | tf_op jit(solution)/shard_map/ppermute | solution.py:96
  43.2 7.5 %all-to-all-done = bf16[32,64,128]{2,1,0:T(8,128)(2,1)S(1)} async-done(((bf16[32,64,128]{2,1,0:T(8,128)(2,1)}), bf16[32,64,128]{2,1,0:T(8,128)(2,1)S(1)}, u32[]{:S(2)}, u32[]{:S(2)}) %all-to-all-start) | async-done | bytes 524320 | tf_op jit(solution)/shard_map/all_to_all | solution.py:45
  50.6 1.9 %collective-permute-start = (bf16[32,64,128]{2,1,0:T(8,128)(2,1)S(1)}, bf16[32,64,128]{2,1,0:T(8,128)(2,1)S(1)}, u32[]{:S(2)}, u32[]{:S(2)}) collective-permute-start(bf16[32,64,128]{2,1,0:T(8,128)(2,1)S(1)} %all-to-all-done), channel_id=1, source_target_pairs={{0,1},{1,0},{2,3},{3,2},{4,5},{5,4},{6,7},{7,6},{8,9},{9,8},{10,11... | collective-permute-start | bytes 1572872 | tf_op jit(solution)/shard_map/ppermute | solution.py:61
  53.3 0.7 slice.93
  54.4 2.5 %fusion.1 = bf16[32,64,512]{2,1,0:T(8,128)(2,1)S(1)} fusion(bf16[32,64,128]{2,1,0:T(8,128)(2,1)S(1)} %collective-permute-done, bf16[128,512,1]{1,0,2:T(8,128)(2,1)S(1)} %bitcast.114, bf16[32,2,64,512]{3,2,1,0:T(8,128)(2,1)} %bitcast.118, s32[]{:T(128)S(6)} %select_n.36, f32[32,512]{1,0:T(8,128)S(1)} %bitcast.122), kind=kOutput, calls=%fused_computation.2 | convolution fusion | flops 272629760 | bytes 4915204 | tf_op jit(solution)/shard_map/dot_general | solution.py:75
  57.0 0.7 fusion.6
  57.7 2.0 %collective-permute-start.1 = (bf16[32,64,128]{2,1,0:T(8,128)(2,1)S(1)}, bf16[32,64,128]{2,1,0:T(8,128)(2,1)S(1)}, u32[]{:S(2)}, u32[]{:S(2)}) collective-permute-start(bf16[32,64,128]{2,1,0:T(8,128)(2,1)S(1)} %bitcast.125), channel_id=1, source_target_pairs={{0,1},{1,0},{2,3},{3,2},{4,5},{5,4},{6,7},{7,6},{8,9},{9,8},{10,11... | collective-permute-start | bytes 1572872 | tf_op jit(solution)/shard_map/ppermute | solution.py:84
  61.5 1.0 add_convert_fusion
  62.4 5.2 %all-to-all-start.2 = ((bf16[32,64,128]{2,1,0:T(8,128)(2,1)}), bf16[32,64,128]{2,1,0:T(8,128)(2,1)S(1)}, u32[]{:S(2)}, u32[]{:S(2)}) async-start(bf16[32,64,128]{2,1,0:T(8,128)(2,1)} %add_convert_fusion), calls=%async_computation.2 | async-start | bytes 1048576 | tf_op jit(solution)/shard_map/all_to_all | solution.py:85
  67.6 1.0 %fusion.30 = f32[640,128]{0,1:T(8,128)S(1)} fusion(s32[]{:T(128)S(6)} %select_n.44, bf16[128,640]{1,0:T(8,128)(2,1)S(1)} %get-tuple-element.23, bf16[4,2,128,128]{3,2,1,0:T(8,128)(2,1)} %param.16), kind=kOutput, calls=%fused_computation.51 | convolution fusion | flops 20971520 | bytes 524292 | tf_op jit(solution)/shard_map/dot_general | solution.py:37
  68.7 1.1 %fusion.18 = f32[128,640]{1,0:T(8,128)S(1)} fusion(f32[640,128]{0,1:T(8,128)S(1)} %fusion.30, bf16[128,640]{1,0:T(8,128)(2,1)S(1)} %get-tuple-element.23, f32[128]{0:T(128)S(1)} %get-tuple-element.11, bf16[4,2,128,128]{3,2,1,0:T(8,128)(2,1)} %param.16), kind=kOutput, calls=%fused_computation.26 | convolution fusion | flops 21217280 | bytes 852480 | tf_op jit(solution)/shard_map/dot_general | solution.py:38
  70.4 1.2 %fusion.25 = bf16[512,128]{0,1:T(8,128)(2,1)} fusion(f32[512,128]{0,1:T(8,128)S(1)} %convolution_bitcast_fusion.1, bf16[32,64,512]{2,1,0:T(8,128)(2,1)S(1)} %copy-done.2, bf16[32,64,128]{2,1,0:T(8,128)(2,1)S(1)} %copy-done.4), kind=kOutput, calls=%fused_computation.35 | convolution fusion | flops 268697600 | bytes 3014656 | tf_op jit(solution)/shard_map/dot_general | solution.py:79
  71.6 13.1 %all-to-all-done.2 = bf16[32,64,128]{2,1,0:T(8,128)(2,1)S(1)} async-done(((bf16[32,64,128]{2,1,0:T(8,128)(2,1)}), bf16[32,64,128]{2,1,0:T(8,128)(2,1)S(1)}, u32[]{:S(2)}, u32[]{:S(2)}) %all-to-all-start.2) | async-done | bytes 524320 | tf_op jit(solution)/shard_map/all_to_all | solution.py:85
  84.8 3.4 %all-to-all-start.3 = ((bf16[8,16,512]{2,1,0:T(8,128)(2,1)}), bf16[8,16,512]{2,1,0:T(8,128)(2,1)S(1)}, u32[]{:S(2)}, u32[]{:S(2)}) async-start(bf16[8,16,512]{2,1,0:T(8,128)(2,1)} %bitcast.13), calls=%async_computation.3 | async-start | bytes 262144 | tf_op jit(solution)/shard_map/all_to_all | solution.py:90
  88.8 10.0 %all-to-all-done.3 = bf16[8,16,512]{2,1,0:T(8,128)(2,1)S(1)} async-done(((bf16[8,16,512]{2,1,0:T(8,128)(2,1)}), bf16[8,16,512]{2,1,0:T(8,128)(2,1)S(1)}, u32[]{:S(2)}, u32[]{:S(2)}) %all-to-all-start.3) | async-done | bytes 131104 | tf_op jit(solution)/shard_map/all_to_all | solution.py:90
  98.9 1.4 %fusion.35 = f32[16,512]{1,0:T(8,128)} fusion(f32[16,512]{1,0:T(8,128)S(1)} %copy-done.7, f32[16,512]{1,0:T(8,128)S(1)} %convert_reduce_fusion.1, f32[128,512]{1,0:T(8,128)S(1)} %slice.94, s32[]{:T(128)S(6)} %select_n.45, f32[128,512]{1,0:T(8,128)} %slice.93), kind=kLoop, calls=%fused_computation.60 | loop fusion | flops 40960 | bytes 163844 | tf_op jit(solution)/shard_map/sub | solution.py:107
  (46 shorter events, 5.9 us)
Async XLA Ops:
  0.6 41.4 %copy-start.10 = (s32[32,4]{0,1:T(4,128)S(1)}, s32[32,4]{0,1:T(4,128)}, u32[]{:S(2)}) copy-start(s32[32,4]{0,1:T(4,128)} %param.10) | copy-start | bytes 1540
  0.6 41.7 %copy-start.5 = (bf16[4,2,128,128]{3,2,1,0:T(8,128)(2,1)S(1)}, bf16[4,2,128,128]{3,2,1,0:T(8,128)(2,1)}, u32[]{:S(2)}) copy-start(bf16[4,2,128,128]{3,2,1,0:T(8,128)(2,1)} %param.16) | copy-start | bytes 786436
  2.1 19.8 %all-to-all-start.1 = ((bf16[8,16,512]{2,1,0:T(8,128)(2,1)}), bf16[8,16,512]{2,1,0:T(8,128)(2,1)S(1)}, u32[]{:S(2)}, u32[]{:S(2)}) async-start(bf16[8,16,512]{2,1,0:T(8,128)(2,1)} %broadcast_in_dim.43), calls=%async_computation.1 | async-start | bytes 262144 | tf_op jit(solution)/shard_map/all_to_all | solution.py:45
  22.8 27.8 %all-to-all-start = ((bf16[32,64,128]{2,1,0:T(8,128)(2,1)}), bf16[32,64,128]{2,1,0:T(8,128)(2,1)S(1)}, u32[]{:S(2)}, u32[]{:S(2)}) async-start(bf16[32,64,128]{2,1,0:T(8,128)(2,1)} %broadcast_in_dim.42), calls=%async_computation | async-start | bytes 1048576 | tf_op jit(solution)/shard_map/all_to_all | solution.py:45
  34.9 7.4 %collective-permute-start.2 = (bf16[128,128]{1,0:T(8,128)(2,1)S(1)}, bf16[128,128]{1,0:T(8,128)(2,1)S(1)}, u32[]{:S(2)}, u32[]{:S(2)}) collective-permute-start(bf16[128,128]{1,0:T(8,128)(2,1)S(1)} %slice.92), channel_id=1, source_target_pairs={{0,1},{1,2},{2,3},{3,4},{4,5},{5,6},{6,7},{7,8},{8,9},{9,10},{10,1... | collective-permute-start | bytes 98312 | tf_op jit(solution)/shard_map/ppermute | solution.py:96
  50.6 3.8 %collective-permute-start = (bf16[32,64,128]{2,1,0:T(8,128)(2,1)S(1)}, bf16[32,64,128]{2,1,0:T(8,128)(2,1)S(1)}, u32[]{:S(2)}, u32[]{:S(2)}) collective-permute-start(bf16[32,64,128]{2,1,0:T(8,128)(2,1)S(1)} %all-to-all-done), channel_id=1, source_target_pairs={{0,1},{1,0},{2,3},{3,2},{4,5},{5,4},{6,7},{7,6},{8,9},{9,8},{10,11... | collective-permute-start | bytes 1572872 | tf_op jit(solution)/shard_map/ppermute | solution.py:61
  54.4 2.5 %copy-start.3 = (bf16[32,64,128]{2,1,0:T(8,128)(2,1)}, bf16[32,64,128]{2,1,0:T(8,128)(2,1)S(1)}, u32[]{:S(2)}) copy-start(bf16[32,64,128]{2,1,0:T(8,128)(2,1)S(1)} %collective-permute-done) | copy-start | bytes 1572868
  54.4 5.3 %copy-start = (bf16[4096,512]{1,0:T(8,128)(2,1)S(1)}, bf16[4096,512]{1,0:T(8,128)(2,1)}, u32[]{:S(2)}) copy-start(bf16[4096,512]{1,0:T(8,128)(2,1)} %param.9) | copy-start | bytes 12582916
  57.0 3.5 %copy-start.1 = (bf16[32,64,512]{2,1,0:T(8,128)(2,1)}, bf16[32,64,512]{2,1,0:T(8,128)(2,1)S(1)}, u32[]{:S(2)}) copy-start(bf16[32,64,512]{2,1,0:T(8,128)(2,1)S(1)} %fusion.1) | copy-start | bytes 6291460
  57.7 3.8 %collective-permute-start.1 = (bf16[32,64,128]{2,1,0:T(8,128)(2,1)S(1)}, bf16[32,64,128]{2,1,0:T(8,128)(2,1)S(1)}, u32[]{:S(2)}, u32[]{:S(2)}) collective-permute-start(bf16[32,64,128]{2,1,0:T(8,128)(2,1)S(1)} %bitcast.125), channel_id=1, source_target_pairs={{0,1},{1,0},{2,3},{3,2},{4,5},{5,4},{6,7},{7,6},{8,9},{9,8},{10,11... | collective-permute-start | bytes 1572872 | tf_op jit(solution)/shard_map/ppermute | solution.py:84
  62.4 22.2 %all-to-all-start.2 = ((bf16[32,64,128]{2,1,0:T(8,128)(2,1)}), bf16[32,64,128]{2,1,0:T(8,128)(2,1)S(1)}, u32[]{:S(2)}, u32[]{:S(2)}) async-start(bf16[32,64,128]{2,1,0:T(8,128)(2,1)} %add_convert_fusion), calls=%async_computation.2 | async-start | bytes 1048576 | tf_op jit(solution)/shard_map/all_to_all | solution.py:85
  68.7 1.7 %copy-start.2 = (bf16[32,64,512]{2,1,0:T(8,128)(2,1)S(1)}, bf16[32,64,512]{2,1,0:T(8,128)(2,1)}, u32[]{:S(2)}) copy-start(bf16[32,64,512]{2,1,0:T(8,128)(2,1)} %copy-done.1) | copy-start | bytes 6291460
  68.7 1.7 %copy-start.4 = (bf16[32,64,128]{2,1,0:T(8,128)(2,1)S(1)}, bf16[32,64,128]{2,1,0:T(8,128)(2,1)}, u32[]{:S(2)}) copy-start(bf16[32,64,128]{2,1,0:T(8,128)(2,1)} %copy-done.3) | copy-start | bytes 1572868
  70.4 17.8 %copy-start.6 = (f32[64,128]{1,0:T(8,128)S(1)}, f32[64,128]{1,0:T(8,128)}, u32[]{:S(2)}) copy-start(f32[64,128]{1,0:T(8,128)} %param.11) | copy-start | bytes 98308
  70.4 17.8 %copy-start.8 = (f32[64,128]{1,0:T(8,128)S(1)}, f32[64,128]{1,0:T(8,128)}, u32[]{:S(2)}) copy-start(f32[64,128]{1,0:T(8,128)} %param.12) | copy-start | bytes 98308
  70.4 17.8 %copy-start.9 = (f32[64,128]{1,0:T(8,128)S(1)}, f32[64,128]{1,0:T(8,128)}, u32[]{:S(2)}) copy-start(f32[64,128]{1,0:T(8,128)} %param.13) | copy-start | bytes 98308
  70.4 28.5 %copy-start.7 = (f32[16,512]{1,0:T(8,128)S(1)}, f32[16,512]{1,0:T(8,128)}, u32[]{:S(2)}) copy-start(f32[16,512]{1,0:T(8,128)} %param.14) | copy-start | bytes 98308
  84.8 14.1 %all-to-all-start.3 = ((bf16[8,16,512]{2,1,0:T(8,128)(2,1)}), bf16[8,16,512]{2,1,0:T(8,128)(2,1)S(1)}, u32[]{:S(2)}, u32[]{:S(2)}) async-start(bf16[8,16,512]{2,1,0:T(8,128)(2,1)} %bitcast.13), calls=%async_computation.3 | async-start | bytes 262144 | tf_op jit(solution)/shard_map/all_to_all | solution.py:90

commit v11 on v9

--- a/solution.py
+++ b/solution.py
@@ -45,6 +45,18 @@
     return lax.all_to_all(copies, axis, 0, 0, tiled=True)
 
 
+def gather_by_doubling(x, axis, count):
+    me = lax.axis_index(axis)
+    held = x
+    step = 1
+    while step < count:
+        came = lax.ppermute(held, axis, [(i, i ^ step) for i in range(count)])
+        low = (me // step) % 2 == 0
+        held = jnp.where(low, jnp.concatenate([held, came]), jnp.concatenate([came, held]))
+        step *= 2
+    return held
+
+
 def on_device(y_obs, tile_mask, factors, adam_m, adam_v, basis, dilations, conv_w, conv_b):
     own_rows = factors.shape[0]
     width = basis.shape[1]
@@ -60,8 +72,7 @@
     core = lax.axis_index("core")
     f_other = lax.ppermute(f_rows, "core", [(0, 1), (1, 0)])
 
-    x_parts = gather_by_a2a(basis.astype(jnp.bfloat16), "series", n_series)
-    x_full = x_parts.reshape(n_series * rank_part, width)
+    x_full = gather_by_doubling(basis.astype(jnp.bfloat16), "series", n_series)
 
     tiles = tile_mask.shape[0]
     mask_cols = jnp.repeat(tile_mask.astype(jnp.float32), TILE, axis=1)

time: 98.7 us -> 136 us (1.38)
  local copies, waits for them, and re-layouts: 4.1 us -> 24.6 us
  starting transfers between devices: 36.1 us -> 51.3 us
  waiting for transfers between devices: 38.6 us -> 32 us
  other arithmetic: 3.97 us -> 9.41 us
  matrix products: 9 us -> 11.7 us
    all_to_all x2 -> x1, waiting for transfers between devices: 15.1 us -> 0.01 us  [gather_by_a2a(): return lax.all_to_all(copies, axis, 0, 0, tiled=True)]
    ppermute x0 -> x3, starting transfers between devices: none -> 13.1 us  [gather_by_doubling(): came = lax.ppermute(held, axis, [(i, i ^ step) for i in range(count)])]
    convert_element_type x0 -> x2, local copies, waits for them, and re-layouts: none -> 10.8 us  [half(): gap = y_half.astype(jnp.float32) - pred]
    mul x0 -> x2, local copies, waits for them, and re-layouts: none -> 7.96 us  [half(): mask_cols[:, None, :] * gap]
    ppermute x0 -> x3, waiting for transfers between devices: none -> 7.09 us  [gather_by_doubling(): came = lax.ppermute(held, axis, [(i, i ^ step) for i in range(count)])]
    all_to_all x2 -> x1, starting transfers between devices: 20.7 us -> 14 us  [gather_by_a2a(): return lax.all_to_all(copies, axis, 0, 0, tiled=True)]
    convert_element_type x1 -> x3, other arithmetic: 0.81 us -> 6.2 us  [the longest x2 5.44 us: half(): gap = y_half.astype(jnp.float32) - pred]
    all_to_all x1, starting transfers between devices: 5.79 us -> 10.2 us  [on_device(): by_row = lax.all_to_all(by_core.astype(jnp.bfloat16), ROW, 0, 0, tiled=True)]
  transfers between devices with their start and end apart: 7 -> 9, of which waited for: 4 -> 4; matrix products, arithmetic and copies ran while one was open for 12% -> 30% of each run, Pallas kernels for 0% -> 0%
where the time goes in v11:
time: 136 us; the launch traced here: 135 us
  starting transfers between devices  51.3 us (38%)
  waiting for transfers between devices  32 us (24%)
  local copies, waits for them, and re-layouts  24.6 us (18%)
  matrix products  11.7 us (9%)
  other arithmetic  9.41 us (7%)
  between operations  6.25 us (5%)
    all_to_all x1, waiting for transfers between devices, on_device(): by_row = lax.all_to_all(by_core.astype(jnp.bfloat16), ROW, 0, 0, tiled=True)  15.3 us
    all_to_all x1, starting transfers between devices, gather_by_a2a(): return lax.all_to_all(copies, axis, 0, 0, tiled=True)  14 us
    ppermute x3, starting transfers between devices, gather_by_doubling(): came = lax.ppermute(held, axis, [(i, i ^ step) for i in range(count)])  13.1 us
    convert_element_type x2, local copies, waits for them, and re-layouts, half(): gap = y_half.astype(jnp.float32) - pred  10.8 us
    all_to_all x1, starting transfers between devices, on_device(): by_row = lax.all_to_all(by_core.astype(jnp.bfloat16), ROW, 0, 0, tiled=True)  10.2 us
    all_to_all x1, waiting for transfers between devices, on_device(): lax.all_to_all(pieces.astype(jnp.bfloat16), 'series', 0, 0, tiled=True)  9.53 us
    mul x2, local copies, waits for them, and re-layouts, half(): mask_cols[:, None, :] * gap  7.96 us
    ppermute x3, waiting for transfers between devices, gather_by_doubling(): came = lax.ppermute(held, axis, [(i, i ^ step) for i in range(count)])  7.09 us
  transfers between devices with their start and end apart: 9, of which 4 were waited for; matrix products, arithmetic and copies ran while one was open for 30% of the time, Pallas kernels for 0%

profile of v11, /device:TPU:8, one launch (start us, length us, event | category | flops | bytes accessed | tf_op | source)
XLA Modules:
  0.0 135.1 jit_solution(9530877795955720060)
XLA Ops:
  1.4 3.4 %collective-permute-start = (bf16[16,512]{1,0:T(8,128)(2,1)S(1)}, bf16[16,512]{1,0:T(8,128)(2,1)S(1)}, u32[]{:S(2)}, u32[]{:S(2)}) collective-permute-start(bf16[16,512]{1,0:T(8,128)(2,1)S(1)} %convert_element_type.74), channel_id=1, source_target_pairs={{0,64},{64,0},{128,192},{192,128},{256,320},{320,256},{384,448},{4... | collective-permute-start | bytes 49160 | tf_op jit(solution)/shard_map/ppermute | solution.py:53
  6.5 14.0 %all-to-all-start = ((bf16[32,64,128]{2,1,0:T(8,128)(2,1)}), bf16[32,64,128]{2,1,0:T(8,128)(2,1)S(1)}, u32[]{:S(2)}, u32[]{:S(2)}) async-start(bf16[32,64,128]{2,1,0:T(8,128)(2,1)} %broadcast_in_dim.36), calls=%async_computation | async-start | bytes 1048576 | tf_op jit(solution)/shard_map/all_to_all | solution.py:45
  20.4 2.5 %constant_dynamic-slice_fusion = (bf16[32,1,64,512]{3,2,1,0:T(8,128)(2,1)S(1)}, bf16[32,1,64,512]{3,2,1,0:T(8,128)(2,1)S(1)}) fusion(bf16[32,2,64,512]{3,2,1,0:T(8,128)(2,1)} %bitcast.108, s32[]{:T(128)S(6)} %select_n.94, s32[]{:T(128)S(6)} %select_n.82), kind=kLoop, calls=%fused_computation.88 | loop fusion | bytes 8388616 | tf_op jit(solution)/shard_map/jit(dynamic_index_in_dim)/dynamic_slice | solution.py:85
  23.0 2.7 %bitcast_convert_fusion = f32[2048,512]{1,0:T(8,128)} fusion(bf16[32,1,64,512]{3,2,1,0:T(8,128)(2,1)S(1)} %get-tuple-element.23), kind=kLoop, calls=%fused_computation.11 | loop fusion | flops 1048576 | bytes 6291456 | tf_op jit(solution)/shard_map/convert_element_type | solution.py:87
  25.7 2.7 %bitcast_convert_fusion.1 = f32[2048,512]{1,0:T(8,128)} fusion(bf16[32,1,64,512]{3,2,1,0:T(8,128)(2,1)S(1)} %get-tuple-element.24), kind=kLoop, calls=%fused_computation.12 | loop fusion | flops 1048576 | bytes 6291456 | tf_op jit(solution)/shard_map/convert_element_type | solution.py:87
  28.4 4.6 %collective-permute-start.1 = (bf16[32,512]{1,0:T(8,128)(2,1)S(1)}, bf16[32,512]{1,0:T(8,128)(2,1)S(1)}, u32[]{:S(2)}, u32[]{:S(2)}) collective-permute-start(bf16[32,512]{1,0:T(8,128)(2,1)S(1)} %maximum_select_fusion.2), channel_id=1, source_target_pairs={{0,128},{64,192},{128,0},{192,64},{256,384},{320,448},{384,256},{4... | collective-permute-start | bytes 98312 | tf_op jit(solution)/shard_map/ppermute | solution.py:53
  33.1 2.6 %collective-permute-done.1 = bf16[32,512]{1,0:T(8,128)(2,1)S(1)} collective-permute-done((bf16[32,512]{1,0:T(8,128)(2,1)S(1)}, bf16[32,512]{1,0:T(8,128)(2,1)S(1)}, u32[]{:S(2)}, u32[]{:S(2)}) %collective-permute-start.1) | collective-permute-done | bytes 32800 | tf_op jit(solution)/shard_map/ppermute | solution.py:53
  35.7 5.0 %collective-permute-start.2 = (bf16[64,512]{1,0:T(8,128)(2,1)S(1)}, bf16[64,512]{1,0:T(8,128)(2,1)S(1)}, u32[]{:S(2)}, u32[]{:S(2)}) collective-permute-start(bf16[64,512]{1,0:T(8,128)(2,1)S(1)} %maximum_select_fusion.1), channel_id=1, source_target_pairs={{0,256},{64,320},{128,384},{192,448},{256,0},{320,64},{384,128},{4... | collective-permute-start | bytes 196616 | tf_op jit(solution)/shard_map/ppermute | solution.py:53
  41.4 4.5 %collective-permute-done.2 = bf16[64,512]{1,0:T(8,128)(2,1)S(1)} collective-permute-done((bf16[64,512]{1,0:T(8,128)(2,1)S(1)}, bf16[64,512]{1,0:T(8,128)(2,1)S(1)}, u32[]{:S(2)}, u32[]{:S(2)}) %collective-permute-start.2) | collective-permute-done | bytes 65568 | tf_op jit(solution)/shard_map/ppermute | solution.py:53
  46.0 1.9 %collective-permute-start.5 = (bf16[128,128]{1,0:T(8,128)(2,1)S(1)}, bf16[128,128]{1,0:T(8,128)(2,1)S(1)}, u32[]{:S(2)}, u32[]{:S(2)}) collective-permute-start(bf16[128,128]{1,0:T(8,128)(2,1)S(1)} %slice.92), channel_id=1, source_target_pairs={{0,1},{1,2},{2,3},{3,4},{4,5},{5,6},{6,7},{7,8},{8,9},{9,10},{10,1... | collective-permute-start | bytes 98312 | tf_op jit(solution)/shard_map/ppermute | solution.py:106
  53.1 5.4 %copy.59 = f32[2048,512]{0,1:T(8,128)} copy(f32[2048,512]{1,0:T(8,128)} %bitcast_convert_fusion) | data formatting | bytes 8388608 | tf_op jit(solution)/shard_map/convert_element_type | solution.py:87
  58.7 2.5 %mul.84 = f32[32,64,512]{2,1,0:T(8,128)} broadcast(f32[32,512]{1,0:T(8,128)S(1)} %bitcast.111), dimensions={0,2} | broadcast | bytes 4259840 | tf_op jit(solution)/shard_map/mul | solution.py:88
  61.2 5.5 %copy.58 = f32[2048,512]{0,1:T(8,128)} copy(f32[2048,512]{1,0:T(8,128)} %bitcast.104) | data formatting | bytes 8388608 | tf_op jit(solution)/shard_map/mul | solution.py:88
  66.6 5.4 %copy.57 = f32[2048,512]{0,1:T(8,128)} copy(f32[2048,512]{1,0:T(8,128)} %bitcast_convert_fusion.1) | data formatting | bytes 8388608 | tf_op jit(solution)/shard_map/convert_element_type | solution.py:87
  73.5 3.8 %collective-permute-start.3 = (bf16[32,64,128]{2,1,0:T(8,128)(2,1)S(1)}, bf16[32,64,128]{2,1,0:T(8,128)(2,1)S(1)}, u32[]{:S(2)}, u32[]{:S(2)}) collective-permute-start(bf16[32,64,128]{2,1,0:T(8,128)(2,1)S(1)} %all-to-all-done), channel_id=1, source_target_pairs={{0,1},{1,0},{2,3},{3,2},{4,5},{5,4},{6,7},{7,6},{8,9},{9,8},{10,11... | collective-permute-start | bytes 1572872 | tf_op jit(solution)/shard_map/ppermute | solution.py:73
  77.2 4.3 %fusion.3 = bf16[2048,512]{0,1:T(8,128)(2,1)S(1)} fusion(f32[2048,512]{0,1:T(8,128)} %copy.58, f32[2048,512]{0,1:T(8,128)} %copy.57, bf16[128,512]{1,0:T(8,128)(2,1)S(1)} %maximum_select_fusion, bf16[2048,128]{1,0:T(8,128)(2,1)S(1)} %bitcast.106), kind=kOutput, calls=%fused_computation.5 | convolution fusion | flops 271581184 | bytes 11141120 | tf_op jit(solution)/shard_map/dot_general | solution.py:86
  82.4 1.5 %copy-done = f32[2048,512]{0,1:T(8,128)S(1)} copy-done((f32[2048,512]{0,1:T(8,128)S(1)}, f32[2048,512]{0,1:T(8,128)}, u32[]{:S(2)}) %copy-start) | copy-done | bytes 4194328
  84.6 1.6 %fusion.6 = bf16[2048,128]{1,0:T(8,128)(2,1)} fusion(bf16[2048,512]{0,1:T(8,128)(2,1)S(1)} %fusion.1, bf16[128,512]{1,0:T(8,128)(2,1)S(1)} %maximum_select_fusion), kind=kOutput, calls=%fused_computation.10 | convolution fusion | flops 269221888 | bytes 2752512 | tf_op jit(solution)/shard_map/dot_general | solution.py:89
  86.2 1.9 %collective-permute-start.4 = (bf16[32,64,128]{2,1,0:T(8,128)(2,1)}, bf16[32,64,128]{2,1,0:T(8,128)(2,1)S(1)}, u32[]{:S(2)}, u32[]{:S(2)}) collective-permute-start(bf16[32,64,128]{2,1,0:T(8,128)(2,1)} %bitcast.9), channel_id=1, source_target_pairs={{0,1},{1,0},{2,3},{3,2},{4,5},{5,4},{6,7},{7,6},{8,9},{9,8},{10,11... | collective-permute-start | bytes 1572872 | tf_op jit(solution)/shard_map/ppermute | solution.py:95
  88.9 1.5 %fusion.24 = bf16[512,128]{0,1:T(8,128)(2,1)} fusion(f32[512,128]{0,1:T(8,128)S(1)} %fusion.67, bf16[2048,512]{0,1:T(8,128)(2,1)S(1)} %fusion.1, bf16[2048,128]{1,0:T(8,128)(2,1)S(1)} %bitcast.110), kind=kOutput, calls=%fused_computation.35 | convolution fusion | flops 268697600 | bytes 3014656 | tf_op jit(solution)/shard_map/dot_general | solution.py:90
  90.4 6.4 %all-to-all-start.2 = ((bf16[8,16,512]{2,1,0:T(8,128)(2,1)}), bf16[8,16,512]{2,1,0:T(8,128)(2,1)S(1)}, u32[]{:S(2)}, u32[]{:S(2)}) async-start(bf16[8,16,512]{2,1,0:T(8,128)(2,1)} %bitcast.11), calls=%async_computation.2 | async-start | bytes 262144 | tf_op jit(solution)/shard_map/all_to_all | solution.py:102
  97.8 9.5 %all-to-all-done.2 = bf16[8,16,512]{2,1,0:T(8,128)(2,1)S(1)} async-done(((bf16[8,16,512]{2,1,0:T(8,128)(2,1)}), bf16[8,16,512]{2,1,0:T(8,128)(2,1)S(1)}, u32[]{:S(2)}, u32[]{:S(2)}) %all-to-all-start.2) | async-done | bytes 131104 | tf_op jit(solution)/shard_map/all_to_all | solution.py:102
  107.3 10.2 %all-to-all-start.1 = ((bf16[32,64,128]{2,1,0:T(8,128)(2,1)}), bf16[32,64,128]{2,1,0:T(8,128)(2,1)S(1)}, u32[]{:S(2)}, u32[]{:S(2)}) async-start(bf16[32,64,128]{2,1,0:T(8,128)(2,1)} %add_convert_fusion), calls=%async_computation.1 | async-start | bytes 1048576 | tf_op jit(solution)/shard_map/all_to_all | solution.py:96
  119.0 15.3 %all-to-all-done.1 = bf16[32,64,128]{2,1,0:T(8,128)(2,1)S(1)} async-done(((bf16[32,64,128]{2,1,0:T(8,128)(2,1)}), bf16[32,64,128]{2,1,0:T(8,128)(2,1)S(1)}, u32[]{:S(2)}, u32[]{:S(2)}) %all-to-all-start.1) | async-done | bytes 524320 | tf_op jit(solution)/shard_map/all_to_all | solution.py:96
  (57 shorter events, 10.1 us)
Async XLA Ops:
  1.4 27.0 %collective-permute-start = (bf16[16,512]{1,0:T(8,128)(2,1)S(1)}, bf16[16,512]{1,0:T(8,128)(2,1)S(1)}, u32[]{:S(2)}, u32[]{:S(2)}) collective-permute-start(bf16[16,512]{1,0:T(8,128)(2,1)S(1)} %convert_element_type.74), channel_id=1, source_target_pairs={{0,64},{64,0},{128,192},{192,128},{256,320},{320,256},{384,448},{4... | collective-permute-start | bytes 49160 | tf_op jit(solution)/shard_map/ppermute | solution.py:53
  6.5 67.0 %all-to-all-start = ((bf16[32,64,128]{2,1,0:T(8,128)(2,1)}), bf16[32,64,128]{2,1,0:T(8,128)(2,1)S(1)}, u32[]{:S(2)}, u32[]{:S(2)}) async-start(bf16[32,64,128]{2,1,0:T(8,128)(2,1)} %broadcast_in_dim.36), calls=%async_computation | async-start | bytes 1048576 | tf_op jit(solution)/shard_map/all_to_all | solution.py:45
  25.7 7.4 %copy-start.8 = (f32[4,128]{1,0:T(4,128)S(1)}, f32[4,128]{1,0:T(4,128)}, u32[]{:S(2)}) copy-start(f32[4,128]{1,0:T(4,128)} %param.17) | copy-start | bytes 6148
  25.7 15.1 %copy-start.7 = (s32[4]{0:T(128)S(1)}, s32[4]{0:T(128)}, u32[]{:S(2)}) copy-start(s32[4]{0:T(128)} %param.15) | copy-start | bytes 52
  28.4 7.3 %collective-permute-start.1 = (bf16[32,512]{1,0:T(8,128)(2,1)S(1)}, bf16[32,512]{1,0:T(8,128)(2,1)S(1)}, u32[]{:S(2)}, u32[]{:S(2)}) collective-permute-start(bf16[32,512]{1,0:T(8,128)(2,1)S(1)} %maximum_select_fusion.2), channel_id=1, source_target_pairs={{0,128},{64,192},{128,0},{192,64},{256,384},{320,448},{384,256},{4... | collective-permute-start | bytes 98312 | tf_op jit(solution)/shard_map/ppermute | solution.py:53
  35.7 10.2 %collective-permute-start.2 = (bf16[64,512]{1,0:T(8,128)(2,1)S(1)}, bf16[64,512]{1,0:T(8,128)(2,1)S(1)}, u32[]{:S(2)}, u32[]{:S(2)}) collective-permute-start(bf16[64,512]{1,0:T(8,128)(2,1)S(1)} %maximum_select_fusion.1), channel_id=1, source_target_pairs={{0,256},{64,320},{128,384},{192,448},{256,0},{320,64},{384,128},{4... | collective-permute-start | bytes 196616 | tf_op jit(solution)/shard_map/ppermute | solution.py:53
  46.0 26.1 %collective-permute-start.5 = (bf16[128,128]{1,0:T(8,128)(2,1)S(1)}, bf16[128,128]{1,0:T(8,128)(2,1)S(1)}, u32[]{:S(2)}, u32[]{:S(2)}) collective-permute-start(bf16[128,128]{1,0:T(8,128)(2,1)S(1)} %slice.92), channel_id=1, source_target_pairs={{0,1},{1,2},{2,3},{3,4},{4,5},{5,6},{6,7},{7,8},{8,9},{9,10},{10,1... | collective-permute-start | bytes 98312 | tf_op jit(solution)/shard_map/ppermute | solution.py:106
  53.1 5.4 %copy-start.9 = (s32[32,4]{0,1:T(4,128)S(1)}, s32[32,4]{0,1:T(4,128)}, u32[]{:S(2)}) copy-start(s32[32,4]{0,1:T(4,128)} %param.10) | copy-start | bytes 1540
  66.6 5.5 %copy-start.2 = (bf16[4,2,128,128]{3,2,1,0:T(8,128)(2,1)S(1)}, bf16[4,2,128,128]{3,2,1,0:T(8,128)(2,1)}, u32[]{:S(2)}) copy-start(bf16[4,2,128,128]{3,2,1,0:T(8,128)(2,1)} %param.16) | copy-start | bytes 786436
  73.5 8.9 %collective-permute-start.3 = (bf16[32,64,128]{2,1,0:T(8,128)(2,1)S(1)}, bf16[32,64,128]{2,1,0:T(8,128)(2,1)S(1)}, u32[]{:S(2)}, u32[]{:S(2)}) collective-permute-start(bf16[32,64,128]{2,1,0:T(8,128)(2,1)S(1)} %all-to-all-done), channel_id=1, source_target_pairs={{0,1},{1,0},{2,3},{3,2},{4,5},{5,4},{6,7},{7,6},{8,9},{9,8},{10,11... | collective-permute-start | bytes 1572872 | tf_op jit(solution)/shard_map/ppermute | solution.py:73
  77.2 5.1 %copy-start.1 = (f32[2048,512]{0,1:T(8,128)S(1)}, f32[2048,512]{0,1:T(8,128)}, u32[]{:S(2)}) copy-start(f32[2048,512]{0,1:T(8,128)} %copy.59) | copy-start | bytes 12582916
  81.6 2.3 %copy-start = (f32[2048,512]{0,1:T(8,128)S(1)}, f32[2048,512]{0,1:T(8,128)}, u32[]{:S(2)}) copy-start(f32[2048,512]{0,1:T(8,128)} %copy.58) | copy-start | bytes 12582916
  86.2 10.6 %collective-permute-start.4 = (bf16[32,64,128]{2,1,0:T(8,128)(2,1)}, bf16[32,64,128]{2,1,0:T(8,128)(2,1)S(1)}, u32[]{:S(2)}, u32[]{:S(2)}) collective-permute-start(bf16[32,64,128]{2,1,0:T(8,128)(2,1)} %bitcast.9), channel_id=1, source_target_pairs={{0,1},{1,0},{2,3},{3,2},{4,5},{5,4},{6,7},{7,6},{8,9},{9,8},{10,11... | collective-permute-start | bytes 1572872 | tf_op jit(solution)/shard_map/ppermute | solution.py:95
  90.4 16.9 %all-to-all-start.2 = ((bf16[8,16,512]{2,1,0:T(8,128)(2,1)}), bf16[8,16,512]{2,1,0:T(8,128)(2,1)S(1)}, u32[]{:S(2)}, u32[]{:S(2)}) async-start(bf16[8,16,512]{2,1,0:T(8,128)(2,1)} %bitcast.11), calls=%async_computation.2 | async-start | bytes 262144 | tf_op jit(solution)/shard_map/all_to_all | solution.py:102
  107.3 27.1 %all-to-all-start.1 = ((bf16[32,64,128]{2,1,0:T(8,128)(2,1)}), bf16[32,64,128]{2,1,0:T(8,128)(2,1)S(1)}, u32[]{:S(2)}, u32[]{:S(2)}) async-start(bf16[32,64,128]{2,1,0:T(8,128)(2,1)} %add_convert_fusion), calls=%async_computation.1 | async-start | bytes 1048576 | tf_op jit(solution)/shard_map/all_to_all | solution.py:96
  117.5 0.8 copy-start.3
  117.5 16.9 %copy-start.4 = (f32[64,128]{1,0:T(8,128)S(1)}, f32[64,128]{1,0:T(8,128)}, u32[]{:S(2)}) copy-start(f32[64,128]{1,0:T(8,128)} %param.11) | copy-start | bytes 98308
  117.6 16.9 %copy-start.5 = (f32[64,128]{1,0:T(8,128)S(1)}, f32[64,128]{1,0:T(8,128)}, u32[]{:S(2)}) copy-start(f32[64,128]{1,0:T(8,128)} %param.12) | copy-start | bytes 98308
  117.6 16.9 %copy-start.6 = (f32[64,128]{1,0:T(8,128)S(1)}, f32[64,128]{1,0:T(8,128)}, u32[]{:S(2)}) copy-start(f32[64,128]{1,0:T(8,128)} %param.13) | copy-start | bytes 98308
